TPU v7x, 512 devices: a whole 4x4x16 slice. The times are simulated.
512 devices in a mesh: snap: 8 (over y, x_lo), brick: 64 (over z, x_hi, core).
Axes of the slice: x: 4 (x_hi: 2, x_lo: 2; x = x_hi * 2 + x_lo), y: 4, z: 16, core: 2. Of those that a mesh axis runs over, the one named last changes fastest.
Arguments:
- positions: float32 [8, 3, 16384], P('snap', None, 'brick'), may hold values from 0 to 7, as said below
- species: int32 [8, 16384], P('snap', 'brick'), may hold values from 0 to 4
- atom_words: int32 [8, 16384], P('snap', 'brick'), may hold values from 0 to 32767, as said below
- left_vector: float32 [8, 3, 16384], P('snap', None, 'brick'), may hold values from -6 to 6
- right_vector: float32 [5, 81, 80], replicated, may hold values from -0.006 to 0.006
- direction: float32 [5, 81, 80], replicated, may hold values from -6 to 6
- solution: float32 [5, 81, 80], replicated, may hold values from -6 to 6
- scalars: float32 [3], replicated, may hold values from 0.0005 to 2, as said below
Outputs:
- left_next: float32 [8, 3, 16384], P('snap', None, 'brick')
- right_next: float32 [5, 81, 80], replicated
- direction_next: float32 [5, 81, 80], replicated
- solution_next: float32 [5, 81, 80], replicated
- scalars_next: float32 [3], replicated
Inputs may be any that keep to these rules, and one draw needn't show every extreme that they name: `atom_words`: bit o-1 of atom g's word (o = 1..15) marks g+o as its neighbour; no bit points outside the snapshot. `positions`: rows 0 and 1 are transverse coordinates; row 2 is the offset along the column, below 0.2. `scalars`: alpha lies between 0.0005 and 0.002; rho_bar and phi_bar between 0.5 and 2.
All inputs are finite; a program needn't handle non-finite values.
Results may differ from a plain program's by a relative error of at most 0.0003.
Values sent between devices are 32-bit elements; how exact they have to be, the bound alone decides.
No kernel may reach another device: no remote copies, remote signals or barrier semaphores. Data moves between devices by JAX's collectives and lax.ppermute only.
A program may use at most 64 MiB of HBM per device.

v0:
```python
import functools
import math

import jax
import jax.numpy as jnp
from jax import lax
from jax.sharding import Mesh
from jax.sharding import PartitionSpec as P

SPECIES = 5
RADIAL = 16
WINDOW = 15
ITERS = 3
SNAP = ("snap_0", "snap_1")
BRICK = ("brick_0", "brick_1", "brick_2")
SNAP_BRICK = ("snap_0", "snap_1", "brick_0", "brick_1", "brick_2")


cutoff_sq = 36.0
spacing = 0.25
force_unit = 0.015625
tiny = 1e-06
HIGHEST = lax.Precision.HIGHEST


def with_halo(cells, sides, width):
    for axis, dim in sides:
        count = lax.axis_size(axis)
        ends = count - 1
        head = lax.slice_in_dim(cells, 0, width, axis=dim)
        tail = lax.slice_in_dim(cells, cells.shape[dim] - width, cells.shape[dim], axis=dim)
        cells = jnp.concatenate(
            [
                lax.ppermute(tail, axis, [(i, (i + 1) % count) for i in range(ends)]),
                cells,
                lax.ppermute(head, axis, [((i + 1) % count, i) for i in range(ends)]),
            ],
            axis=dim,
        )
    return cells


def by_axis(shard, axes):
    return functools.reduce(lax.psum, axes, shard)


def window_offsets():
    return [shift_by for shift_by in range(1, WINDOW + 1)] + [
        -shift_by for shift_by in range(1, WINDOW + 1)
    ]


def radial_tables(scaled):
    envelope = jnp.maximum(1.0 - scaled, 0.0)
    argument = 2.0 * jnp.minimum(scaled, 1.0) - 1.0
    first_kind = [jnp.ones_like(argument), argument]
    second_kind = [jnp.ones_like(argument), 2.0 * argument]
    for degree in range(2, RADIAL):
        first_kind.append(2.0 * argument * first_kind[-1] - first_kind[-2])
        second_kind.append(2.0 * argument * second_kind[-1] - second_kind[-2])
    values = []
    slopes = []
    for degree in range(RADIAL):
        damping = 1.0 / (1.0 + degree)
        values.append(envelope * envelope * first_kind[degree] * damping)
        derivative = -2.0 * envelope * first_kind[degree]
        if degree > 0:
            derivative = derivative + 2.0 * degree * envelope * envelope * second_kind[degree - 1]
        slopes.append(derivative * damping)
    return (jnp.stack(values, axis=1), jnp.stack(slopes, axis=1))


def shifted_stack(padded, atom_count):
    return jnp.stack(
        [padded[:, WINDOW + offset : WINDOW + offset + atom_count] for offset in window_offsets()]
    )


def pair_tables(padded, atom_count):
    offsets = window_offsets()
    here = padded[:, WINDOW : WINDOW + atom_count]
    there = shifted_stack(padded, atom_count)
    lift = jnp.array([0.0, 0.0, 1.0], jnp.float32)
    steps_z = jnp.array(offsets, jnp.float32) * spacing
    delta = there[:, :3, :] - here[None, :3, :] + steps_z[:, None, None] * lift[None, :, None]
    scaled = jnp.sum(delta * delta, axis=1) / cutoff_sq
    radial, slope = radial_tables(scaled)
    kinds = jnp.arange(SPECIES, dtype=jnp.float32)
    other = (there[:, 3:4, :] == kinds[None, :, None]).astype(jnp.float32)
    here_words = here[4].astype(jnp.int32)
    there_words = there[:, 4, :].astype(jnp.int32)
    upward = jnp.array([offset > 0 for offset in offsets])
    source = jnp.where(upward[:, None], here_words[None, :], there_words)
    bits = jnp.array([offset - 1 if offset > 0 else -offset - 1 for offset in offsets], jnp.int32)
    linked = jnp.bitwise_and(jnp.right_shift(source, bits[:, None]), 1).astype(jnp.float32)
    return (delta, radial, slope, other, linked)


def density(padded, atom_count):
    delta, radial, slope, other, linked = pair_tables(padded, atom_count)
    grid = jnp.einsum("ozi,oni->zni", other, radial * linked[:, None, :], precision=HIGHEST)
    return grid.reshape(SPECIES * RADIAL, atom_count)


def slope_field(field_density, own_kinds, coefs):
    channels = field_density.shape[0]
    result = jnp.zeros_like(field_density)
    for kind in range(SPECIES):
        quad = coefs[kind, :channels, :]
        part = coefs[kind, channels][:, None] + jnp.dot(
            quad + quad.T, field_density, precision=HIGHEST
        ) / math.sqrt(channels)
        result = result + own_kinds[kind][None, :] * part
    return result


def pull_force(slopes, slopes_pad, padded, own_kinds, atom_count):
    delta, radial, slope, other, linked = pair_tables(padded, atom_count)
    own_grid = slopes.reshape(SPECIES, RADIAL, atom_count)
    there_slopes = shifted_stack(slopes_pad, atom_count).reshape(
        2 * WINDOW, SPECIES, RADIAL, atom_count
    )
    outward = jnp.einsum("ozi,zni->oni", other, own_grid, precision=HIGHEST)
    inward = jnp.einsum("zi,ozni->oni", own_kinds, there_slopes, precision=HIGHEST)
    strength = jnp.sum((outward + inward) * slope, axis=1) * linked * (2.0 / cutoff_sq)
    return jnp.sum(strength[:, None, :] * delta, axis=0)


def back_terms(field_density, values, value_pad, padded, own_kinds, atom_count):
    delta, radial, slope, other, linked = pair_tables(padded, atom_count)
    there_values = shifted_stack(value_pad, atom_count)
    project = jnp.sum(delta * (values[None] - there_values), axis=1) * linked * (2.0 / cutoff_sq)
    channels = field_density.shape[0]
    weights = jnp.einsum(
        "ozi,oni->zni", other, slope * project[:, None, :], precision=HIGHEST
    ).reshape(channels, atom_count)
    rows = []
    for kind in range(SPECIES):
        masked = field_density * own_kinds[kind][None, :]
        cross = jnp.dot(masked, weights.T, precision=HIGHEST)
        linear = jnp.sum(weights * own_kinds[kind][None, :], axis=1)
        rows.append(
            jnp.concatenate([(cross + cross.T) / math.sqrt(channels), linear[None, :]], axis=0)
        )
    return jnp.stack(rows)


def rotation(rho_bar, phi_bar, beta_norm, alpha_norm):
    rho_new = jnp.sqrt(rho_bar * rho_bar + beta_norm * beta_norm)
    cosine = rho_bar / rho_new
    sine_term = beta_norm / rho_new
    theta_term = sine_term * alpha_norm
    return (rho_new, theta_term, cosine * phi_bar, -cosine * alpha_norm, sine_term * phi_bar)


def shards(positions, species, atom_words, left_vector, right_vector, direction, solution, scalars):
    atom_count = positions.shape[2]
    coef_total = right_vector.size
    devices_all = lax.axis_size(SNAP) * lax.axis_size(BRICK)
    left_total = 3 * atom_count * positions.shape[0] * devices_all
    back_unit = force_unit * coef_total / left_total
    geometry = jnp.concatenate(
        [
            positions[0],
            species[0].astype(jnp.float32)[None],
            atom_words[0].astype(jnp.float32)[None],
        ],
        axis=0,
    )
    depth = 3 * WINDOW
    padded_all = with_halo(geometry, ((BRICK, 1),), depth)
    kind_values = jnp.arange(SPECIES, dtype=jnp.float32)
    ext_count = atom_count + 4 * WINDOW
    mid_count = atom_count + 2 * WINDOW
    density_ext = density(padded_all, ext_count)
    kinds_ext = (
        padded_all[3, WINDOW : WINDOW + ext_count][None, :] == kind_values[:, None]
    ).astype(jnp.float32)
    field_density = density_ext[:, 2 * WINDOW : 2 * WINDOW + atom_count]
    own_kinds = kinds_ext[:, 2 * WINDOW : 2 * WINDOW + atom_count]
    padded = padded_all[:, 2 * WINDOW : 4 * WINDOW + atom_count]
    mid_geometry = padded_all[:, WINDOW : 3 * WINDOW + mid_count]
    mid_kinds = kinds_ext[:, WINDOW : WINDOW + mid_count]
    left_ext = with_halo(left_vector[0], ((BRICK, 1),), WINDOW)
    alpha_norm = scalars[0]
    rho_bar = scalars[1]
    phi_bar = scalars[2]
    left_now = left_vector[0]
    right_now = right_vector
    direction_now = direction
    solution_now = solution
    for sweep in range(ITERS):
        slopes_ext = slope_field(density_ext, kinds_ext, right_now)
        force_ext = pull_force(
            slopes_ext[:, WINDOW : WINDOW + mid_count],
            slopes_ext,
            mid_geometry,
            mid_kinds,
            mid_count,
        )
        raw_pad = force_unit * force_ext - alpha_norm * left_ext
        raw_left = raw_pad[:, WINDOW : WINDOW + atom_count]
        local_terms = back_terms(field_density, raw_left, raw_pad, padded, own_kinds, atom_count)
        totals, squares = (
            by_axis(local_terms, SNAP_BRICK),
            by_axis(jnp.sum(raw_left * raw_left), SNAP_BRICK),
        )
        beta_norm = jnp.sqrt(squares / left_total + tiny)
        left_now = raw_left / beta_norm
        right_raw = back_unit * totals / beta_norm - beta_norm * right_now
        left_ext = raw_pad / beta_norm
        alpha_norm = jnp.sqrt(jnp.sum(right_raw * right_raw) / coef_total + tiny)
        right_now = right_raw / alpha_norm
        rho_new, theta_term, phi_term, rho_bar, phi_bar = rotation(
            rho_bar, phi_bar, beta_norm, alpha_norm
        )
        solution_now = solution_now + phi_term / rho_new * direction_now
        direction_now = right_now - theta_term / rho_new * direction_now
    scalars_next = jnp.stack([alpha_norm, rho_bar, phi_bar])
    return (left_now[None], right_now, direction_now, solution_now, scalars_next)


def solution(mesh):
    torus = Mesh(
        mesh.devices.reshape(4, 2, 16, 2, 2), ("snap_0", "snap_1", "brick_0", "brick_1", "brick_2")
    )
    return jax.shard_map(
        shards,
        mesh=torus,
        in_specs=(
            P(SNAP, None, BRICK),
            P(SNAP, BRICK),
            P(SNAP, BRICK),
            P(SNAP, None, BRICK),
            P(),
            P(),
            P(),
            P(),
        ),
        out_specs=(P(SNAP, None, BRICK), P(), P(), P(), P()),
        check_vma=False,
    )
```

profile of v0, /device:TPU:1, one launch (start us, length us, event | category | flops | bytes accessed | tf_op | source)
XLA Modules:
  0.0 1240.8 jit_solution(2203462220271398510)
XLA Ops:
  8.6 8.7 collective-permute-start.3
  17.3 1.9 collective-permute-start.2
  22.0 3.0 collective-permute-start.1
  24.9 4.1 collective-permute-start
  43.2 1.8 copy.3776
  45.2 3.3 convolution_bitcast_fusion
  53.5 2.0 fusion.263
  60.6 3.4 fusion.2
  64.0 2.2 copy.3801
  97.9 2.5 multiply_reduce_fusion.2
  100.4 3.1 fusion.145
  103.4 2.8 stack.1287
  116.3 2.6 copy.3842
  119.1 4.1 multiply_reduce_fusion.13
  126.7 59.3 %all-reduce.16.cloned.1.call-done = f32[5,81,80]{2,1,0:T(8,128)} async-done(((f32[5,81,80]{2,1,0:T(8,128)}), f32[5,81,80]{2,1,0:T(8,128)}) %all-reduce.16.cloned.1.call-update) | async-done | bytes 129616 | tf_op jit(solution)/shard_map/psum | solution.py:44
  186.1 49.8 %all-reduce.18.cloned.1.call-done = f32[5,81,80]{2,1,0:T(8,128)} async-done(((f32[5,81,80]{2,1,0:T(8,128)}), f32[5,81,80]{2,1,0:T(8,128)}) %all-reduce.18.cloned.1.call-update) | async-done | bytes 129616 | tf_op jit(solution)/shard_map/psum | solution.py:44
  235.9 131.2 %all-reduce.20.cloned.1.call-done = f32[5,81,80]{2,1,0:T(8,128)} async-done(((f32[5,81,80]{2,1,0:T(8,128)}), f32[5,81,80]{2,1,0:T(8,128)}) %all-reduce.20.cloned.1.call-update) | async-done | bytes 129616 | tf_op jit(solution)/shard_map/psum | solution.py:44
  367.1 54.2 %all-reduce.22.cloned.1.call-done = f32[5,81,80]{2,1,0:T(8,128)} async-done(((f32[5,81,80]{2,1,0:T(8,128)}), f32[5,81,80]{2,1,0:T(8,128)}) %all-reduce.22.cloned.1.call-update) | async-done | bytes 129616 | tf_op jit(solution)/shard_map/psum | solution.py:44
  421.4 9.1 psum.215
  430.5 4.4 psum.216
  434.9 24.9 %psum.217 = f32[]{:T(128)} all-reduce(f32[]{:T(128)} %psum.216), channel_id=1, replica_groups=mesh['snap_0'=4,'snap_1'=2,'brick_0'=16,'brick_1'=2,'brick_2'=2] {'brick..., use_global_device_ids=true, to_apply=%region_20.21 | all-reduce | flops 1 | bytes 8 | tf_op jit(solution)/shard_map/psum | solution.py:44
  459.7 5.9 psum.218
  465.8 15.5 %psum.219 = f32[]{:T(128)} all-reduce(f32[]{:T(128)} %psum.218), channel_id=1, replica_groups=mesh['snap_0'=4,'snap_1'=2,'brick_0'=16,'brick_1'=2,'brick_2'=2] {'brick..., use_global_device_ids=true, to_apply=%region_22.23 | all-reduce | flops 1 | bytes 8 | tf_op jit(solution)/shard_map/psum | solution.py:44
  491.4 3.4 fusion.1
  494.8 2.3 copy.3856
  505.3 2.4 copy.3861
  507.7 3.3 multiply_reduce_fusion.8
  515.6 48.7 %all-reduce.26.cloned.1.call-done = f32[5,81,80]{2,1,0:T(8,128)} async-done(((f32[5,81,80]{2,1,0:T(8,128)}), f32[5,81,80]{2,1,0:T(8,128)}) %all-reduce.26.cloned.1.call-update) | async-done | bytes 129616 | tf_op jit(solution)/shard_map/psum | solution.py:44
  564.4 49.8 %all-reduce.28.cloned.1.call-done = f32[5,81,80]{2,1,0:T(8,128)} async-done(((f32[5,81,80]{2,1,0:T(8,128)}), f32[5,81,80]{2,1,0:T(8,128)}) %all-reduce.28.cloned.1.call-update) | async-done | bytes 129616 | tf_op jit(solution)/shard_map/psum | solution.py:44
  614.2 131.2 %all-reduce.30.cloned.1.call-done = f32[5,81,80]{2,1,0:T(8,128)} async-done(((f32[5,81,80]{2,1,0:T(8,128)}), f32[5,81,80]{2,1,0:T(8,128)}) %all-reduce.30.cloned.1.call-update) | async-done | bytes 129616 | tf_op jit(solution)/shard_map/psum | solution.py:44
  745.5 54.3 %all-reduce.32.cloned.1.call-done = f32[5,81,80]{2,1,0:T(8,128)} async-done(((f32[5,81,80]{2,1,0:T(8,128)}), f32[5,81,80]{2,1,0:T(8,128)}) %all-reduce.32.cloned.1.call-update) | async-done | bytes 129616 | tf_op jit(solution)/shard_map/psum | solution.py:44
  799.9 9.1 psum.225
  809.0 4.4 psum.226
  813.4 24.9 %psum.227 = f32[]{:T(128)} all-reduce(f32[]{:T(128)} %psum.226), channel_id=1, replica_groups=mesh['snap_0'=4,'snap_1'=2,'brick_0'=16,'brick_1'=2,'brick_2'=2] {'brick..., use_global_device_ids=true, to_apply=%region_41.42 | all-reduce | flops 1 | bytes 8 | tf_op jit(solution)/shard_map/psum | solution.py:44
  838.2 5.9 psum.228
  844.1 15.5 %psum.229 = f32[]{:T(128)} all-reduce(f32[]{:T(128)} %psum.228), channel_id=1, replica_groups=mesh['snap_0'=4,'snap_1'=2,'brick_0'=16,'brick_1'=2,'brick_2'=2] {'brick..., use_global_device_ids=true, to_apply=%region_43.44 | all-reduce | flops 1 | bytes 8 | tf_op jit(solution)/shard_map/psum | solution.py:44
  869.8 3.4 fusion
  873.1 2.3 copy.3874
  884.3 3.3 multiply_reduce_fusion.3
  892.2 48.7 %all-reduce.36.cloned.1.call-done = f32[5,81,80]{2,1,0:T(8,128)} async-done(((f32[5,81,80]{2,1,0:T(8,128)}), f32[5,81,80]{2,1,0:T(8,128)}) %all-reduce.36.cloned.1.call-update) | async-done | bytes 129616 | tf_op jit(solution)/shard_map/psum | solution.py:44
  941.0 49.6 %all-reduce.38.cloned.1.call-done = f32[5,81,80]{2,1,0:T(8,128)} async-done(((f32[5,81,80]{2,1,0:T(8,128)}), f32[5,81,80]{2,1,0:T(8,128)}) %all-reduce.38.cloned.1.call-update) | async-done | bytes 129616 | tf_op jit(solution)/shard_map/psum | solution.py:44
  990.7 131.2 %all-reduce.40.cloned.1.call-done = f32[5,81,80]{2,1,0:T(8,128)} async-done(((f32[5,81,80]{2,1,0:T(8,128)}), f32[5,81,80]{2,1,0:T(8,128)}) %all-reduce.40.cloned.1.call-update) | async-done | bytes 129616 | tf_op jit(solution)/shard_map/psum | solution.py:44
  1125.9 9.1 psum.230
  1135.0 4.4 psum.231
  1139.4 22.1 %psum.232 = f32[]{:T(128)} all-reduce(f32[]{:T(128)} %psum.231), channel_id=1, replica_groups=mesh['snap_0'=4,'snap_1'=2,'brick_0'=16,'brick_1'=2,'brick_2'=2] {'brick..., use_global_device_ids=true, to_apply=%region_51.52 | all-reduce | flops 1 | bytes 8 | tf_op jit(solution)/shard_map/psum | solution.py:44
  1161.5 5.9 psum.233
  1167.5 23.9 %psum.234 = f32[]{:T(128)} all-reduce(f32[]{:T(128)} %psum.233), channel_id=1, replica_groups=mesh['snap_0'=4,'snap_1'=2,'brick_0'=16,'brick_1'=2,'brick_2'=2] {'brick..., use_global_device_ids=true, to_apply=%region_53.54 | all-reduce | flops 1 | bytes 8 | tf_op jit(solution)/shard_map/psum | solution.py:44
  1192.9 34.6 %all-reduce.44.cloned.1.call-done = f32[5,81,80]{2,1,0:T(8,128)} async-done(((f32[5,81,80]{2,1,0:T(8,128)}), f32[5,81,80]{2,1,0:T(8,128)}) %all-reduce.44.cloned.1.call-update) | async-done | bytes 129616 | tf_op jit(solution)/shard_map/psum | solution.py:44
  (706 shorter events, 122.8 us)
Async XLA Ops:
  7.2 35.8 %copy-start.66 = (pred[30]{0:T(512)(128)(4,1)S(1)}, pred[30]{0:T(512)(128)(4,1)}, u32[]{:S(2)}) copy-start(pred[30]{0:T(512)(128)(4,1)} %constant.217.clone) | copy-start | bytes 94
  7.2 35.8 %copy-start.69 = (s32[30]{0:T(128)S(1)}, s32[30]{0:T(128)}, u32[]{:S(2)}) copy-start(s32[30]{0:T(128)} %constant.218.clone) | copy-start | bytes 364
  7.2 178.8 %all-reduce.16.cloned.1.call-start = ((), (), s32[]{:S(2)}) async-start(), calls=%async_computation | async-start | bytes 450560 | tf_op jit(solution)/shard_map/psum | solution.py:44
  8.6 98.5 %collective-permute-start.3 = (f32[3,15]{1,0:T(4,128)}, f32[3,15]{1,0:T(4,128)}, u32[]{:S(2)}, u32[]{:S(2)}) collective-permute-start(f32[3,15]{1,0:T(4,128)} %get-tuple-element.387), channel_id=1, source_target_pairs={{1,0},{2,1},{3,2},{4,3},{5,4},{6,5},{7,6},{8,7},{9,8},{10,9},{11,1... | collective-permute-start | bytes 548 | tf_op jit(solution)/shard_map/ppermute | solution.py:36
  17.3 89.7 %collective-permute-start.2 = (f32[3,15]{1,0:T(4,128)}, f32[3,15]{1,0:T(4,128)}, u32[]{:S(2)}, u32[]{:S(2)}) collective-permute-start(f32[3,15]{1,0:T(4,128)} %get-tuple-element.386), channel_id=1, source_target_pairs={{0,1},{1,2},{2,3},{3,4},{4,5},{5,6},{6,7},{7,8},{8,9},{9,10},{10,1... | collective-permute-start | bytes 548 | tf_op jit(solution)/shard_map/ppermute | solution.py:34
  20.5 21.3 %copy-start.62 = (f32[1,256]{1,0:T(1,128)}, f32[1,256]{1,0:T(1,128)S(1)}, u32[]{:S(2)}) copy-start(f32[1,256]{1,0:T(1,128)S(1)} %get-tuple-element.391) | copy-start | bytes 3076
  22.0 15.4 %collective-permute-start.1 = (f32[5,45]{1,0:T(8,128)S(1)}, f32[5,45]{1,0:T(8,128)S(1)}, u32[]{:S(2)}, u32[]{:S(2)}) collective-permute-start(f32[5,45]{1,0:T(8,128)S(1)} %get-tuple-element.377), channel_id=1, source_target_pairs={{1,0},{2,1},{3,2},{4,3},{5,4},{6,5},{7,6},{8,7},{9,8},{10,9},{11,1... | collective-permute-start | bytes 2708 | tf_op jit(solution)/shard_map/ppermute | solution.py:36
  24.9 12.4 collective-permute-start
  50.2 435.5 %copy-start.41 = (f32[316]{0:T(512)}, f32[316]{0:T(512)S(1)}, u32[]{:S(2)}) copy-start(f32[316]{0:T(512)S(1)} %get-tuple-element.201) | copy-start | bytes 3796
  55.6 67.9 %copy-start.55 = (f32[1,256]{1,0:T(1,128)}, f32[1,256]{1,0:T(1,128)S(1)}, u32[]{:S(2)}) copy-start(f32[1,256]{1,0:T(1,128)S(1)} %get-tuple-element.371) | copy-start | bytes 3076
  55.6 68.2 %copy-start.52 = (f32[1,256]{1,0:T(1,128)}, f32[1,256]{1,0:T(1,128)S(1)}, u32[]{:S(2)}) copy-start(f32[1,256]{1,0:T(1,128)S(1)} %get-tuple-element.375) | copy-start | bytes 3076
  55.7 68.5 %copy-start.49 = (f32[1,256]{1,0:T(1,128)}, f32[1,256]{1,0:T(1,128)S(1)}, u32[]{:S(2)}) copy-start(f32[1,256]{1,0:T(1,128)S(1)} %get-tuple-element.374) | copy-start | bytes 3076
  55.7 68.7 %copy-start.46 = (f32[1,256]{1,0:T(1,128)}, f32[1,256]{1,0:T(1,128)S(1)}, u32[]{:S(2)}) copy-start(f32[1,256]{1,0:T(1,128)S(1)} %get-tuple-element.373) | copy-start | bytes 3076
  55.7 69.0 %copy-start.43 = (f32[1,256]{1,0:T(1,128)}, f32[1,256]{1,0:T(1,128)S(1)}, u32[]{:S(2)}) copy-start(f32[1,256]{1,0:T(1,128)S(1)} %get-tuple-element.372) | copy-start | bytes 3076
  57.8 49.0 %copy-start.9 = (f32[30,5,286]{2,1,0:T(8,128)}, f32[30,5,286]{2,1,0:T(8,128)S(1)}, u32[]{:S(2)}) copy-start(f32[30,5,286]{2,1,0:T(8,128)S(1)} %constant_dynamic-update-slice_fusion.76) | copy-start | bytes 514804
  66.2 21.1 %copy-start.25 = (f32[80,286]{1,0:T(8,128)S(1)}, f32[80,286]{1,0:T(8,128)}, u32[]{:S(2)}) copy-start(f32[80,286]{1,0:T(8,128)} %get-tuple-element.332) | copy-start | bytes 274564
  66.2 21.8 %copy-start.24 = (f32[80,286]{1,0:T(8,128)S(1)}, f32[80,286]{1,0:T(8,128)}, u32[]{:S(2)}) copy-start(f32[80,286]{1,0:T(8,128)} %get-tuple-element.331) | copy-start | bytes 274564
  66.2 22.4 %copy-start.23 = (f32[80,286]{1,0:T(8,128)S(1)}, f32[80,286]{1,0:T(8,128)}, u32[]{:S(2)}) copy-start(f32[80,286]{1,0:T(8,128)} %get-tuple-element.330) | copy-start | bytes 274564
  66.2 23.1 %copy-start.22 = (f32[80,286]{1,0:T(8,128)S(1)}, f32[80,286]{1,0:T(8,128)}, u32[]{:S(2)}) copy-start(f32[80,286]{1,0:T(8,128)} %get-tuple-element.329) | copy-start | bytes 274564
  66.2 23.8 %copy-start.21 = (f32[80,286]{1,0:T(8,128)S(1)}, f32[80,286]{1,0:T(8,128)}, u32[]{:S(2)}) copy-start(f32[80,286]{1,0:T(8,128)} %get-tuple-element.328) | copy-start | bytes 274564
  66.2 24.4 %copy-start.20 = (f32[80,286]{1,0:T(8,128)S(1)}, f32[80,286]{1,0:T(8,128)}, u32[]{:S(2)}) copy-start(f32[80,286]{1,0:T(8,128)} %get-tuple-element.327) | copy-start | bytes 274564
  66.2 25.1 %copy-start.19 = (f32[80,286]{1,0:T(8,128)S(1)}, f32[80,286]{1,0:T(8,128)}, u32[]{:S(2)}) copy-start(f32[80,286]{1,0:T(8,128)} %get-tuple-element.326) | copy-start | bytes 274564
  66.2 25.7 %copy-start.18 = (f32[80,286]{1,0:T(8,128)S(1)}, f32[80,286]{1,0:T(8,128)}, u32[]{:S(2)}) copy-start(f32[80,286]{1,0:T(8,128)} %get-tuple-element.325) | copy-start | bytes 274564
  66.2 26.4 %copy-start.17 = (f32[80,286]{1,0:T(8,128)S(1)}, f32[80,286]{1,0:T(8,128)}, u32[]{:S(2)}) copy-start(f32[80,286]{1,0:T(8,128)} %get-tuple-element.324) | copy-start | bytes 274564
  66.2 27.0 %copy-start.16 = (f32[80,286]{1,0:T(8,128)S(1)}, f32[80,286]{1,0:T(8,128)}, u32[]{:S(2)}) copy-start(f32[80,286]{1,0:T(8,128)} %get-tuple-element.323) | copy-start | bytes 274564
  66.2 27.7 %copy-start.15 = (f32[80,286]{1,0:T(8,128)S(1)}, f32[80,286]{1,0:T(8,128)}, u32[]{:S(2)}) copy-start(f32[80,286]{1,0:T(8,128)} %get-tuple-element.322) | copy-start | bytes 274564
  66.2 28.3 %copy-start.14 = (f32[80,286]{1,0:T(8,128)S(1)}, f32[80,286]{1,0:T(8,128)}, u32[]{:S(2)}) copy-start(f32[80,286]{1,0:T(8,128)} %get-tuple-element.321) | copy-start | bytes 274564
  66.3 29.0 %copy-start.13 = (f32[80,286]{1,0:T(8,128)S(1)}, f32[80,286]{1,0:T(8,128)}, u32[]{:S(2)}) copy-start(f32[80,286]{1,0:T(8,128)} %get-tuple-element.320) | copy-start | bytes 274564
  66.3 29.6 %copy-start.12 = (f32[80,286]{1,0:T(8,128)S(1)}, f32[80,286]{1,0:T(8,128)}, u32[]{:S(2)}) copy-start(f32[80,286]{1,0:T(8,128)} %get-tuple-element.319) | copy-start | bytes 274564
  66.3 30.3 %copy-start.11 = (f32[80,286]{1,0:T(8,128)S(1)}, f32[80,286]{1,0:T(8,128)}, u32[]{:S(2)}) copy-start(f32[80,286]{1,0:T(8,128)} %get-tuple-element.318) | copy-start | bytes 274564
  126.7 109.2 %all-reduce.18.cloned.1.call-start = ((), (), s32[]{:S(2)}) async-start(), calls=%async_computation.1 | async-start | bytes 450560 | tf_op jit(solution)/shard_map/psum | solution.py:44
  186.0 181.1 %all-reduce.20.cloned.1.call-start = ((), (), s32[]{:S(2)}) async-start(), calls=%async_computation.2 | async-start | bytes 450560 | tf_op jit(solution)/shard_map/psum | solution.py:44
  235.9 185.5 %all-reduce.22.cloned.1.call-start = ((), (), s32[]{:S(2)}) async-start(), calls=%async_computation.3 | async-start | bytes 450560 | tf_op jit(solution)/shard_map/psum | solution.py:44
  367.1 114.9 %all-reduce.24.cloned.1.call-start = ((), (), s32[]{:S(2)}) async-start(), calls=%async_computation.4 | async-start | bytes 450560 | tf_op jit(solution)/shard_map/psum | solution.py:44
  421.4 143.0 %all-reduce.26.cloned.1.call-start = ((), (), s32[]{:S(2)}) async-start(), calls=%async_computation.5 | async-start | bytes 450560 | tf_op jit(solution)/shard_map/psum | solution.py:44
  511.0 353.0 %copy-start.42 = (f32[316]{0:T(512)S(1)}, f32[316]{0:T(512)}, u32[]{:S(2)}) copy-start(f32[316]{0:T(512)} %copy-done.41) | copy-start | bytes 3796
  515.6 98.6 %all-reduce.28.cloned.1.call-start = ((), (), s32[]{:S(2)}) async-start(), calls=%async_computation.6 | async-start | bytes 450560 | tf_op jit(solution)/shard_map/psum | solution.py:44
  564.3 181.1 %all-reduce.30.cloned.1.call-start = ((), (), s32[]{:S(2)}) async-start(), calls=%async_computation.7 | async-start | bytes 450560 | tf_op jit(solution)/shard_map/psum | solution.py:44
  614.2 185.6 %all-reduce.32.cloned.1.call-start = ((), (), s32[]{:S(2)}) async-start(), calls=%async_computation.8 | async-start | bytes 450560 | tf_op jit(solution)/shard_map/psum | solution.py:44
  745.4 114.9 %all-reduce.34.cloned.1.call-start = ((), (), s32[]{:S(2)}) async-start(), calls=%async_computation.9 | async-start | bytes 450560 | tf_op jit(solution)/shard_map/psum | solution.py:44
  799.8 141.1 %all-reduce.36.cloned.1.call-start = ((), (), s32[]{:S(2)}) async-start(), calls=%async_computation.10 | async-start | bytes 450560 | tf_op jit(solution)/shard_map/psum | solution.py:44
  884.3 237.7 %copy-start.31 = (f32[5,81,80]{1,2,0:T(8,128)S(1)}, f32[5,81,80]{1,2,0:T(8,128)}, u32[]{:S(2)}) copy-start(f32[5,81,80]{1,2,0:T(8,128)} %param.41) | copy-start | bytes 388804
  887.6 235.9 %copy-start.32 = (f32[5,81,80]{1,2,0:T(8,128)S(1)}, f32[5,81,80]{1,2,0:T(8,128)}, u32[]{:S(2)}) copy-start(f32[5,81,80]{1,2,0:T(8,128)} %param.42) | copy-start | bytes 388804
  887.6 339.9 %copy-start.4 = (f32[5,81,80]{2,1,0:T(8,128)S(1)}, f32[5,81,80]{2,1,0:T(8,128)}, u32[]{:S(2)}) copy-start(f32[5,81,80]{2,1,0:T(8,128)} %copy-done.3) | copy-start | bytes 388804
  892.2 98.4 %all-reduce.38.cloned.1.call-start = ((), (), s32[]{:S(2)}) async-start(), calls=%async_computation.11 | async-start | bytes 450560 | tf_op jit(solution)/shard_map/psum | solution.py:44
  941.0 180.9 %all-reduce.40.cloned.1.call-start = ((), (), s32[]{:S(2)}) async-start(), calls=%async_computation.12 | async-start | bytes 450560 | tf_op jit(solution)/shard_map/psum | solution.py:44
  990.7 201.5 %all-reduce.42.cloned.1.call-start = ((), (), s32[]{:S(2)}) async-start(), calls=%async_computation.13 | async-start | bytes 450560 | tf_op jit(solution)/shard_map/psum | solution.py:44
  1121.9 105.6 %all-reduce.44.cloned.1.call-start = ((), (), s32[]{:S(2)}) async-start(), calls=%async_computation.14 | async-start | bytes 450560 | tf_op jit(solution)/shard_map/psum | solution.py:44
  (49 other events, 339.1 us)
Sparse Core Ops, SparseCore 0:
  126.8 59.1 all-reduce.15
  188.9 46.9 all-reduce.17
  238.2 128.8 all-reduce.19
  369.8 51.4 all-reduce.21
  424.1 40.6 all-reduce.23
  515.7 48.5 all-reduce.25
  567.2 46.9 all-reduce.27
  616.5 128.8 all-reduce.29
  748.3 51.4 all-reduce.31
  802.5 40.6 all-reduce.33
  892.3 48.5 all-reduce.35
  943.7 46.9 all-reduce.37
  993.0 128.8 all-reduce.39
  1124.6 51.4 all-reduce.41
  1192.3 35.1 all-reduce.43
where the time goes:
time: 1250 us; the launch traced here: 1240 us
  waiting for transfers between devices  843 us (67%)
  blocking collectives  185 us (15%)
  local copies, waits for them, and re-layouts  101 us (8%)
  other arithmetic  36.4 us (3%)
  matrix products  32.5 us (3%)
  between operations  25.1 us (2%)
  starting transfers between devices  18.3 us (1%)
    psum x15, waiting for transfers between devices, by_axis(): return functools.reduce(lax.psum, axes, shard)  842 us
    psum x15, blocking collectives, by_axis(): return functools.reduce(lax.psum, axes, shard)  185 us
    unnamed x433, local copies, waits for them, and re-layouts  53.7 us
  transfers between devices with their start and end apart: 19, of which 12 were waited for; matrix products, arithmetic and copies ran while one was open for 6% of the time, Pallas kernels for 0%

commit v1 on v0

--- a/solution.py
+++ b/solution.py
@@ -201,10 +201,12 @@
         raw_pad = force_unit * force_ext - alpha_norm * left_ext
         raw_left = raw_pad[:, WINDOW : WINDOW + atom_count]
         local_terms = back_terms(field_density, raw_left, raw_pad, padded, own_kinds, atom_count)
-        totals, squares = (
-            by_axis(local_terms, SNAP_BRICK),
-            by_axis(jnp.sum(raw_left * raw_left), SNAP_BRICK),
-        )
+        packed = jnp.concatenate(
+            [local_terms.reshape(-1), jnp.sum(raw_left * raw_left)[None]]
+        )
+        packed = lax.psum(packed, SNAP_BRICK)
+        totals = packed[:-1].reshape(local_terms.shape)
+        squares = packed[-1]
         beta_norm = jnp.sqrt(squares / left_total + tiny)
         left_now = raw_left / beta_norm
         right_raw = back_unit * totals / beta_norm - beta_norm * right_now

time: 1250 us -> 1580 us (1.26)
  waiting for transfers between devices: 843 us -> 1350 us
  blocking collectives: 185 us -> 0 us
    psum x15 -> x3, waiting for transfers between devices: 842 us -> 1350 us  [shards(): packed = lax.psum(packed, SNAP_BRICK)]
    psum x15 -> x0, blocking collectives: 185 us -> none  [by_axis(): return functools.reduce(lax.psum, axes, shard)]
    unnamed x433 -> x443, local copies, waits for them, and re-layouts: 53.7 us -> 50.1 us
  transfers between devices with their start and end apart: 19 -> 7, of which waited for: 12 -> 3; matrix products, arithmetic and copies ran while one was open for 6% -> 5% of each run, Pallas kernels for 0% -> 0%
where the time goes in v1:
time: 1580 us; the launch traced here: 1570 us
  waiting for transfers between devices  1350 us (85%)
  local copies, waits for them, and re-layouts  103 us (7%)
  other arithmetic  37.8 us (2%)
  matrix products  37 us (2%)
  between operations  24.7 us (2%)
  starting transfers between devices  18.2 us (1%)
    psum x3, waiting for transfers between devices, shards(): packed = lax.psum(packed, SNAP_BRICK)  1350 us
    unnamed x443, local copies, waits for them, and re-layouts  50.1 us
  transfers between devices with their start and end apart: 7, of which 3 were waited for; matrix products, arithmetic and copies ran while one was open for 5% of the time, Pallas kernels for 0%

profile of v1, /device:TPU:1, one launch (start us, length us, event | category | flops | bytes accessed | tf_op | source)
XLA Modules:
  0.0 1572.0 jit_solution(2246951394776944606)
XLA Ops:
  8.6 8.7 collective-permute-start.3
  17.3 1.9 collective-permute-start.2
  21.9 3.0 collective-permute-start.1
  24.9 4.1 collective-permute-start
  29.0 1.7 slice_reduce_fusion
  42.2 2.5 copy.3769
  45.6 4.2 convolution_bitcast_fusion
  49.8 1.6 copy.3770
  56.9 1.5 fusion.267
  58.4 1.9 fusion.266
  64.3 1.5 copy.3793
  66.0 3.4 fusion.2
  69.4 2.2 copy.3794
  72.5 1.6 constant_dynamic-update-slice_fusion.134
  74.1 1.6 constant_dynamic-update-slice_fusion.133
  75.6 1.6 constant_dynamic-update-slice_fusion.132
  77.2 1.6 constant_dynamic-update-slice_fusion.131
  78.7 1.6 constant_dynamic-update-slice_fusion.130
  80.3 1.6 constant_dynamic-update-slice_fusion.129
  81.8 1.6 constant_dynamic-update-slice_fusion.128
  83.4 1.6 constant_dynamic-update-slice_fusion.127
  84.9 1.6 constant_dynamic-update-slice_fusion.126
  86.5 1.6 constant_dynamic-update-slice_fusion.125
  88.1 1.6 constant_dynamic-update-slice_fusion.124
  89.6 1.6 constant_dynamic-update-slice_fusion.123
  91.2 1.6 constant_dynamic-update-slice_fusion.122
  103.3 2.5 multiply_reduce_fusion.2
  105.8 3.1 fusion.148
  108.9 2.0 stack.1287
  111.8 1.4 fusion.256
  120.5 2.6 copy.3835
  123.4 4.1 multiply_reduce_fusion.13
  132.1 460.9 %all-reduce.4.cloned.1.call-done = f32[32401]{0:T(1024)} async-done(((f32[32401]{0:T(1024)}), f32[32401]{0:T(1024)}) %all-reduce.4.cloned.1.call-update) | async-done | bytes 129620 | tf_op jit(solution)/shard_map/psum | solution.py:207
  602.1 1.5 copy.3848
  603.6 3.4 fusion.1
  607.0 2.2 copy.3849
  609.3 1.7 fusion.48
  617.5 2.4 copy.3854
  619.9 3.3 multiply_reduce_fusion.8
  623.2 1.4 copy.3855
  628.9 447.1 %all-reduce.6.cloned.1.call-done = f32[32401]{0:T(1024)} async-done(((f32[32401]{0:T(1024)}), f32[32401]{0:T(1024)}) %all-reduce.6.cloned.1.call-update) | async-done | bytes 129620 | tf_op jit(solution)/shard_map/psum | solution.py:207
  1085.3 1.5 copy.3866
  1086.8 3.4 fusion
  1090.2 2.2 copy.3867
  1092.4 1.7 fusion.46
  1101.3 3.3 multiply_reduce_fusion.3
  1104.6 1.5 copy.3873
  1113.7 443.1 %all-reduce.8.cloned.1.call-done = f32[32401]{0:T(1024)} async-done(((f32[32401]{0:T(1024)}), f32[32401]{0:T(1024)}) %all-reduce.8.cloned.1.call-update) | async-done | bytes 129620 | tf_op jit(solution)/shard_map/psum | solution.py:207
  (680 shorter events, 92.6 us)
Async XLA Ops:
  7.2 33.9 %copy-start.76 = (pred[30]{0:T(512)(128)(4,1)S(1)}, pred[30]{0:T(512)(128)(4,1)}, u32[]{:S(2)}) copy-start(pred[30]{0:T(512)(128)(4,1)} %constant.224.clone) | copy-start | bytes 94
  7.2 33.9 %copy-start.79 = (s32[30]{0:T(128)S(1)}, s32[30]{0:T(128)}, u32[]{:S(2)}) copy-start(s32[30]{0:T(128)} %constant.225.clone) | copy-start | bytes 364
  7.2 585.8 %all-reduce.4.cloned.1.call-start = ((), (), s32[]{:S(2)}) async-start(), calls=%async_computation | async-start | bytes 262144 | tf_op jit(solution)/shard_map/psum | solution.py:207
  8.6 103.2 %collective-permute-start.3 = (f32[3,15]{1,0:T(4,128)}, f32[3,15]{1,0:T(4,128)}, u32[]{:S(2)}, u32[]{:S(2)}) collective-permute-start(f32[3,15]{1,0:T(4,128)} %get-tuple-element.382), channel_id=1, source_target_pairs={{1,0},{2,1},{3,2},{4,3},{5,4},{6,5},{7,6},{8,7},{9,8},{10,9},{11,1... | collective-permute-start | bytes 548 | tf_op jit(solution)/shard_map/ppermute | solution.py:36
  17.3 94.5 %collective-permute-start.2 = (f32[3,15]{1,0:T(4,128)}, f32[3,15]{1,0:T(4,128)}, u32[]{:S(2)}, u32[]{:S(2)}) collective-permute-start(f32[3,15]{1,0:T(4,128)} %get-tuple-element.381), channel_id=1, source_target_pairs={{0,1},{1,2},{2,3},{3,4},{4,5},{5,6},{6,7},{7,8},{8,9},{9,10},{10,1... | collective-permute-start | bytes 548 | tf_op jit(solution)/shard_map/ppermute | solution.py:34
  20.5 24.3 %copy-start.72 = (f32[1,256]{1,0:T(1,128)}, f32[1,256]{1,0:T(1,128)S(1)}, u32[]{:S(2)}) copy-start(f32[1,256]{1,0:T(1,128)S(1)} %get-tuple-element.386) | copy-start | bytes 3076
  21.1 23.6 %copy-start.74 = (f32[1,256]{1,0:T(1,128)}, f32[1,256]{1,0:T(1,128)S(1)}, u32[]{:S(2)}) copy-start(f32[1,256]{1,0:T(1,128)S(1)} %convert_element_type.90) | copy-start | bytes 3076
  21.9 15.3 collective-permute-start.1
  24.9 12.3 collective-permute-start
  37.4 26.0 %copy-start.32 = (f32[3,286]{1,0:T(4,128)}, f32[3,286]{1,0:T(4,128)S(1)}, u32[]{:S(2)}) copy-start(f32[3,286]{1,0:T(4,128)S(1)} %slice.1812) | copy-start | bytes 10300
  44.8 11.1 copy-start.31
  51.5 8.8 copy-start.39
  51.5 8.8 copy-start.41
  64.3 536.6 %copy-start.28 = (f32[286,5]{0,1:T(8,128)}, f32[286,5]{0,1:T(8,128)S(1)}, u32[]{:S(2)}) copy-start(f32[286,5]{0,1:T(8,128)S(1)} %fusion.255) | copy-start | bytes 17164
  71.6 21.1 %copy-start.25 = (f32[80,286]{1,0:T(8,128)S(1)}, f32[80,286]{1,0:T(8,128)}, u32[]{:S(2)}) copy-start(f32[80,286]{1,0:T(8,128)} %get-tuple-element.327) | copy-start | bytes 274564
  71.6 21.8 %copy-start.24 = (f32[80,286]{1,0:T(8,128)S(1)}, f32[80,286]{1,0:T(8,128)}, u32[]{:S(2)}) copy-start(f32[80,286]{1,0:T(8,128)} %get-tuple-element.326) | copy-start | bytes 274564
  71.6 22.4 %copy-start.23 = (f32[80,286]{1,0:T(8,128)S(1)}, f32[80,286]{1,0:T(8,128)}, u32[]{:S(2)}) copy-start(f32[80,286]{1,0:T(8,128)} %get-tuple-element.325) | copy-start | bytes 274564
  71.6 23.1 %copy-start.22 = (f32[80,286]{1,0:T(8,128)S(1)}, f32[80,286]{1,0:T(8,128)}, u32[]{:S(2)}) copy-start(f32[80,286]{1,0:T(8,128)} %get-tuple-element.324) | copy-start | bytes 274564
  71.6 23.8 %copy-start.21 = (f32[80,286]{1,0:T(8,128)S(1)}, f32[80,286]{1,0:T(8,128)}, u32[]{:S(2)}) copy-start(f32[80,286]{1,0:T(8,128)} %get-tuple-element.323) | copy-start | bytes 274564
  71.6 24.4 %copy-start.20 = (f32[80,286]{1,0:T(8,128)S(1)}, f32[80,286]{1,0:T(8,128)}, u32[]{:S(2)}) copy-start(f32[80,286]{1,0:T(8,128)} %get-tuple-element.322) | copy-start | bytes 274564
  71.6 25.1 %copy-start.19 = (f32[80,286]{1,0:T(8,128)S(1)}, f32[80,286]{1,0:T(8,128)}, u32[]{:S(2)}) copy-start(f32[80,286]{1,0:T(8,128)} %get-tuple-element.321) | copy-start | bytes 274564
  71.7 25.7 %copy-start.18 = (f32[80,286]{1,0:T(8,128)S(1)}, f32[80,286]{1,0:T(8,128)}, u32[]{:S(2)}) copy-start(f32[80,286]{1,0:T(8,128)} %get-tuple-element.320) | copy-start | bytes 274564
  71.7 26.4 %copy-start.17 = (f32[80,286]{1,0:T(8,128)S(1)}, f32[80,286]{1,0:T(8,128)}, u32[]{:S(2)}) copy-start(f32[80,286]{1,0:T(8,128)} %get-tuple-element.319) | copy-start | bytes 274564
  71.7 27.0 %copy-start.16 = (f32[80,286]{1,0:T(8,128)S(1)}, f32[80,286]{1,0:T(8,128)}, u32[]{:S(2)}) copy-start(f32[80,286]{1,0:T(8,128)} %get-tuple-element.318) | copy-start | bytes 274564
  71.7 27.7 %copy-start.15 = (f32[80,286]{1,0:T(8,128)S(1)}, f32[80,286]{1,0:T(8,128)}, u32[]{:S(2)}) copy-start(f32[80,286]{1,0:T(8,128)} %get-tuple-element.317) | copy-start | bytes 274564
  71.7 28.3 %copy-start.14 = (f32[80,286]{1,0:T(8,128)S(1)}, f32[80,286]{1,0:T(8,128)}, u32[]{:S(2)}) copy-start(f32[80,286]{1,0:T(8,128)} %get-tuple-element.316) | copy-start | bytes 274564
  71.7 29.0 %copy-start.13 = (f32[80,286]{1,0:T(8,128)S(1)}, f32[80,286]{1,0:T(8,128)}, u32[]{:S(2)}) copy-start(f32[80,286]{1,0:T(8,128)} %get-tuple-element.315) | copy-start | bytes 274564
  71.7 29.6 %copy-start.12 = (f32[80,286]{1,0:T(8,128)S(1)}, f32[80,286]{1,0:T(8,128)}, u32[]{:S(2)}) copy-start(f32[80,286]{1,0:T(8,128)} %get-tuple-element.314) | copy-start | bytes 274564
  127.5 470.4 %copy-start.51 = (f32[316]{0:T(512)S(1)}, f32[316]{0:T(512)}, u32[]{:S(2)}) copy-start(f32[316]{0:T(512)} %copy-done.50) | copy-start | bytes 3796
  127.5 470.7 %copy-start.48 = (f32[316]{0:T(512)S(1)}, f32[316]{0:T(512)}, u32[]{:S(2)}) copy-start(f32[316]{0:T(512)} %copy-done.47) | copy-start | bytes 3796
  127.8 470.7 %copy-start.45 = (f32[316]{0:T(512)S(1)}, f32[316]{0:T(512)}, u32[]{:S(2)}) copy-start(f32[316]{0:T(512)} %copy-done.44) | copy-start | bytes 3796
  128.1 470.6 %copy-start.42 = (f32[316]{0:T(512)S(1)}, f32[316]{0:T(512)}, u32[]{:S(2)}) copy-start(f32[316]{0:T(512)} %copy-done.41) | copy-start | bytes 3796
  128.6 470.3 %copy-start.40 = (f32[316]{0:T(512)S(1)}, f32[316]{0:T(512)}, u32[]{:S(2)}) copy-start(f32[316]{0:T(512)} %copy-done.39) | copy-start | bytes 3796
  131.8 944.3 %all-reduce.6.cloned.1.call-start = ((), (), s32[]{:S(2)}) async-start(), calls=%async_computation.1 | async-start | bytes 262144 | tf_op jit(solution)/shard_map/psum | solution.py:207
  609.3 10.6 copy-start.37
  609.3 10.6 copy-start.54
  609.3 10.6 copy-start.57
  609.3 10.6 copy-start.60
  609.3 10.6 copy-start.63
  609.3 10.6 copy-start.66
  623.2 457.7 %copy-start.52 = (f32[316]{0:T(512)S(1)}, f32[316]{0:T(512)}, u32[]{:S(2)}) copy-start(f32[316]{0:T(512)} %copy-done.50) | copy-start | bytes 3796
  623.2 458.0 %copy-start.49 = (f32[316]{0:T(512)S(1)}, f32[316]{0:T(512)}, u32[]{:S(2)}) copy-start(f32[316]{0:T(512)} %copy-done.47) | copy-start | bytes 3796
  623.2 458.2 %copy-start.46 = (f32[316]{0:T(512)S(1)}, f32[316]{0:T(512)}, u32[]{:S(2)}) copy-start(f32[316]{0:T(512)} %copy-done.44) | copy-start | bytes 3796
  624.7 457.1 %copy-start.43 = (f32[316]{0:T(512)S(1)}, f32[316]{0:T(512)}, u32[]{:S(2)}) copy-start(f32[316]{0:T(512)} %copy-done.41) | copy-start | bytes 3796
  628.6 928.2 %all-reduce.8.cloned.1.call-start = ((), (), s32[]{:S(2)}) async-start(), calls=%async_computation.2 | async-start | bytes 262144 | tf_op jit(solution)/shard_map/psum | solution.py:207
  1092.4 8.8 copy-start.64
  1092.4 8.8 copy-start.67
  1104.6 456.0 %copy-start.4 = (f32[5,81,80]{2,1,0:T(8,128)S(1)}, f32[5,81,80]{2,1,0:T(8,128)}, u32[]{:S(2)}) copy-start(f32[5,81,80]{2,1,0:T(8,128)} %copy-done.3) | copy-start | bytes 388804
  (42 other events, 259.5 us)
Sparse Core Ops, SparseCore 0:
  131.9 461.0 all-reduce.3
  628.7 447.2 all-reduce.5
  1110.2 446.5 all-reduce.7

commit v2 on v1

--- a/solution.py
+++ b/solution.py
@@ -14,6 +14,7 @@
 SNAP = ("snap_0", "snap_1")
 BRICK = ("brick_0", "brick_1", "brick_2")
 SNAP_BRICK = ("snap_0", "snap_1", "brick_0", "brick_1", "brick_2")
+BUTTERFLY_ORDER = ("brick_2", "snap_1", "brick_1", "snap_0", "brick_0")
 
 
 cutoff_sq = 36.0
@@ -42,6 +43,17 @@
 
 def by_axis(shard, axes):
     return functools.reduce(lax.psum, axes, shard)
+
+
+def butterfly_sum(shard, axes):
+    for axis in axes:
+        count = lax.axis_size(axis)
+        step = 1
+        while step < count:
+            partners = [(i, i ^ step) for i in range(count)]
+            shard = shard + lax.ppermute(shard, axis, partners)
+            step *= 2
+    return shard
 
 
 def window_offsets():
@@ -204,7 +216,7 @@
         packed = jnp.concatenate(
             [local_terms.reshape(-1), jnp.sum(raw_left * raw_left)[None]]
         )
-        packed = lax.psum(packed, SNAP_BRICK)
+        packed = butterfly_sum(packed, BUTTERFLY_ORDER)
         totals = packed[:-1].reshape(local_terms.shape)
         squares = packed[-1]
         beta_norm = jnp.sqrt(squares / left_total + tiny)

time: 1580 us -> 455 us (0.29)
  the two profiles are of different devices: /device:TPU:1 before, /device:TPU:486 now
where the time goes in v2:
time: 455 us; the launch traced here: 450 us
  waiting for transfers between devices  164 us (36%)
  starting transfers between devices  104 us (23%)
  local copies, waits for them, and re-layouts  102 us (22%)
  other arithmetic  35.4 us (8%)
  matrix products  32.5 us (7%)
  between operations  12.2 us (3%)
    ppermute x27, waiting for transfers between devices, butterfly_sum(): shard = shard + lax.ppermute(shard, axis, partners)  164 us
    ppermute x27, starting transfers between devices, butterfly_sum(): shard = shard + lax.ppermute(shard, axis, partners)  92.1 us
    unnamed x427, local copies, waits for them, and re-layouts  51.7 us
    dot_general x3, matrix products, back_terms(): jnp.einsum('ozi,oni->zni', other, slope * project[:, None, :], precision=...  10.8 us
    dot_general x3, matrix products, pull_force(): outward = jnp.einsum('ozi,zni->oni', other, own_grid, precision=HIGHEST)  10.1 us
  transfers between devices with their start and end apart: 31, of which 27 were waited for; matrix products, arithmetic and copies ran while one was open for 18% of the time, Pallas kernels for 0%

profile of v2, /device:TPU:486, one launch (start us, length us, event | category | flops | bytes accessed | tf_op | source)
XLA Modules:
  0.0 449.6 jit_solution(3149868012729092813)
XLA Ops:
  2.0 2.7 collective-permute-start.3
  9.6 4.9 %collective-permute-start.1 = (f32[5,45]{1,0:T(8,128)S(1)}, f32[5,45]{1,0:T(8,128)S(1)}, u32[]{:S(2)}, u32[]{:S(2)}) collective-permute-start(f32[5,45]{1,0:T(8,128)S(1)} %get-tuple-element.372), channel_id=1, source_target_pairs={{1,0},{2,1},{3,2},{4,3},{5,4},{6,5},{7,6},{8,7},{9,8},{10,9},{11,1... | collective-permute-start | bytes 2708 | tf_op jit(solution)/shard_map/ppermute | solution.py:37
  32.7 3.3 convolution_bitcast_fusion
  48.0 3.4 fusion.2
  87.8 3.1 fusion.148
  90.9 2.8 stack.1287
  106.5 4.1 multiply_reduce_fusion.13
  120.2 5.5 %collective-permute-done.5 = f32[32401]{0:T(1024)S(1)} collective-permute-done((f32[32401]{0:T(1024)S(1)}, f32[32401]{0:T(1024)S(1)}, u32[]{:S(2)}, u32[]{:S(2)}) %collective-permute-start.5) | collective-permute-done | bytes 129636 | tf_op jit(solution)/shard_map/ppermute | solution.py:54
  125.7 5.4 %collective-permute-start.6 = (f32[32401]{0:T(1024)S(1)}, f32[32401]{0:T(1024)S(1)}, u32[]{:S(2)}, u32[]{:S(2)}) collective-permute-start(f32[32401]{0:T(1024)S(1)} %add.2656), channel_id=1, source_target_pairs={{0,2},{2,0},{1,3},{3,1},{4,6},{6,4},{5,7},{7,5},{8,10},{10,8},{9,1... | collective-permute-start | bytes 388820 | tf_op jit(solution)/shard_map/ppermute | solution.py:54
  131.1 3.0 collective-permute-done.6
  134.1 3.5 collective-permute-start.7
  137.6 3.4 collective-permute-done.7
  141.0 5.1 %collective-permute-start.8 = (f32[32401]{0:T(1024)S(1)}, f32[32401]{0:T(1024)S(1)}, u32[]{:S(2)}, u32[]{:S(2)}) collective-permute-start(f32[32401]{0:T(1024)S(1)} %add.2658), channel_id=1, source_target_pairs={{0,256},{128,384},{256,0},{384,128},{1,257},{129,385},{257,1},{385... | collective-permute-start | bytes 388820 | tf_op jit(solution)/shard_map/ppermute | solution.py:54
  146.1 3.3 collective-permute-done.8
  149.4 6.8 %collective-permute-start.9 = (f32[32401]{0:T(1024)S(1)}, f32[32401]{0:T(1024)S(1)}, u32[]{:S(2)}, u32[]{:S(2)}) collective-permute-start(f32[32401]{0:T(1024)S(1)} %add.2659), channel_id=1, source_target_pairs={{0,4},{4,0},{8,12},{12,8},{16,20},{20,16},{24,28},{28,24},{32,36},... | collective-permute-start | bytes 388820 | tf_op jit(solution)/shard_map/ppermute | solution.py:54
  156.2 2.9 collective-permute-done.9
  159.1 4.5 %collective-permute-start.10 = (f32[32401]{0:T(1024)S(1)}, f32[32401]{0:T(1024)S(1)}, u32[]{:S(2)}, u32[]{:S(2)}) collective-permute-start(f32[32401]{0:T(1024)S(1)} %add.2660), channel_id=1, source_target_pairs={{0,8},{4,12},{8,0},{12,4},{16,24},{20,28},{24,16},{28,20},{32,40},... | collective-permute-start | bytes 388820 | tf_op jit(solution)/shard_map/ppermute | solution.py:54
  163.6 3.2 collective-permute-done.10
  166.9 12.4 %collective-permute-start.11 = (f32[32401]{0:T(1024)S(1)}, f32[32401]{0:T(1024)S(1)}, u32[]{:S(2)}, u32[]{:S(2)}) collective-permute-start(f32[32401]{0:T(1024)S(1)} %add.2661), channel_id=1, source_target_pairs={{0,16},{4,20},{8,24},{12,28},{16,0},{20,4},{24,8},{28,12},{32,48},... | collective-permute-start | bytes 388820 | tf_op jit(solution)/shard_map/ppermute | solution.py:54
  179.3 9.1 %collective-permute-done.11 = f32[32401]{0:T(1024)S(1)} collective-permute-done((f32[32401]{0:T(1024)S(1)}, f32[32401]{0:T(1024)S(1)}, u32[]{:S(2)}, u32[]{:S(2)}) %collective-permute-start.11) | collective-permute-done | bytes 129636 | tf_op jit(solution)/shard_map/ppermute | solution.py:54
  188.4 3.4 collective-permute-start.12
  192.0 12.0 %collective-permute-done.12 = f32[32401]{0:T(1024)S(1)} collective-permute-done((f32[32401]{0:T(1024)S(1)}, f32[32401]{0:T(1024)S(1)}, u32[]{:S(2)}, u32[]{:S(2)}) %collective-permute-start.12) | collective-permute-done | bytes 129636 | tf_op jit(solution)/shard_map/ppermute | solution.py:54
  213.1 3.4 fusion.1
  229.4 3.3 multiply_reduce_fusion.8
  241.3 2.7 collective-permute-start.14
  244.1 4.7 %collective-permute-done.14 = f32[32401]{0:T(1024)S(1)} collective-permute-done((f32[32401]{0:T(1024)S(1)}, f32[32401]{0:T(1024)S(1)}, u32[]{:S(2)}, u32[]{:S(2)}) %collective-permute-start.14) | collective-permute-done | bytes 129636 | tf_op jit(solution)/shard_map/ppermute | solution.py:54
  250.7 6.4 %collective-permute-done.15 = f32[32401]{0:T(1024)S(1)} collective-permute-done((f32[32401]{0:T(1024)S(1)}, f32[32401]{0:T(1024)S(1)}, u32[]{:S(2)}, u32[]{:S(2)}) %collective-permute-start.15) | collective-permute-done | bytes 129636 | tf_op jit(solution)/shard_map/ppermute | solution.py:54
  257.2 3.5 collective-permute-start.16
  260.7 3.4 collective-permute-done.16
  264.0 5.1 %collective-permute-start.17 = (f32[32401]{0:T(1024)S(1)}, f32[32401]{0:T(1024)S(1)}, u32[]{:S(2)}, u32[]{:S(2)}) collective-permute-start(f32[32401]{0:T(1024)S(1)} %add.2716), channel_id=1, source_target_pairs={{0,256},{128,384},{256,0},{384,128},{1,257},{129,385},{257,1},{385... | collective-permute-start | bytes 388820 | tf_op jit(solution)/shard_map/ppermute | solution.py:54
  269.1 3.3 collective-permute-done.17
  274.4 4.9 %collective-permute-done.18 = f32[32401]{0:T(1024)S(1)} collective-permute-done((f32[32401]{0:T(1024)S(1)}, f32[32401]{0:T(1024)S(1)}, u32[]{:S(2)}, u32[]{:S(2)}) %collective-permute-start.18) | collective-permute-done | bytes 129636 | tf_op jit(solution)/shard_map/ppermute | solution.py:54
  281.2 7.2 %collective-permute-done.19 = f32[32401]{0:T(1024)S(1)} collective-permute-done((f32[32401]{0:T(1024)S(1)}, f32[32401]{0:T(1024)S(1)}, u32[]{:S(2)}, u32[]{:S(2)}) %collective-permute-start.19) | collective-permute-done | bytes 129636 | tf_op jit(solution)/shard_map/ppermute | solution.py:54
  291.0 14.8 %collective-permute-done.20 = f32[32401]{0:T(1024)S(1)} collective-permute-done((f32[32401]{0:T(1024)S(1)}, f32[32401]{0:T(1024)S(1)}, u32[]{:S(2)}, u32[]{:S(2)}) %collective-permute-start.20) | collective-permute-done | bytes 129636 | tf_op jit(solution)/shard_map/ppermute | solution.py:54
  305.8 2.9 collective-permute-start.21
  308.8 12.6 %collective-permute-done.21 = f32[32401]{0:T(1024)S(1)} collective-permute-done((f32[32401]{0:T(1024)S(1)}, f32[32401]{0:T(1024)S(1)}, u32[]{:S(2)}, u32[]{:S(2)}) %collective-permute-start.21) | collective-permute-done | bytes 129636 | tf_op jit(solution)/shard_map/ppermute | solution.py:54
  330.4 3.4 fusion
  344.9 3.3 multiply_reduce_fusion.3
  359.6 4.7 %collective-permute-done.23 = f32[32401]{0:T(1024)S(1)} collective-permute-done((f32[32401]{0:T(1024)S(1)}, f32[32401]{0:T(1024)S(1)}, u32[]{:S(2)}, u32[]{:S(2)}) %collective-permute-start.23) | collective-permute-done | bytes 129636 | tf_op jit(solution)/shard_map/ppermute | solution.py:54
  366.3 6.4 %collective-permute-done.24 = f32[32401]{0:T(1024)S(1)} collective-permute-done((f32[32401]{0:T(1024)S(1)}, f32[32401]{0:T(1024)S(1)}, u32[]{:S(2)}, u32[]{:S(2)}) %collective-permute-start.24) | collective-permute-done | bytes 129636 | tf_op jit(solution)/shard_map/ppermute | solution.py:54
  372.8 3.5 collective-permute-start.25
  376.2 3.4 collective-permute-done.25
  379.6 5.1 %collective-permute-start.26 = (f32[32401]{0:T(1024)S(1)}, f32[32401]{0:T(1024)S(1)}, u32[]{:S(2)}, u32[]{:S(2)}) collective-permute-start(f32[32401]{0:T(1024)S(1)} %add.2791), channel_id=1, source_target_pairs={{0,256},{128,384},{256,0},{384,128},{1,257},{129,385},{257,1},{385... | collective-permute-start | bytes 388820 | tf_op jit(solution)/shard_map/ppermute | solution.py:54
  384.7 3.3 collective-permute-done.26
  390.0 4.9 %collective-permute-done.27 = f32[32401]{0:T(1024)S(1)} collective-permute-done((f32[32401]{0:T(1024)S(1)}, f32[32401]{0:T(1024)S(1)}, u32[]{:S(2)}, u32[]{:S(2)}) %collective-permute-start.27) | collective-permute-done | bytes 129636 | tf_op jit(solution)/shard_map/ppermute | solution.py:54
  396.8 7.2 %collective-permute-done.28 = f32[32401]{0:T(1024)S(1)} collective-permute-done((f32[32401]{0:T(1024)S(1)}, f32[32401]{0:T(1024)S(1)}, u32[]{:S(2)}, u32[]{:S(2)}) %collective-permute-start.28) | collective-permute-done | bytes 129636 | tf_op jit(solution)/shard_map/ppermute | solution.py:54
  406.0 20.7 %collective-permute-done.29 = f32[32401]{0:T(1024)S(1)} collective-permute-done((f32[32401]{0:T(1024)S(1)}, f32[32401]{0:T(1024)S(1)}, u32[]{:S(2)}, u32[]{:S(2)}) %collective-permute-start.29) | collective-permute-done | bytes 129636 | tf_op jit(solution)/shard_map/ppermute | solution.py:54
  432.7 9.6 %collective-permute-done.30 = f32[32401]{0:T(1024)S(1)} collective-permute-done((f32[32401]{0:T(1024)S(1)}, f32[32401]{0:T(1024)S(1)}, u32[]{:S(2)}, u32[]{:S(2)}) %collective-permute-start.30) | collective-permute-done | bytes 129636 | tf_op jit(solution)/shard_map/ppermute | solution.py:54
  (736 shorter events, 175.8 us)
Async XLA Ops:
  0.6 29.7 %copy-start.63 = (pred[30]{0:T(512)(128)(4,1)S(1)}, pred[30]{0:T(512)(128)(4,1)}, u32[]{:S(2)}) copy-start(pred[30]{0:T(512)(128)(4,1)} %constant.224.clone) | copy-start | bytes 94
  0.6 29.7 %copy-start.66 = (s32[30]{0:T(128)S(1)}, s32[30]{0:T(128)}, u32[]{:S(2)}) copy-start(s32[30]{0:T(128)} %constant.225.clone) | copy-start | bytes 364
  2.0 92.5 %collective-permute-start.3 = (f32[3,15]{1,0:T(4,128)}, f32[3,15]{1,0:T(4,128)}, u32[]{:S(2)}, u32[]{:S(2)}) collective-permute-start(f32[3,15]{1,0:T(4,128)} %get-tuple-element.382), channel_id=1, source_target_pairs={{1,0},{2,1},{3,2},{4,3},{5,4},{6,5},{7,6},{8,7},{9,8},{10,9},{11,1... | collective-permute-start | bytes 548 | tf_op jit(solution)/shard_map/ppermute | solution.py:37
  4.8 89.7 %collective-permute-start.2 = (f32[3,15]{1,0:T(4,128)}, f32[3,15]{1,0:T(4,128)}, u32[]{:S(2)}, u32[]{:S(2)}) collective-permute-start(f32[3,15]{1,0:T(4,128)} %get-tuple-element.381), channel_id=1, source_target_pairs={{0,1},{1,2},{2,3},{3,4},{4,5},{5,6},{6,7},{7,8},{8,9},{9,10},{10,1... | collective-permute-start | bytes 548 | tf_op jit(solution)/shard_map/ppermute | solution.py:35
  9.6 15.2 %collective-permute-start.1 = (f32[5,45]{1,0:T(8,128)S(1)}, f32[5,45]{1,0:T(8,128)S(1)}, u32[]{:S(2)}, u32[]{:S(2)}) collective-permute-start(f32[5,45]{1,0:T(8,128)S(1)} %get-tuple-element.372), channel_id=1, source_target_pairs={{1,0},{2,1},{3,2},{4,3},{5,4},{6,5},{7,6},{8,7},{9,8},{10,9},{11,1... | collective-permute-start | bytes 2708 | tf_op jit(solution)/shard_map/ppermute | solution.py:37
  14.6 10.2 %collective-permute-start = (f32[5,45]{1,0:T(8,128)S(1)}, f32[5,45]{1,0:T(8,128)S(1)}, u32[]{:S(2)}, u32[]{:S(2)}) collective-permute-start(f32[5,45]{1,0:T(8,128)S(1)} %get-tuple-element.371), channel_id=1, source_target_pairs={{0,1},{1,2},{2,3},{3,4},{4,5},{5,6},{6,7},{7,8},{8,9},{9,10},{10,1... | collective-permute-start | bytes 2708 | tf_op jit(solution)/shard_map/ppermute | solution.py:35
  37.7 169.7 %copy-start.38 = (f32[316]{0:T(512)}, f32[316]{0:T(512)S(1)}, u32[]{:S(2)}) copy-start(f32[316]{0:T(512)S(1)} %get-tuple-element.196) | copy-start | bytes 3796
  43.1 67.9 %copy-start.52 = (f32[1,256]{1,0:T(1,128)}, f32[1,256]{1,0:T(1,128)S(1)}, u32[]{:S(2)}) copy-start(f32[1,256]{1,0:T(1,128)S(1)} %get-tuple-element.366) | copy-start | bytes 3076
  43.1 68.2 %copy-start.49 = (f32[1,256]{1,0:T(1,128)}, f32[1,256]{1,0:T(1,128)S(1)}, u32[]{:S(2)}) copy-start(f32[1,256]{1,0:T(1,128)S(1)} %get-tuple-element.370) | copy-start | bytes 3076
  43.1 68.5 %copy-start.46 = (f32[1,256]{1,0:T(1,128)}, f32[1,256]{1,0:T(1,128)S(1)}, u32[]{:S(2)}) copy-start(f32[1,256]{1,0:T(1,128)S(1)} %get-tuple-element.369) | copy-start | bytes 3076
  43.1 68.7 %copy-start.43 = (f32[1,256]{1,0:T(1,128)}, f32[1,256]{1,0:T(1,128)S(1)}, u32[]{:S(2)}) copy-start(f32[1,256]{1,0:T(1,128)S(1)} %get-tuple-element.368) | copy-start | bytes 3076
  43.1 69.0 %copy-start.40 = (f32[1,256]{1,0:T(1,128)}, f32[1,256]{1,0:T(1,128)S(1)}, u32[]{:S(2)}) copy-start(f32[1,256]{1,0:T(1,128)S(1)} %get-tuple-element.367) | copy-start | bytes 3076
  45.3 49.0 %copy-start.9 = (f32[30,5,286]{2,1,0:T(8,128)}, f32[30,5,286]{2,1,0:T(8,128)S(1)}, u32[]{:S(2)}) copy-start(f32[30,5,286]{2,1,0:T(8,128)S(1)} %constant_dynamic-update-slice_fusion.76) | copy-start | bytes 514804
  53.7 28.3 %copy-start.14 = (f32[80,286]{1,0:T(8,128)S(1)}, f32[80,286]{1,0:T(8,128)}, u32[]{:S(2)}) copy-start(f32[80,286]{1,0:T(8,128)} %get-tuple-element.316) | copy-start | bytes 274564
  53.7 29.0 %copy-start.13 = (f32[80,286]{1,0:T(8,128)S(1)}, f32[80,286]{1,0:T(8,128)}, u32[]{:S(2)}) copy-start(f32[80,286]{1,0:T(8,128)} %get-tuple-element.315) | copy-start | bytes 274564
  53.7 29.6 %copy-start.12 = (f32[80,286]{1,0:T(8,128)S(1)}, f32[80,286]{1,0:T(8,128)}, u32[]{:S(2)}) copy-start(f32[80,286]{1,0:T(8,128)} %get-tuple-element.314) | copy-start | bytes 274564
  53.7 30.3 %copy-start.11 = (f32[80,286]{1,0:T(8,128)S(1)}, f32[80,286]{1,0:T(8,128)}, u32[]{:S(2)}) copy-start(f32[80,286]{1,0:T(8,128)} %get-tuple-element.313) | copy-start | bytes 274564
  114.3 3.2 collective-permute-start.4
  118.3 7.4 %collective-permute-start.5 = (f32[32401]{0:T(1024)S(1)}, f32[32401]{0:T(1024)S(1)}, u32[]{:S(2)}, u32[]{:S(2)}) collective-permute-start(f32[32401]{0:T(1024)S(1)} %fusion.314), channel_id=1, source_target_pairs={{0,64},{64,0},{1,65},{65,1},{2,66},{66,2},{3,67},{67,3},{4,68},{68... | collective-permute-start | bytes 388820 | tf_op jit(solution)/shard_map/ppermute | solution.py:54
  125.7 8.4 %collective-permute-start.6 = (f32[32401]{0:T(1024)S(1)}, f32[32401]{0:T(1024)S(1)}, u32[]{:S(2)}, u32[]{:S(2)}) collective-permute-start(f32[32401]{0:T(1024)S(1)} %add.2656), channel_id=1, source_target_pairs={{0,2},{2,0},{1,3},{3,1},{4,6},{6,4},{5,7},{7,5},{8,10},{10,8},{9,1... | collective-permute-start | bytes 388820 | tf_op jit(solution)/shard_map/ppermute | solution.py:54
  134.1 6.9 %collective-permute-start.7 = (f32[32401]{0:T(1024)S(1)}, f32[32401]{0:T(1024)S(1)}, u32[]{:S(2)}, u32[]{:S(2)}) collective-permute-start(f32[32401]{0:T(1024)S(1)} %add.2657), channel_id=1, source_target_pairs={{0,128},{128,0},{256,384},{384,256},{1,129},{129,1},{257,385},{385... | collective-permute-start | bytes 388820 | tf_op jit(solution)/shard_map/ppermute | solution.py:54
  141.0 8.4 %collective-permute-start.8 = (f32[32401]{0:T(1024)S(1)}, f32[32401]{0:T(1024)S(1)}, u32[]{:S(2)}, u32[]{:S(2)}) collective-permute-start(f32[32401]{0:T(1024)S(1)} %add.2658), channel_id=1, source_target_pairs={{0,256},{128,384},{256,0},{384,128},{1,257},{129,385},{257,1},{385... | collective-permute-start | bytes 388820 | tf_op jit(solution)/shard_map/ppermute | solution.py:54
  149.4 9.7 %collective-permute-start.9 = (f32[32401]{0:T(1024)S(1)}, f32[32401]{0:T(1024)S(1)}, u32[]{:S(2)}, u32[]{:S(2)}) collective-permute-start(f32[32401]{0:T(1024)S(1)} %add.2659), channel_id=1, source_target_pairs={{0,4},{4,0},{8,12},{12,8},{16,20},{20,16},{24,28},{28,24},{32,36},... | collective-permute-start | bytes 388820 | tf_op jit(solution)/shard_map/ppermute | solution.py:54
  159.1 7.8 %collective-permute-start.10 = (f32[32401]{0:T(1024)S(1)}, f32[32401]{0:T(1024)S(1)}, u32[]{:S(2)}, u32[]{:S(2)}) collective-permute-start(f32[32401]{0:T(1024)S(1)} %add.2660), channel_id=1, source_target_pairs={{0,8},{4,12},{8,0},{12,4},{16,24},{20,28},{24,16},{28,20},{32,40},... | collective-permute-start | bytes 388820 | tf_op jit(solution)/shard_map/ppermute | solution.py:54
  166.9 21.5 %collective-permute-start.11 = (f32[32401]{0:T(1024)S(1)}, f32[32401]{0:T(1024)S(1)}, u32[]{:S(2)}, u32[]{:S(2)}) collective-permute-start(f32[32401]{0:T(1024)S(1)} %add.2661), channel_id=1, source_target_pairs={{0,16},{4,20},{8,24},{12,28},{16,0},{20,4},{24,8},{28,12},{32,48},... | collective-permute-start | bytes 388820 | tf_op jit(solution)/shard_map/ppermute | solution.py:54
  188.4 15.6 %collective-permute-start.12 = (f32[32401]{0:T(1024)S(1)}, f32[32401]{0:T(1024)S(1)}, u32[]{:S(2)}, u32[]{:S(2)}) collective-permute-start(f32[32401]{0:T(1024)S(1)} %add.2662), channel_id=1, source_target_pairs={{0,32},{4,36},{8,40},{12,44},{16,48},{20,52},{24,56},{28,60},{32,0... | collective-permute-start | bytes 388820 | tf_op jit(solution)/shard_map/ppermute | solution.py:54
  236.3 88.4 %copy-start.39 = (f32[316]{0:T(512)S(1)}, f32[316]{0:T(512)}, u32[]{:S(2)}) copy-start(f32[316]{0:T(512)} %copy-done.38) | copy-start | bytes 3796
  237.4 3.2 collective-permute-start.13
  241.3 7.4 %collective-permute-start.14 = (f32[32401]{0:T(1024)S(1)}, f32[32401]{0:T(1024)S(1)}, u32[]{:S(2)}, u32[]{:S(2)}) collective-permute-start(f32[32401]{0:T(1024)S(1)} %fusion.313), channel_id=1, source_target_pairs={{0,64},{64,0},{1,65},{65,1},{2,66},{66,2},{3,67},{67,3},{4,68},{68... | collective-permute-start | bytes 388820 | tf_op jit(solution)/shard_map/ppermute | solution.py:54
  248.8 8.4 %collective-permute-start.15 = (f32[32401]{0:T(1024)S(1)}, f32[32401]{0:T(1024)S(1)}, u32[]{:S(2)}, u32[]{:S(2)}) collective-permute-start(f32[32401]{0:T(1024)S(1)} %add.2714), channel_id=1, source_target_pairs={{0,2},{2,0},{1,3},{3,1},{4,6},{6,4},{5,7},{7,5},{8,10},{10,8},{9,1... | collective-permute-start | bytes 388820 | tf_op jit(solution)/shard_map/ppermute | solution.py:54
  257.2 6.9 %collective-permute-start.16 = (f32[32401]{0:T(1024)S(1)}, f32[32401]{0:T(1024)S(1)}, u32[]{:S(2)}, u32[]{:S(2)}) collective-permute-start(f32[32401]{0:T(1024)S(1)} %add.2715), channel_id=1, source_target_pairs={{0,128},{128,0},{256,384},{384,256},{1,129},{129,1},{257,385},{385... | collective-permute-start | bytes 388820 | tf_op jit(solution)/shard_map/ppermute | solution.py:54
  264.0 8.4 %collective-permute-start.17 = (f32[32401]{0:T(1024)S(1)}, f32[32401]{0:T(1024)S(1)}, u32[]{:S(2)}, u32[]{:S(2)}) collective-permute-start(f32[32401]{0:T(1024)S(1)} %add.2716), channel_id=1, source_target_pairs={{0,256},{128,384},{256,0},{384,128},{1,257},{129,385},{257,1},{385... | collective-permute-start | bytes 388820 | tf_op jit(solution)/shard_map/ppermute | solution.py:54
  272.4 6.9 %collective-permute-start.18 = (f32[32401]{0:T(1024)S(1)}, f32[32401]{0:T(1024)S(1)}, u32[]{:S(2)}, u32[]{:S(2)}) collective-permute-start(f32[32401]{0:T(1024)S(1)} %add.2717), channel_id=1, source_target_pairs={{0,4},{4,0},{8,12},{12,8},{16,20},{20,16},{24,28},{28,24},{32,36},... | collective-permute-start | bytes 388820 | tf_op jit(solution)/shard_map/ppermute | solution.py:54
  279.3 9.1 %collective-permute-start.19 = (f32[32401]{0:T(1024)S(1)}, f32[32401]{0:T(1024)S(1)}, u32[]{:S(2)}, u32[]{:S(2)}) collective-permute-start(f32[32401]{0:T(1024)S(1)} %add.2718), channel_id=1, source_target_pairs={{0,8},{4,12},{8,0},{12,4},{16,24},{20,28},{24,16},{28,20},{32,40},... | collective-permute-start | bytes 388820 | tf_op jit(solution)/shard_map/ppermute | solution.py:54
  288.5 17.4 %collective-permute-start.20 = (f32[32401]{0:T(1024)S(1)}, f32[32401]{0:T(1024)S(1)}, u32[]{:S(2)}, u32[]{:S(2)}) collective-permute-start(f32[32401]{0:T(1024)S(1)} %add.2719), channel_id=1, source_target_pairs={{0,16},{4,20},{8,24},{12,28},{16,0},{20,4},{24,8},{28,12},{32,48},... | collective-permute-start | bytes 388820 | tf_op jit(solution)/shard_map/ppermute | solution.py:54
  305.8 15.6 %collective-permute-start.21 = (f32[32401]{0:T(1024)S(1)}, f32[32401]{0:T(1024)S(1)}, u32[]{:S(2)}, u32[]{:S(2)}) collective-permute-start(f32[32401]{0:T(1024)S(1)} %add.2720), channel_id=1, source_target_pairs={{0,32},{4,36},{8,40},{12,44},{16,48},{20,52},{24,56},{28,60},{32,0... | collective-permute-start | bytes 388820 | tf_op jit(solution)/shard_map/ppermute | solution.py:54
  348.2 80.4 %copy-start.28 = (f32[5,81,80]{1,2,0:T(8,128)S(1)}, f32[5,81,80]{1,2,0:T(8,128)}, u32[]{:S(2)}) copy-start(f32[5,81,80]{1,2,0:T(8,128)} %param.41) | copy-start | bytes 388804
  348.2 82.0 %copy-start.29 = (f32[5,81,80]{1,2,0:T(8,128)S(1)}, f32[5,81,80]{1,2,0:T(8,128)}, u32[]{:S(2)}) copy-start(f32[5,81,80]{1,2,0:T(8,128)} %param.42) | copy-start | bytes 388804
  350.8 93.7 %copy-start.4 = (f32[5,81,80]{2,1,0:T(8,128)S(1)}, f32[5,81,80]{2,1,0:T(8,128)}, u32[]{:S(2)}) copy-start(f32[5,81,80]{2,1,0:T(8,128)} %copy-done.3) | copy-start | bytes 388804
  353.0 3.2 collective-permute-start.22
  356.9 7.4 %collective-permute-start.23 = (f32[32401]{0:T(1024)S(1)}, f32[32401]{0:T(1024)S(1)}, u32[]{:S(2)}, u32[]{:S(2)}) collective-permute-start(f32[32401]{0:T(1024)S(1)} %fusion.312), channel_id=1, source_target_pairs={{0,64},{64,0},{1,65},{65,1},{2,66},{66,2},{3,67},{67,3},{4,68},{68... | collective-permute-start | bytes 388820 | tf_op jit(solution)/shard_map/ppermute | solution.py:54
  364.4 8.4 %collective-permute-start.24 = (f32[32401]{0:T(1024)S(1)}, f32[32401]{0:T(1024)S(1)}, u32[]{:S(2)}, u32[]{:S(2)}) collective-permute-start(f32[32401]{0:T(1024)S(1)} %add.2789), channel_id=1, source_target_pairs={{0,2},{2,0},{1,3},{3,1},{4,6},{6,4},{5,7},{7,5},{8,10},{10,8},{9,1... | collective-permute-start | bytes 388820 | tf_op jit(solution)/shard_map/ppermute | solution.py:54
  372.8 6.9 %collective-permute-start.25 = (f32[32401]{0:T(1024)S(1)}, f32[32401]{0:T(1024)S(1)}, u32[]{:S(2)}, u32[]{:S(2)}) collective-permute-start(f32[32401]{0:T(1024)S(1)} %add.2790), channel_id=1, source_target_pairs={{0,128},{128,0},{256,384},{384,256},{1,129},{129,1},{257,385},{385... | collective-permute-start | bytes 388820 | tf_op jit(solution)/shard_map/ppermute | solution.py:54
  379.6 8.4 %collective-permute-start.26 = (f32[32401]{0:T(1024)S(1)}, f32[32401]{0:T(1024)S(1)}, u32[]{:S(2)}, u32[]{:S(2)}) collective-permute-start(f32[32401]{0:T(1024)S(1)} %add.2791), channel_id=1, source_target_pairs={{0,256},{128,384},{256,0},{384,128},{1,257},{129,385},{257,1},{385... | collective-permute-start | bytes 388820 | tf_op jit(solution)/shard_map/ppermute | solution.py:54
  388.0 6.9 %collective-permute-start.27 = (f32[32401]{0:T(1024)S(1)}, f32[32401]{0:T(1024)S(1)}, u32[]{:S(2)}, u32[]{:S(2)}) collective-permute-start(f32[32401]{0:T(1024)S(1)} %add.2792), channel_id=1, source_target_pairs={{0,4},{4,0},{8,12},{12,8},{16,20},{20,16},{24,28},{28,24},{32,36},... | collective-permute-start | bytes 388820 | tf_op jit(solution)/shard_map/ppermute | solution.py:54
  394.9 9.1 %collective-permute-start.28 = (f32[32401]{0:T(1024)S(1)}, f32[32401]{0:T(1024)S(1)}, u32[]{:S(2)}, u32[]{:S(2)}) collective-permute-start(f32[32401]{0:T(1024)S(1)} %add.2793), channel_id=1, source_target_pairs={{0,8},{4,12},{8,0},{12,4},{16,24},{20,28},{24,16},{28,20},{32,40},... | collective-permute-start | bytes 388820 | tf_op jit(solution)/shard_map/ppermute | solution.py:54
  404.1 22.6 %collective-permute-start.29 = (f32[32401]{0:T(1024)S(1)}, f32[32401]{0:T(1024)S(1)}, u32[]{:S(2)}, u32[]{:S(2)}) collective-permute-start(f32[32401]{0:T(1024)S(1)} %add.2794), channel_id=1, source_target_pairs={{0,16},{4,20},{8,24},{12,28},{16,0},{20,4},{24,8},{28,12},{32,48},... | collective-permute-start | bytes 388820 | tf_op jit(solution)/shard_map/ppermute | solution.py:54
  426.7 15.6 %collective-permute-start.30 = (f32[32401]{0:T(1024)S(1)}, f32[32401]{0:T(1024)S(1)}, u32[]{:S(2)}, u32[]{:S(2)}) collective-permute-start(f32[32401]{0:T(1024)S(1)} %add.2795), channel_id=1, source_target_pairs={{0,32},{4,36},{8,40},{12,44},{16,48},{20,52},{24,56},{28,60},{32,0... | collective-permute-start | bytes 388820 | tf_op jit(solution)/shard_map/ppermute | solution.py:54
  (58 other events, 626.5 us)

commit v3 on v2

--- a/solution.py
+++ b/solution.py
@@ -14,7 +14,7 @@
 SNAP = ("snap_0", "snap_1")
 BRICK = ("brick_0", "brick_1", "brick_2")
 SNAP_BRICK = ("snap_0", "snap_1", "brick_0", "brick_1", "brick_2")
-BUTTERFLY_ORDER = ("brick_2", "snap_1", "brick_1", "snap_0", "brick_0")
+BUTTERFLY_ORDER = ("brick_2", "snap_1", "brick_1", "snap_0")
 
 
 cutoff_sq = 36.0
@@ -43,6 +43,17 @@
 
 def by_axis(shard, axes):
     return functools.reduce(lax.psum, axes, shard)
+
+
+def group_sum(shard, spread_axis, axes):
+    count = lax.axis_size(spread_axis)
+    length = shard.shape[0]
+    padded = jnp.pad(shard, (0, (-length) % count))
+    parts = lax.all_to_all(padded.reshape(count, -1), spread_axis, 0, 0, tiled=False)
+    mine = butterfly_sum(jnp.sum(parts, axis=0), axes)
+    spread = jnp.broadcast_to(mine[None], (count,) + mine.shape)
+    whole = lax.all_to_all(spread, spread_axis, 0, 0, tiled=False)
+    return whole.reshape(-1)[:length]
 
 
 def butterfly_sum(shard, axes):
@@ -216,7 +227,7 @@
         packed = jnp.concatenate(
             [local_terms.reshape(-1), jnp.sum(raw_left * raw_left)[None]]
         )
-        packed = butterfly_sum(packed, BUTTERFLY_ORDER)
+        packed = group_sum(packed, "brick_0", BUTTERFLY_ORDER)
         totals = packed[:-1].reshape(local_terms.shape)
         squares = packed[-1]
         beta_norm = jnp.sqrt(squares / left_total + tiny)

time: 455 us -> 397 us (0.87)
  the two profiles are of different devices: /device:TPU:486 before, /device:TPU:8 now
where the time goes in v3:
time: 397 us; the launch traced here: 392 us
  local copies, waits for them, and re-layouts  104 us (26%)
  blocking collectives  84.2 us (21%)
  starting transfers between devices  67.1 us (17%)
  waiting for transfers between devices  58.4 us (15%)
  other arithmetic  34.2 us (9%)
  matrix products  32.5 us (8%)
  between operations  12 us (3%)
    all_to_all x3, blocking collectives, group_sum(): lax.all_to_all(padded.reshape(count, -1), spread_axis, 0, 0, tiled=False)  67.1 us
    unnamed x427, local copies, waits for them, and re-layouts  51.7 us
    ppermute x15, starting transfers between devices, butterfly_sum(): shard = shard + lax.ppermute(shard, axis, partners)  48.2 us
    ppermute x15, waiting for transfers between devices, butterfly_sum(): shard = shard + lax.ppermute(shard, axis, partners)  36.3 us
    all_to_all x2, waiting for transfers between devices, group_sum(): whole = lax.all_to_all(spread, spread_axis, 0, 0, tiled=False)  22.1 us
    all_to_all x1, blocking collectives, group_sum(): whole = lax.all_to_all(spread, spread_axis, 0, 0, tiled=False)  17.1 us
    dot_general x3, matrix products, back_terms(): jnp.einsum('ozi,oni->zni', other, slope * project[:, None, :], precision=...  10.8 us
    dot_general x3, matrix products, pull_force(): outward = jnp.einsum('ozi,zni->oni', other, own_grid, precision=HIGHEST)  10.1 us
  transfers between devices with their start and end apart: 21, of which 17 were waited for; matrix products, arithmetic and copies ran while one was open for 20% of the time, Pallas kernels for 0%

profile of v3, /device:TPU:8, one launch (start us, length us, event | category | flops | bytes accessed | tf_op | source)
XLA Modules:
  0.0 392.3 jit_solution(2160559848853835419)
XLA Ops:
  3.3 3.6 collective-permute-start.2
  10.9 4.6 %collective-permute-start = (f32[5,45]{1,0:T(8,128)S(1)}, f32[5,45]{1,0:T(8,128)S(1)}, u32[]{:S(2)}, u32[]{:S(2)}) collective-permute-start(f32[5,45]{1,0:T(8,128)S(1)} %get-tuple-element.371), channel_id=1, source_target_pairs={{0,1},{1,2},{2,3},{3,4},{4,5},{5,6},{6,7},{7,8},{8,9},{9,10},{10,1... | collective-permute-start | bytes 2708 | tf_op jit(solution)/shard_map/ppermute | solution.py:35
  31.4 3.3 convolution_bitcast_fusion
  46.8 3.4 fusion.2
  84.1 2.5 multiply_reduce_fusion.2
  86.6 3.1 fusion.151
  89.7 2.8 stack.1287
  102.6 2.6 copy.3835
  105.4 4.1 %multiply_reduce_fusion.13 = (f32[5,16]{1,0:T(8,128)S(1)}, f32[5,16]{1,0:T(8,128)S(1)}, f32[5,16]{1,0:T(8,128)S(1)}, f32[5,16]{1,0:T(8,128)S(1)}, f32[5,16]{1,0:T(8,128)S(1)}, /*index=5*/f32[5,16,256]{1,0,2:T(8,128)S(1)}) fusion(f32[256]{0:T(256)S(1)} %bitcast.1817, f32[256]{0:T(256)S(1)} %bitcast.1823, f32[256]{0:T(256)S(1)} %bitcast.1829, ...), kind=kOutput, calls=%fused_computation.79 | convolution fusion | flops 7615600 | bytes 610880 | tf_op jit(solution)/shard_map/ozi,oni->zni/dot_general | solution.py:157
  113.3 33.2 %all_to_all.45 = f32[16,1,2026]{2,1,0:T(1,128)S(1)} all-to-all(f32[16,1,2026]{2,1,0:T(1,128)S(1)} %all_to_all.30), channel_id=1, replica_groups=mesh['snap_0'=4,'snap_1'=2,'brick_0'=16,'brick_1'=2,'brick_2'=2] {'brick..., dimensions={0} | all-to-all | bytes 259328 | tf_op jit(solution)/shard_map/all_to_all | solution.py:52
  149.7 3.3 collective-permute-start.5
  153.0 2.2 collective-permute-done.5
  155.2 4.2 %collective-permute-start.6 = (f32[2026]{0:T(1024)S(1)}, f32[2026]{0:T(1024)S(1)}, u32[]{:S(2)}, u32[]{:S(2)}) collective-permute-start(f32[2026]{0:T(1024)S(1)} %add.2626), channel_id=1, source_target_pairs={{0,2},{2,0},{1,3},{3,1},{4,6},{6,4},{5,7},{7,5},{8,10},{10,8},{9,1... | collective-permute-start | bytes 24320 | tf_op jit(solution)/shard_map/ppermute | solution.py:65
  159.4 2.8 collective-permute-done.6
  162.2 2.3 collective-permute-start.7
  164.6 3.2 collective-permute-done.7
  167.8 4.2 %collective-permute-start.8 = (f32[2026]{0:T(1024)S(1)}, f32[2026]{0:T(1024)S(1)}, u32[]{:S(2)}, u32[]{:S(2)}) collective-permute-start(f32[2026]{0:T(1024)S(1)} %add.2628), channel_id=1, source_target_pairs={{0,256},{128,384},{256,0},{384,128},{1,257},{129,385},{257,1},{385... | collective-permute-start | bytes 24320 | tf_op jit(solution)/shard_map/ppermute | solution.py:65
  172.0 2.8 collective-permute-done.8
  175.6 4.2 %all-to-all-start.1 = ((f32[16,1,2026]{2,1,0:T(1,128)}), f32[16,1,2026]{2,1,0:T(1,128)S(1)}, u32[]{:S(2)}, u32[]{:S(2)}) async-start(f32[16,1,2026]{2,1,0:T(1,128)} %broadcast_in_dim.229), calls=%async_computation.1 | async-start | bytes 262144 | tf_op jit(solution)/shard_map/all_to_all | solution.py:55
  179.9 13.0 %all-to-all-done.1 = f32[16,1,2026]{2,1,0:T(1,128)S(1)} async-done(((f32[16,1,2026]{2,1,0:T(1,128)}), f32[16,1,2026]{2,1,0:T(1,128)S(1)}, u32[]{:S(2)}, u32[]{:S(2)}) %all-to-all-start.1) | async-done | bytes 129696 | tf_op jit(solution)/shard_map/all_to_all | solution.py:55
  202.3 3.4 fusion.1
  205.7 2.2 copy.3849
  216.2 2.4 copy.3854
  218.6 3.3 multiply_reduce_fusion.8
  226.9 17.0 %all_to_all.46 = f32[16,1,2026]{2,1,0:T(1,128)S(1)} all-to-all(f32[16,1,2026]{2,1,0:T(1,128)S(1)} %all_to_all.33), channel_id=1, replica_groups=mesh['snap_0'=4,'snap_1'=2,'brick_0'=16,'brick_1'=2,'brick_2'=2] {'brick..., dimensions={0} | all-to-all | bytes 259328 | tf_op jit(solution)/shard_map/all_to_all | solution.py:52
  247.0 3.3 collective-permute-start.10
  250.3 2.2 collective-permute-done.10
  252.5 4.3 %collective-permute-start.11 = (f32[2026]{0:T(1024)S(1)}, f32[2026]{0:T(1024)S(1)}, u32[]{:S(2)}, u32[]{:S(2)}) collective-permute-start(f32[2026]{0:T(1024)S(1)} %add.2680), channel_id=1, source_target_pairs={{0,2},{2,0},{1,3},{3,1},{4,6},{6,4},{5,7},{7,5},{8,10},{10,8},{9,1... | collective-permute-start | bytes 24320 | tf_op jit(solution)/shard_map/ppermute | solution.py:65
  256.8 2.7 collective-permute-done.11
  259.6 2.3 collective-permute-start.12
  261.9 3.2 collective-permute-done.12
  265.1 4.2 %collective-permute-start.13 = (f32[2026]{0:T(1024)S(1)}, f32[2026]{0:T(1024)S(1)}, u32[]{:S(2)}, u32[]{:S(2)}) collective-permute-start(f32[2026]{0:T(1024)S(1)} %add.2682), channel_id=1, source_target_pairs={{0,256},{128,384},{256,0},{384,128},{1,257},{129,385},{257,1},{385... | collective-permute-start | bytes 24320 | tf_op jit(solution)/shard_map/ppermute | solution.py:65
  269.3 2.8 collective-permute-done.13
  272.2 17.1 %all_to_all.47 = f32[16,1,2026]{2,1,0:T(1,128)S(1)} all-to-all(f32[16,1,2026]{2,1,0:T(1,128)S(1)} %broadcast_in_dim.238), channel_id=1, replica_groups=mesh['snap_0'=4,'snap_1'=2,'brick_0'=16,'brick_1'=2,'brick_2'=2] {'brick..., dimensions={0} | all-to-all | bytes 259328 | tf_op jit(solution)/shard_map/all_to_all | solution.py:55
  298.8 3.4 fusion
  302.2 2.2 copy.3867
  313.3 3.3 multiply_reduce_fusion.3
  321.6 17.0 %all_to_all.48 = f32[16,1,2026]{2,1,0:T(1,128)S(1)} all-to-all(f32[16,1,2026]{2,1,0:T(1,128)S(1)} %all_to_all.36), channel_id=1, replica_groups=mesh['snap_0'=4,'snap_1'=2,'brick_0'=16,'brick_1'=2,'brick_2'=2] {'brick..., dimensions={0} | all-to-all | bytes 259328 | tf_op jit(solution)/shard_map/all_to_all | solution.py:52
  341.7 3.3 collective-permute-start.15
  345.1 2.2 collective-permute-done.15
  347.3 4.4 %collective-permute-start.16 = (f32[2026]{0:T(1024)S(1)}, f32[2026]{0:T(1024)S(1)}, u32[]{:S(2)}, u32[]{:S(2)}) collective-permute-start(f32[2026]{0:T(1024)S(1)} %add.2751), channel_id=1, source_target_pairs={{0,2},{2,0},{1,3},{3,1},{4,6},{6,4},{5,7},{7,5},{8,10},{10,8},{9,1... | collective-permute-start | bytes 24320 | tf_op jit(solution)/shard_map/ppermute | solution.py:65
  351.7 2.6 collective-permute-done.16
  354.3 2.3 collective-permute-start.17
  356.7 3.2 collective-permute-done.17
  359.9 4.2 %collective-permute-start.18 = (f32[2026]{0:T(1024)S(1)}, f32[2026]{0:T(1024)S(1)}, u32[]{:S(2)}, u32[]{:S(2)}) collective-permute-start(f32[2026]{0:T(1024)S(1)} %add.2753), channel_id=1, source_target_pairs={{0,256},{128,384},{256,0},{384,128},{1,257},{129,385},{257,1},{385... | collective-permute-start | bytes 24320 | tf_op jit(solution)/shard_map/ppermute | solution.py:65
  364.0 2.8 collective-permute-done.18
  367.6 3.9 %all-to-all-start.5 = ((f32[16,1,2026]{2,1,0:T(1,128)}), f32[16,1,2026]{2,1,0:T(1,128)S(1)}, u32[]{:S(2)}, u32[]{:S(2)}) async-start(f32[16,1,2026]{2,1,0:T(1,128)} %broadcast_in_dim.247), calls=%async_computation.5 | async-start | bytes 262144 | tf_op jit(solution)/shard_map/all_to_all | solution.py:55
  375.6 9.1 %all-to-all-done.5 = f32[16,1,2026]{2,1,0:T(1,128)S(1)} async-done(((f32[16,1,2026]{2,1,0:T(1,128)}), f32[16,1,2026]{2,1,0:T(1,128)S(1)}, u32[]{:S(2)}, u32[]{:S(2)}) %all-to-all-start.5) | async-done | bytes 129696 | tf_op jit(solution)/shard_map/all_to_all | solution.py:55
  (723 shorter events, 140.3 us)
Async XLA Ops:
  0.6 28.8 %copy-start.63 = (pred[30]{0:T(512)(128)(4,1)S(1)}, pred[30]{0:T(512)(128)(4,1)}, u32[]{:S(2)}) copy-start(pred[30]{0:T(512)(128)(4,1)} %constant.226.clone) | copy-start | bytes 94
  0.6 28.8 %copy-start.66 = (s32[30]{0:T(128)S(1)}, s32[30]{0:T(128)}, u32[]{:S(2)}) copy-start(s32[30]{0:T(128)} %constant.227.clone) | copy-start | bytes 364
  2.0 91.3 %collective-permute-start.3 = (f32[3,15]{1,0:T(4,128)}, f32[3,15]{1,0:T(4,128)}, u32[]{:S(2)}, u32[]{:S(2)}) collective-permute-start(f32[3,15]{1,0:T(4,128)} %get-tuple-element.382), channel_id=1, source_target_pairs={{1,0},{2,1},{3,2},{4,3},{5,4},{6,5},{7,6},{8,7},{9,8},{10,9},{11,1... | collective-permute-start | bytes 548 | tf_op jit(solution)/shard_map/ppermute | solution.py:37
  3.3 90.0 %collective-permute-start.2 = (f32[3,15]{1,0:T(4,128)}, f32[3,15]{1,0:T(4,128)}, u32[]{:S(2)}, u32[]{:S(2)}) collective-permute-start(f32[3,15]{1,0:T(4,128)} %get-tuple-element.381), channel_id=1, source_target_pairs={{0,1},{1,2},{2,3},{3,4},{4,5},{5,6},{6,7},{7,8},{8,9},{9,10},{10,1... | collective-permute-start | bytes 548 | tf_op jit(solution)/shard_map/ppermute | solution.py:35
  9.6 14.2 %collective-permute-start.1 = (f32[5,45]{1,0:T(8,128)S(1)}, f32[5,45]{1,0:T(8,128)S(1)}, u32[]{:S(2)}, u32[]{:S(2)}) collective-permute-start(f32[5,45]{1,0:T(8,128)S(1)} %get-tuple-element.372), channel_id=1, source_target_pairs={{1,0},{2,1},{3,2},{4,3},{5,4},{6,5},{7,6},{8,7},{9,8},{10,9},{11,1... | collective-permute-start | bytes 2708 | tf_op jit(solution)/shard_map/ppermute | solution.py:37
  10.9 12.9 %collective-permute-start = (f32[5,45]{1,0:T(8,128)S(1)}, f32[5,45]{1,0:T(8,128)S(1)}, u32[]{:S(2)}, u32[]{:S(2)}) collective-permute-start(f32[5,45]{1,0:T(8,128)S(1)} %get-tuple-element.371), channel_id=1, source_target_pairs={{0,1},{1,2},{2,3},{3,4},{4,5},{5,6},{6,7},{7,8},{8,9},{9,10},{10,1... | collective-permute-start | bytes 2708 | tf_op jit(solution)/shard_map/ppermute | solution.py:35
  36.4 160.3 %copy-start.38 = (f32[316]{0:T(512)}, f32[316]{0:T(512)S(1)}, u32[]{:S(2)}) copy-start(f32[316]{0:T(512)S(1)} %get-tuple-element.196) | copy-start | bytes 3796
  41.8 67.9 %copy-start.52 = (f32[1,256]{1,0:T(1,128)}, f32[1,256]{1,0:T(1,128)S(1)}, u32[]{:S(2)}) copy-start(f32[1,256]{1,0:T(1,128)S(1)} %get-tuple-element.366) | copy-start | bytes 3076
  41.8 68.2 %copy-start.49 = (f32[1,256]{1,0:T(1,128)}, f32[1,256]{1,0:T(1,128)S(1)}, u32[]{:S(2)}) copy-start(f32[1,256]{1,0:T(1,128)S(1)} %get-tuple-element.370) | copy-start | bytes 3076
  41.9 68.5 %copy-start.46 = (f32[1,256]{1,0:T(1,128)}, f32[1,256]{1,0:T(1,128)S(1)}, u32[]{:S(2)}) copy-start(f32[1,256]{1,0:T(1,128)S(1)} %get-tuple-element.369) | copy-start | bytes 3076
  41.9 68.8 %copy-start.43 = (f32[1,256]{1,0:T(1,128)}, f32[1,256]{1,0:T(1,128)S(1)}, u32[]{:S(2)}) copy-start(f32[1,256]{1,0:T(1,128)S(1)} %get-tuple-element.368) | copy-start | bytes 3076
  41.9 69.1 %copy-start.40 = (f32[1,256]{1,0:T(1,128)}, f32[1,256]{1,0:T(1,128)S(1)}, u32[]{:S(2)}) copy-start(f32[1,256]{1,0:T(1,128)S(1)} %get-tuple-element.367) | copy-start | bytes 3076
  44.0 49.1 %copy-start.9 = (f32[30,5,286]{2,1,0:T(8,128)}, f32[30,5,286]{2,1,0:T(8,128)S(1)}, u32[]{:S(2)}) copy-start(f32[30,5,286]{2,1,0:T(8,128)S(1)} %constant_dynamic-update-slice_fusion.76) | copy-start | bytes 514804
  52.4 21.8 %copy-start.24 = (f32[80,286]{1,0:T(8,128)S(1)}, f32[80,286]{1,0:T(8,128)}, u32[]{:S(2)}) copy-start(f32[80,286]{1,0:T(8,128)} %get-tuple-element.326) | copy-start | bytes 274564
  52.4 22.4 %copy-start.23 = (f32[80,286]{1,0:T(8,128)S(1)}, f32[80,286]{1,0:T(8,128)}, u32[]{:S(2)}) copy-start(f32[80,286]{1,0:T(8,128)} %get-tuple-element.325) | copy-start | bytes 274564
  52.4 23.1 %copy-start.22 = (f32[80,286]{1,0:T(8,128)S(1)}, f32[80,286]{1,0:T(8,128)}, u32[]{:S(2)}) copy-start(f32[80,286]{1,0:T(8,128)} %get-tuple-element.324) | copy-start | bytes 274564
  52.4 23.8 %copy-start.21 = (f32[80,286]{1,0:T(8,128)S(1)}, f32[80,286]{1,0:T(8,128)}, u32[]{:S(2)}) copy-start(f32[80,286]{1,0:T(8,128)} %get-tuple-element.323) | copy-start | bytes 274564
  52.4 24.4 %copy-start.20 = (f32[80,286]{1,0:T(8,128)S(1)}, f32[80,286]{1,0:T(8,128)}, u32[]{:S(2)}) copy-start(f32[80,286]{1,0:T(8,128)} %get-tuple-element.322) | copy-start | bytes 274564
  52.4 25.1 %copy-start.19 = (f32[80,286]{1,0:T(8,128)S(1)}, f32[80,286]{1,0:T(8,128)}, u32[]{:S(2)}) copy-start(f32[80,286]{1,0:T(8,128)} %get-tuple-element.321) | copy-start | bytes 274564
  52.4 25.7 %copy-start.18 = (f32[80,286]{1,0:T(8,128)S(1)}, f32[80,286]{1,0:T(8,128)}, u32[]{:S(2)}) copy-start(f32[80,286]{1,0:T(8,128)} %get-tuple-element.320) | copy-start | bytes 274564
  52.4 26.4 %copy-start.17 = (f32[80,286]{1,0:T(8,128)S(1)}, f32[80,286]{1,0:T(8,128)}, u32[]{:S(2)}) copy-start(f32[80,286]{1,0:T(8,128)} %get-tuple-element.319) | copy-start | bytes 274564
  52.4 27.0 %copy-start.16 = (f32[80,286]{1,0:T(8,128)S(1)}, f32[80,286]{1,0:T(8,128)}, u32[]{:S(2)}) copy-start(f32[80,286]{1,0:T(8,128)} %get-tuple-element.318) | copy-start | bytes 274564
  52.4 27.7 %copy-start.15 = (f32[80,286]{1,0:T(8,128)S(1)}, f32[80,286]{1,0:T(8,128)}, u32[]{:S(2)}) copy-start(f32[80,286]{1,0:T(8,128)} %get-tuple-element.317) | copy-start | bytes 274564
  52.4 28.3 %copy-start.14 = (f32[80,286]{1,0:T(8,128)S(1)}, f32[80,286]{1,0:T(8,128)}, u32[]{:S(2)}) copy-start(f32[80,286]{1,0:T(8,128)} %get-tuple-element.316) | copy-start | bytes 274564
  52.5 29.0 %copy-start.13 = (f32[80,286]{1,0:T(8,128)S(1)}, f32[80,286]{1,0:T(8,128)}, u32[]{:S(2)}) copy-start(f32[80,286]{1,0:T(8,128)} %get-tuple-element.315) | copy-start | bytes 274564
  52.5 29.6 %copy-start.12 = (f32[80,286]{1,0:T(8,128)S(1)}, f32[80,286]{1,0:T(8,128)}, u32[]{:S(2)}) copy-start(f32[80,286]{1,0:T(8,128)} %get-tuple-element.314) | copy-start | bytes 274564
  52.5 30.3 %copy-start.11 = (f32[80,286]{1,0:T(8,128)S(1)}, f32[80,286]{1,0:T(8,128)}, u32[]{:S(2)}) copy-start(f32[80,286]{1,0:T(8,128)} %get-tuple-element.313) | copy-start | bytes 274564
  146.6 3.1 collective-permute-start.4
  149.7 5.5 %collective-permute-start.5 = (f32[2026]{0:T(1024)S(1)}, f32[2026]{0:T(1024)S(1)}, u32[]{:S(2)}, u32[]{:S(2)}) collective-permute-start(f32[2026]{0:T(1024)S(1)} %add.2625), channel_id=1, source_target_pairs={{0,64},{64,0},{1,65},{65,1},{2,66},{66,2},{3,67},{67,3},{4,68},{68... | collective-permute-start | bytes 24320 | tf_op jit(solution)/shard_map/ppermute | solution.py:65
  155.2 7.0 %collective-permute-start.6 = (f32[2026]{0:T(1024)S(1)}, f32[2026]{0:T(1024)S(1)}, u32[]{:S(2)}, u32[]{:S(2)}) collective-permute-start(f32[2026]{0:T(1024)S(1)} %add.2626), channel_id=1, source_target_pairs={{0,2},{2,0},{1,3},{3,1},{4,6},{6,4},{5,7},{7,5},{8,10},{10,8},{9,1... | collective-permute-start | bytes 24320 | tf_op jit(solution)/shard_map/ppermute | solution.py:65
  162.2 5.5 %collective-permute-start.7 = (f32[2026]{0:T(1024)S(1)}, f32[2026]{0:T(1024)S(1)}, u32[]{:S(2)}, u32[]{:S(2)}) collective-permute-start(f32[2026]{0:T(1024)S(1)} %add.2627), channel_id=1, source_target_pairs={{0,128},{128,0},{256,384},{384,256},{1,129},{129,1},{257,385},{385... | collective-permute-start | bytes 24320 | tf_op jit(solution)/shard_map/ppermute | solution.py:65
  167.8 7.0 %collective-permute-start.8 = (f32[2026]{0:T(1024)S(1)}, f32[2026]{0:T(1024)S(1)}, u32[]{:S(2)}, u32[]{:S(2)}) collective-permute-start(f32[2026]{0:T(1024)S(1)} %add.2628), channel_id=1, source_target_pairs={{0,256},{128,384},{256,0},{384,128},{1,257},{129,385},{257,1},{385... | collective-permute-start | bytes 24320 | tf_op jit(solution)/shard_map/ppermute | solution.py:65
  175.6 17.3 %all-to-all-start.1 = ((f32[16,1,2026]{2,1,0:T(1,128)}), f32[16,1,2026]{2,1,0:T(1,128)S(1)}, u32[]{:S(2)}, u32[]{:S(2)}) async-start(f32[16,1,2026]{2,1,0:T(1,128)} %broadcast_in_dim.229), calls=%async_computation.1 | async-start | bytes 262144 | tf_op jit(solution)/shard_map/all_to_all | solution.py:55
  223.4 69.7 %copy-start.39 = (f32[316]{0:T(512)S(1)}, f32[316]{0:T(512)}, u32[]{:S(2)}) copy-start(f32[316]{0:T(512)} %copy-done.38) | copy-start | bytes 3796
  243.9 3.1 collective-permute-start.9
  247.0 5.5 %collective-permute-start.10 = (f32[2026]{0:T(1024)S(1)}, f32[2026]{0:T(1024)S(1)}, u32[]{:S(2)}, u32[]{:S(2)}) collective-permute-start(f32[2026]{0:T(1024)S(1)} %add.2679), channel_id=1, source_target_pairs={{0,64},{64,0},{1,65},{65,1},{2,66},{66,2},{3,67},{67,3},{4,68},{68... | collective-permute-start | bytes 24320 | tf_op jit(solution)/shard_map/ppermute | solution.py:65
  252.5 7.0 %collective-permute-start.11 = (f32[2026]{0:T(1024)S(1)}, f32[2026]{0:T(1024)S(1)}, u32[]{:S(2)}, u32[]{:S(2)}) collective-permute-start(f32[2026]{0:T(1024)S(1)} %add.2680), channel_id=1, source_target_pairs={{0,2},{2,0},{1,3},{3,1},{4,6},{6,4},{5,7},{7,5},{8,10},{10,8},{9,1... | collective-permute-start | bytes 24320 | tf_op jit(solution)/shard_map/ppermute | solution.py:65
  259.6 5.5 %collective-permute-start.12 = (f32[2026]{0:T(1024)S(1)}, f32[2026]{0:T(1024)S(1)}, u32[]{:S(2)}, u32[]{:S(2)}) collective-permute-start(f32[2026]{0:T(1024)S(1)} %add.2681), channel_id=1, source_target_pairs={{0,128},{128,0},{256,384},{384,256},{1,129},{129,1},{257,385},{385... | collective-permute-start | bytes 24320 | tf_op jit(solution)/shard_map/ppermute | solution.py:65
  265.1 7.0 %collective-permute-start.13 = (f32[2026]{0:T(1024)S(1)}, f32[2026]{0:T(1024)S(1)}, u32[]{:S(2)}, u32[]{:S(2)}) collective-permute-start(f32[2026]{0:T(1024)S(1)} %add.2682), channel_id=1, source_target_pairs={{0,256},{128,384},{256,0},{384,128},{1,257},{129,385},{257,1},{385... | collective-permute-start | bytes 24320 | tf_op jit(solution)/shard_map/ppermute | solution.py:65
  316.6 55.0 %copy-start.28 = (f32[5,81,80]{1,2,0:T(8,128)S(1)}, f32[5,81,80]{1,2,0:T(8,128)}, u32[]{:S(2)}) copy-start(f32[5,81,80]{1,2,0:T(8,128)} %param.41) | copy-start | bytes 388804
  316.6 56.5 %copy-start.29 = (f32[5,81,80]{1,2,0:T(8,128)S(1)}, f32[5,81,80]{1,2,0:T(8,128)}, u32[]{:S(2)}) copy-start(f32[5,81,80]{1,2,0:T(8,128)} %param.42) | copy-start | bytes 388804
  316.6 70.8 %copy-start.4 = (f32[5,81,80]{2,1,0:T(8,128)S(1)}, f32[5,81,80]{2,1,0:T(8,128)}, u32[]{:S(2)}) copy-start(f32[5,81,80]{2,1,0:T(8,128)} %copy-done.3) | copy-start | bytes 388804
  338.7 3.1 collective-permute-start.14
  341.7 5.5 %collective-permute-start.15 = (f32[2026]{0:T(1024)S(1)}, f32[2026]{0:T(1024)S(1)}, u32[]{:S(2)}, u32[]{:S(2)}) collective-permute-start(f32[2026]{0:T(1024)S(1)} %add.2750), channel_id=1, source_target_pairs={{0,64},{64,0},{1,65},{65,1},{2,66},{66,2},{3,67},{67,3},{4,68},{68... | collective-permute-start | bytes 24320 | tf_op jit(solution)/shard_map/ppermute | solution.py:65
  347.3 7.0 %collective-permute-start.16 = (f32[2026]{0:T(1024)S(1)}, f32[2026]{0:T(1024)S(1)}, u32[]{:S(2)}, u32[]{:S(2)}) collective-permute-start(f32[2026]{0:T(1024)S(1)} %add.2751), channel_id=1, source_target_pairs={{0,2},{2,0},{1,3},{3,1},{4,6},{6,4},{5,7},{7,5},{8,10},{10,8},{9,1... | collective-permute-start | bytes 24320 | tf_op jit(solution)/shard_map/ppermute | solution.py:65
  354.3 5.5 %collective-permute-start.17 = (f32[2026]{0:T(1024)S(1)}, f32[2026]{0:T(1024)S(1)}, u32[]{:S(2)}, u32[]{:S(2)}) collective-permute-start(f32[2026]{0:T(1024)S(1)} %add.2752), channel_id=1, source_target_pairs={{0,128},{128,0},{256,384},{384,256},{1,129},{129,1},{257,385},{385... | collective-permute-start | bytes 24320 | tf_op jit(solution)/shard_map/ppermute | solution.py:65
  359.9 7.0 %collective-permute-start.18 = (f32[2026]{0:T(1024)S(1)}, f32[2026]{0:T(1024)S(1)}, u32[]{:S(2)}, u32[]{:S(2)}) collective-permute-start(f32[2026]{0:T(1024)S(1)} %add.2753), channel_id=1, source_target_pairs={{0,256},{128,384},{256,0},{384,128},{1,257},{129,385},{257,1},{385... | collective-permute-start | bytes 24320 | tf_op jit(solution)/shard_map/ppermute | solution.py:65
  367.6 17.1 %all-to-all-start.5 = ((f32[16,1,2026]{2,1,0:T(1,128)}), f32[16,1,2026]{2,1,0:T(1,128)S(1)}, u32[]{:S(2)}, u32[]{:S(2)}) async-start(f32[16,1,2026]{2,1,0:T(1,128)} %broadcast_in_dim.247), calls=%async_computation.5 | async-start | bytes 262144 | tf_op jit(solution)/shard_map/all_to_all | solution.py:55
  (48 other events, 377.8 us)

commit v4 on v3

--- a/solution.py
+++ b/solution.py
@@ -121,20 +121,18 @@
 
 def density(padded, atom_count):
     delta, radial, slope, other, linked = pair_tables(padded, atom_count)
-    grid = jnp.einsum("ozi,oni->zni", other, radial * linked[:, None, :], precision=HIGHEST)
+    grid = jnp.sum(other[:, :, None, :] * (radial * linked[:, None, :])[:, None], axis=0)
     return grid.reshape(SPECIES * RADIAL, atom_count)
 
 
 def slope_field(field_density, own_kinds, coefs):
     channels = field_density.shape[0]
-    result = jnp.zeros_like(field_density)
-    for kind in range(SPECIES):
-        quad = coefs[kind, :channels, :]
-        part = coefs[kind, channels][:, None] + jnp.dot(
-            quad + quad.T, field_density, precision=HIGHEST
-        ) / math.sqrt(channels)
-        result = result + own_kinds[kind][None, :] * part
-    return result
+    quad = coefs[:, :channels, :]
+    both = quad + jnp.transpose(quad, (0, 2, 1))
+    part = coefs[:, channels][:, :, None] + jnp.einsum(
+        "zab,bn->zan", both, field_density, precision=HIGHEST
+    ) / math.sqrt(channels)
+    return jnp.sum(own_kinds[:, None, :] * part, axis=0)
 
 
 def pull_force(slopes, slopes_pad, padded, own_kinds, atom_count):
@@ -143,8 +141,8 @@
     there_slopes = shifted_stack(slopes_pad, atom_count).reshape(
         2 * WINDOW, SPECIES, RADIAL, atom_count
     )
-    outward = jnp.einsum("ozi,zni->oni", other, own_grid, precision=HIGHEST)
-    inward = jnp.einsum("zi,ozni->oni", own_kinds, there_slopes, precision=HIGHEST)
+    outward = jnp.sum(other[:, :, None, :] * own_grid[None], axis=1)
+    inward = jnp.sum(own_kinds[None, :, None, :] * there_slopes, axis=1)
     strength = jnp.sum((outward + inward) * slope, axis=1) * linked * (2.0 / cutoff_sq)
     return jnp.sum(strength[:, None, :] * delta, axis=0)
 
@@ -154,18 +152,14 @@
     there_values = shifted_stack(value_pad, atom_count)
     project = jnp.sum(delta * (values[None] - there_values), axis=1) * linked * (2.0 / cutoff_sq)
     channels = field_density.shape[0]
-    weights = jnp.einsum(
-        "ozi,oni->zni", other, slope * project[:, None, :], precision=HIGHEST
+    weights = jnp.sum(
+        other[:, :, None, :] * (slope * project[:, None, :])[:, None], axis=0
     ).reshape(channels, atom_count)
-    rows = []
-    for kind in range(SPECIES):
-        masked = field_density * own_kinds[kind][None, :]
-        cross = jnp.dot(masked, weights.T, precision=HIGHEST)
-        linear = jnp.sum(weights * own_kinds[kind][None, :], axis=1)
-        rows.append(
-            jnp.concatenate([(cross + cross.T) / math.sqrt(channels), linear[None, :]], axis=0)
-        )
-    return jnp.stack(rows)
+    masked = own_kinds[:, None, :] * field_density[None]
+    cross = jnp.einsum("zbi,ai->zba", masked, weights, precision=HIGHEST)
+    linear = jnp.sum(own_kinds[:, None, :] * weights[None], axis=2)
+    both = (cross + jnp.transpose(cross, (0, 2, 1))) / math.sqrt(channels)
+    return jnp.concatenate([both, linear[:, None, :]], axis=1)
 
 
 def rotation(rho_bar, phi_bar, beta_norm, alpha_norm):

time: 397 us -> 326 us (0.82)
  the two profiles are of different devices: /device:TPU:8 before, /device:TPU:10 now
where the time goes in v4:
time: 326 us; the launch traced here: 325 us
  blocking collectives  87.4 us (27%)
  waiting for transfers between devices  68.7 us (21%)
  local copies, waits for them, and re-layouts  68.3 us (21%)
  starting transfers between devices  56.2 us (17%)
  other arithmetic  30.1 us (9%)
  between operations  10.5 us (3%)
  matrix products  3.51 us (1%)
    all_to_all x3, blocking collectives, group_sum(): lax.all_to_all(padded.reshape(count, -1), spread_axis, 0, 0, tiled=False)  70.5 us
    ppermute x15, waiting for transfers between devices, butterfly_sum(): shard = shard + lax.ppermute(shard, axis, partners)  46.1 us
    unnamed x312, local copies, waits for them, and re-layouts  44.6 us
    ppermute x15, starting transfers between devices, butterfly_sum(): shard = shard + lax.ppermute(shard, axis, partners)  38.4 us
    all_to_all x2, waiting for transfers between devices, group_sum(): whole = lax.all_to_all(spread, spread_axis, 0, 0, tiled=False)  22.5 us
    all_to_all x1, blocking collectives, group_sum(): whole = lax.all_to_all(spread, spread_axis, 0, 0, tiled=False)  16.9 us
    all_to_all x2, starting transfers between devices, group_sum(): whole = lax.all_to_all(spread, spread_axis, 0, 0, tiled=False)  7.99 us
    ppermute x2, starting transfers between devices, with_halo(): lax.ppermute(tail, axis, [(i, (i + 1) % count) for i in range(ends)])  7.25 us
  transfers between devices with their start and end apart: 21, of which 17 were waited for; matrix products, arithmetic and copies ran while one was open for 18% of the time, Pallas kernels for 0%

profile of v4, /device:TPU:10, one launch (start us, length us, event | category | flops | bytes accessed | tf_op | source)
XLA Modules:
  0.0 324.6 jit_solution(155565351321272263)
XLA Ops:
  3.3 1.7 collective-permute-start
  7.7 5.5 %collective-permute-start.2 = (f32[3,15]{1,0:T(4,128)}, f32[3,15]{1,0:T(4,128)}, u32[]{:S(2)}, u32[]{:S(2)}) collective-permute-start(f32[3,15]{1,0:T(4,128)} %get-tuple-element.212), channel_id=1, source_target_pairs={{0,1},{1,2},{2,3},{3,4},{4,5},{5,6},{6,7},{7,8},{8,9},{9,10},{10,1... | collective-permute-start | bytes 548 | tf_op jit(solution)/shard_map/ppermute | solution.py:35
  33.7 1.6 constant_dynamic-update-slice_fusion.88
  35.2 1.6 constant_dynamic-update-slice_fusion.87
  36.8 1.6 constant_dynamic-update-slice_fusion.86
  38.3 1.6 constant_dynamic-update-slice_fusion.85
  39.9 1.6 constant_dynamic-update-slice_fusion.84
  41.4 1.6 constant_dynamic-update-slice_fusion.83
  43.0 1.6 constant_dynamic-update-slice_fusion.82
  44.6 1.6 constant_dynamic-update-slice_fusion.81
  60.8 3.6 %fusion.94 = (f32[30,1,286]{2,1,0:T(1,128)S(1)}, f32[30,1,286]{2,1,0:T(1,128)S(1)}, f32[30,1,286]{2,1,0:T(1,128)S(1)}, f32[30,1,286]{2,1,0:T(1,128)S(1)}, f32[30...) fusion(f32[30,286]{1,0:T(8,128)S(1)} %get-tuple-element.170, ...), kind=kLoop, calls=%fused_computation.497 | loop fusion | flops 1244100 | bytes 617760 | tf_op jit(solution)/shard_map/mul | solution.py:92
  64.6 2.8 multiply_reduce_fusion.4
  67.4 3.0 stack.1233
  83.7 36.6 %all_to_all.45 = f32[16,1,2026]{2,1,0:T(1,128)S(1)} all-to-all(f32[16,1,2026]{2,1,0:T(1,128)S(1)} %all_to_all.30), channel_id=1, replica_groups=mesh['snap_0'=4,'snap_1'=2,'brick_0'=16,'brick_1'=2,'brick_2'=2] {'brick..., dimensions={0} | all-to-all | bytes 259328 | tf_op jit(solution)/shard_map/all_to_all | solution.py:52
  120.4 1.9 collective-permute-start.4
  123.4 2.4 collective-permute-start.5
  125.9 3.1 collective-permute-done.5
  129.0 1.9 collective-permute-start.6
  130.9 5.1 %collective-permute-done.6 = f32[2026]{0:T(1024)S(1)} collective-permute-done((f32[2026]{0:T(1024)S(1)}, f32[2026]{0:T(1024)S(1)}, u32[]{:S(2)}, u32[]{:S(2)}) %collective-permute-start.6) | collective-permute-done | bytes 8136 | tf_op jit(solution)/shard_map/ppermute | solution.py:65
  136.0 2.3 collective-permute-start.7
  138.4 3.2 collective-permute-done.7
  141.5 4.2 %collective-permute-start.8 = (f32[2026]{0:T(1024)S(1)}, f32[2026]{0:T(1024)S(1)}, u32[]{:S(2)}, u32[]{:S(2)}) collective-permute-start(f32[2026]{0:T(1024)S(1)} %add.2776), channel_id=1, source_target_pairs={{0,256},{128,384},{256,0},{384,128},{1,257},{129,385},{257,1},{385... | collective-permute-start | bytes 24320 | tf_op jit(solution)/shard_map/ppermute | solution.py:65
  145.7 2.8 collective-permute-done.8
  149.3 4.0 %all-to-all-start.1 = ((f32[16,1,2026]{2,1,0:T(1,128)}), f32[16,1,2026]{2,1,0:T(1,128)S(1)}, u32[]{:S(2)}, u32[]{:S(2)}) async-start(f32[16,1,2026]{2,1,0:T(1,128)} %broadcast_in_dim.108), calls=%async_computation.1 | async-start | bytes 262144 | tf_op jit(solution)/shard_map/all_to_all | solution.py:55
  153.5 13.0 %all-to-all-done.1 = f32[16,1,2026]{2,1,0:T(1,128)S(1)} async-done(((f32[16,1,2026]{2,1,0:T(1,128)}), f32[16,1,2026]{2,1,0:T(1,128)S(1)}, u32[]{:S(2)}, u32[]{:S(2)}) %all-to-all-start.1) | async-done | bytes 129696 | tf_op jit(solution)/shard_map/all_to_all | solution.py:55
  179.3 16.9 %all_to_all.46 = f32[16,1,2026]{2,1,0:T(1,128)S(1)} all-to-all(f32[16,1,2026]{2,1,0:T(1,128)S(1)} %all_to_all.33), channel_id=1, replica_groups=mesh['snap_0'=4,'snap_1'=2,'brick_0'=16,'brick_1'=2,'brick_2'=2] {'brick..., dimensions={0} | all-to-all | bytes 259328 | tf_op jit(solution)/shard_map/all_to_all | solution.py:52
  196.3 1.9 collective-permute-start.9
  199.4 2.4 collective-permute-start.10
  201.8 3.1 collective-permute-done.10
  204.9 1.9 collective-permute-start.11
  206.9 5.1 %collective-permute-done.11 = f32[2026]{0:T(1024)S(1)} collective-permute-done((f32[2026]{0:T(1024)S(1)}, f32[2026]{0:T(1024)S(1)}, u32[]{:S(2)}, u32[]{:S(2)}) %collective-permute-start.11) | collective-permute-done | bytes 8136 | tf_op jit(solution)/shard_map/ppermute | solution.py:65
  212.0 2.3 collective-permute-start.12
  214.3 3.2 collective-permute-done.12
  217.5 4.2 %collective-permute-start.13 = (f32[2026]{0:T(1024)S(1)}, f32[2026]{0:T(1024)S(1)}, u32[]{:S(2)}, u32[]{:S(2)}) collective-permute-start(f32[2026]{0:T(1024)S(1)} %add.2806), channel_id=1, source_target_pairs={{0,256},{128,384},{256,0},{384,128},{1,257},{129,385},{257,1},{385... | collective-permute-start | bytes 24320 | tf_op jit(solution)/shard_map/ppermute | solution.py:65
  221.7 2.8 collective-permute-done.13
  224.6 16.9 %all_to_all.47 = f32[16,1,2026]{2,1,0:T(1,128)S(1)} all-to-all(f32[16,1,2026]{2,1,0:T(1,128)S(1)} %broadcast_in_dim.113), channel_id=1, replica_groups=mesh['snap_0'=4,'snap_1'=2,'brick_0'=16,'brick_1'=2,'brick_2'=2] {'brick..., dimensions={0} | all-to-all | bytes 259328 | tf_op jit(solution)/shard_map/all_to_all | solution.py:55
  254.2 16.9 %all_to_all.48 = f32[16,1,2026]{2,1,0:T(1,128)S(1)} all-to-all(f32[16,1,2026]{2,1,0:T(1,128)S(1)} %all_to_all.36), channel_id=1, replica_groups=mesh['snap_0'=4,'snap_1'=2,'brick_0'=16,'brick_1'=2,'brick_2'=2] {'brick..., dimensions={0} | all-to-all | bytes 259328 | tf_op jit(solution)/shard_map/all_to_all | solution.py:52
  271.2 1.9 collective-permute-start.14
  274.3 2.4 collective-permute-start.15
  276.7 3.1 collective-permute-done.15
  279.8 1.9 collective-permute-start.16
  281.8 5.1 %collective-permute-done.16 = f32[2026]{0:T(1024)S(1)} collective-permute-done((f32[2026]{0:T(1024)S(1)}, f32[2026]{0:T(1024)S(1)}, u32[]{:S(2)}, u32[]{:S(2)}) %collective-permute-start.16) | collective-permute-done | bytes 8136 | tf_op jit(solution)/shard_map/ppermute | solution.py:65
  286.9 2.3 collective-permute-start.17
  289.2 3.2 collective-permute-done.17
  292.4 4.2 %collective-permute-start.18 = (f32[2026]{0:T(1024)S(1)}, f32[2026]{0:T(1024)S(1)}, u32[]{:S(2)}, u32[]{:S(2)}) collective-permute-start(f32[2026]{0:T(1024)S(1)} %add.2853), channel_id=1, source_target_pairs={{0,256},{128,384},{256,0},{384,128},{1,257},{129,385},{257,1},{385... | collective-permute-start | bytes 24320 | tf_op jit(solution)/shard_map/ppermute | solution.py:65
  296.6 2.8 collective-permute-done.18
  300.2 3.9 %all-to-all-start.5 = ((f32[16,1,2026]{2,1,0:T(1,128)}), f32[16,1,2026]{2,1,0:T(1,128)S(1)}, u32[]{:S(2)}, u32[]{:S(2)}) async-start(f32[16,1,2026]{2,1,0:T(1,128)} %broadcast_in_dim.118), calls=%async_computation.5 | async-start | bytes 262144 | tf_op jit(solution)/shard_map/all_to_all | solution.py:55
  307.8 9.5 %all-to-all-done.5 = f32[16,1,2026]{2,1,0:T(1,128)S(1)} async-done(((f32[16,1,2026]{2,1,0:T(1,128)}), f32[16,1,2026]{2,1,0:T(1,128)S(1)}, u32[]{:S(2)}, u32[]{:S(2)}) %all-to-all-start.5) | async-done | bytes 129696 | tf_op jit(solution)/shard_map/all_to_all | solution.py:55
  (512 shorter events, 86.0 us)
Async XLA Ops:
  2.6 19.6 %copy-start.21 = (f32[1,256]{1,0:T(1,128)}, f32[1,256]{1,0:T(1,128)S(1)}, u32[]{:S(2)}) copy-start(f32[1,256]{1,0:T(1,128)S(1)} %get-tuple-element.215) | copy-start | bytes 3076
  3.3 18.9 %copy-start.23 = (f32[1,256]{1,0:T(1,128)}, f32[1,256]{1,0:T(1,128)S(1)}, u32[]{:S(2)}) copy-start(f32[1,256]{1,0:T(1,128)S(1)} %convert_element_type.116) | copy-start | bytes 3076
  3.3 15.7 %collective-permute-start = (f32[5,45]{1,0:T(8,128)S(1)}, f32[5,45]{1,0:T(8,128)S(1)}, u32[]{:S(2)}, u32[]{:S(2)}) collective-permute-start(f32[5,45]{1,0:T(8,128)S(1)} %get-tuple-element.202), channel_id=1, source_target_pairs={{0,1},{1,2},{2,3},{3,4},{4,5},{5,6},{6,7},{7,8},{8,9},{9,10},{10,1... | collective-permute-start | bytes 2708 | tf_op jit(solution)/shard_map/ppermute | solution.py:35
  5.1 14.0 %collective-permute-start.1 = (f32[5,45]{1,0:T(8,128)S(1)}, f32[5,45]{1,0:T(8,128)S(1)}, u32[]{:S(2)}, u32[]{:S(2)}) collective-permute-start(f32[5,45]{1,0:T(8,128)S(1)} %get-tuple-element.203), channel_id=1, source_target_pairs={{1,0},{2,1},{3,2},{4,3},{5,4},{6,5},{7,6},{8,7},{9,8},{10,9},{11,1... | collective-permute-start | bytes 2708 | tf_op jit(solution)/shard_map/ppermute | solution.py:37
  7.1 9.6 %copy-start.12 = (f32[1,3,256]{2,1,0:T(4,128)}, f32[1,3,256]{2,1,0:T(4,128)S(1)}, u32[]{:S(2)}) copy-start(f32[1,3,256]{2,1,0:T(4,128)S(1)} %copy.195) | copy-start | bytes 9220
  7.7 63.1 %collective-permute-start.2 = (f32[3,15]{1,0:T(4,128)}, f32[3,15]{1,0:T(4,128)}, u32[]{:S(2)}, u32[]{:S(2)}) collective-permute-start(f32[3,15]{1,0:T(4,128)} %get-tuple-element.212), channel_id=1, source_target_pairs={{0,1},{1,2},{2,3},{3,4},{4,5},{5,6},{6,7},{7,8},{8,9},{9,10},{10,1... | collective-permute-start | bytes 548 | tf_op jit(solution)/shard_map/ppermute | solution.py:35
  13.2 57.6 %collective-permute-start.3 = (f32[3,15]{1,0:T(4,128)}, f32[3,15]{1,0:T(4,128)}, u32[]{:S(2)}, u32[]{:S(2)}) collective-permute-start(f32[3,15]{1,0:T(4,128)} %get-tuple-element.213), channel_id=1, source_target_pairs={{1,0},{2,1},{3,2},{4,3},{5,4},{6,5},{7,6},{8,7},{9,8},{10,9},{11,1... | collective-permute-start | bytes 548 | tf_op jit(solution)/shard_map/ppermute | solution.py:37
  16.7 5.5 %copy-start.1 = (f32[30,3]{1,0:T(8,128)}, f32[30,3]{1,0:T(8,128)S(1)}, u32[]{:S(2)}) copy-start(f32[30,3]{1,0:T(8,128)S(1)} %copy.141) | copy-start | bytes 1084
  17.9 8.0 %copy-start = (f32[5,81,80]{1,2,0:T(8,128)S(1)}, f32[5,81,80]{1,2,0:T(8,128)}, u32[]{:S(2)}) copy-start(f32[5,81,80]{1,2,0:T(8,128)} %param.40) | copy-start | bytes 388804
  24.1 2.6 copy-start.7
  28.1 0.9 copy-start.8
  28.1 4.1 %copy-start.18 = (f32[5,45]{1,0:T(8,128)S(1)}, f32[5,45]{1,0:T(8,128)}, u32[]{:S(2)}) copy-start(f32[5,45]{1,0:T(8,128)} %copy-done.17) | copy-start | bytes 2704
  28.1 4.1 %copy-start.20 = (f32[5,45]{1,0:T(8,128)S(1)}, f32[5,45]{1,0:T(8,128)}, u32[]{:S(2)}) copy-start(f32[5,45]{1,0:T(8,128)} %copy-done.19) | copy-start | bytes 2704
  28.1 4.1 %copy-start.22 = (f32[1,256]{1,0:T(1,128)S(1)}, f32[1,256]{1,0:T(1,128)}, u32[]{:S(2)}) copy-start(f32[1,256]{1,0:T(1,128)} %copy-done.21) | copy-start | bytes 3076
  28.1 4.1 %copy-start.24 = (f32[1,256]{1,0:T(1,128)S(1)}, f32[1,256]{1,0:T(1,128)}, u32[]{:S(2)}) copy-start(f32[1,256]{1,0:T(1,128)} %copy-done.23) | copy-start | bytes 3076
  38.3 26.2 %copy-start.5 = (f32[5,286]{1,0:T(8,128)S(1)}, f32[5,286]{1,0:T(8,128)}, u32[]{:S(2)}) copy-start(f32[5,286]{1,0:T(8,128)} %slice.1612) | copy-start | bytes 17164
  64.5 6.1 %copy-start.14 = (s32[286]{0:T(512)S(1)}, s32[286]{0:T(512)}, u32[]{:S(2)}) copy-start(s32[286]{0:T(512)} %fusion.144) | copy-start | bytes 3436
  64.5 6.1 %copy-start.25 = (pred[30]{0:T(512)(128)(4,1)S(1)}, pred[30]{0:T(512)(128)(4,1)}, u32[]{:S(2)}) copy-start(pred[30]{0:T(512)(128)(4,1)} %constant.96.clone) | copy-start | bytes 94
  64.5 6.1 %copy-start.28 = (s32[30]{0:T(128)S(1)}, s32[30]{0:T(128)}, u32[]{:S(2)}) copy-start(s32[30]{0:T(128)} %constant.97.clone) | copy-start | bytes 364
  64.5 6.2 %copy-start.10 = (f32[3,286]{1,0:T(4,128)S(1)}, f32[3,286]{1,0:T(4,128)}, u32[]{:S(2)}) copy-start(f32[3,286]{1,0:T(4,128)} %slice.1644) | copy-start | bytes 10300
  64.5 6.3 %copy-start.13 = (f32[1,3,256]{2,1,0:T(4,128)S(1)}, f32[1,3,256]{2,1,0:T(4,128)}, u32[]{:S(2)}) copy-start(f32[1,3,256]{2,1,0:T(4,128)} %copy-done.12) | copy-start | bytes 9220
  67.4 10.7 %copy-start.2 = (f32[30,3]{1,0:T(8,128)S(1)}, f32[30,3]{1,0:T(8,128)}, u32[]{:S(2)}) copy-start(f32[30,3]{1,0:T(8,128)} %copy-done.1) | copy-start | bytes 1084
  81.7 88.3 %copy-start.9 = (f32[5,316]{1,0:T(8,128)S(1)}, f32[5,316]{1,0:T(8,128)}, u32[]{:S(2)}) copy-start(f32[5,316]{1,0:T(8,128)} %copy-done.7) | copy-start | bytes 18964
  120.4 3.1 collective-permute-start.4
  123.4 5.5 %collective-permute-start.5 = (f32[2026]{0:T(1024)S(1)}, f32[2026]{0:T(1024)S(1)}, u32[]{:S(2)}, u32[]{:S(2)}) collective-permute-start(f32[2026]{0:T(1024)S(1)} %add.2773), channel_id=1, source_target_pairs={{0,64},{64,0},{1,65},{65,1},{2,66},{66,2},{3,67},{67,3},{4,68},{68... | collective-permute-start | bytes 24320 | tf_op jit(solution)/shard_map/ppermute | solution.py:65
  129.0 7.0 %collective-permute-start.6 = (f32[2026]{0:T(1024)S(1)}, f32[2026]{0:T(1024)S(1)}, u32[]{:S(2)}, u32[]{:S(2)}) collective-permute-start(f32[2026]{0:T(1024)S(1)} %add.2774), channel_id=1, source_target_pairs={{0,2},{2,0},{1,3},{3,1},{4,6},{6,4},{5,7},{7,5},{8,10},{10,8},{9,1... | collective-permute-start | bytes 24320 | tf_op jit(solution)/shard_map/ppermute | solution.py:65
  136.0 5.5 %collective-permute-start.7 = (f32[2026]{0:T(1024)S(1)}, f32[2026]{0:T(1024)S(1)}, u32[]{:S(2)}, u32[]{:S(2)}) collective-permute-start(f32[2026]{0:T(1024)S(1)} %add.2775), channel_id=1, source_target_pairs={{0,128},{128,0},{256,384},{384,256},{1,129},{129,1},{257,385},{385... | collective-permute-start | bytes 24320 | tf_op jit(solution)/shard_map/ppermute | solution.py:65
  141.5 7.0 %collective-permute-start.8 = (f32[2026]{0:T(1024)S(1)}, f32[2026]{0:T(1024)S(1)}, u32[]{:S(2)}, u32[]{:S(2)}) collective-permute-start(f32[2026]{0:T(1024)S(1)} %add.2776), channel_id=1, source_target_pairs={{0,256},{128,384},{256,0},{384,128},{1,257},{129,385},{257,1},{385... | collective-permute-start | bytes 24320 | tf_op jit(solution)/shard_map/ppermute | solution.py:65
  149.3 17.2 %all-to-all-start.1 = ((f32[16,1,2026]{2,1,0:T(1,128)}), f32[16,1,2026]{2,1,0:T(1,128)S(1)}, u32[]{:S(2)}, u32[]{:S(2)}) async-start(f32[16,1,2026]{2,1,0:T(1,128)} %broadcast_in_dim.108), calls=%async_computation.1 | async-start | bytes 262144 | tf_op jit(solution)/shard_map/all_to_all | solution.py:55
  172.5 0.9 copy-start.26
  172.5 0.9 copy-start.29
  172.6 1.0 copy-start.11
  196.3 3.1 collective-permute-start.9
  199.4 5.5 %collective-permute-start.10 = (f32[2026]{0:T(1024)S(1)}, f32[2026]{0:T(1024)S(1)}, u32[]{:S(2)}, u32[]{:S(2)}) collective-permute-start(f32[2026]{0:T(1024)S(1)} %add.2803), channel_id=1, source_target_pairs={{0,64},{64,0},{1,65},{65,1},{2,66},{66,2},{3,67},{67,3},{4,68},{68... | collective-permute-start | bytes 24320 | tf_op jit(solution)/shard_map/ppermute | solution.py:65
  204.9 7.0 %collective-permute-start.11 = (f32[2026]{0:T(1024)S(1)}, f32[2026]{0:T(1024)S(1)}, u32[]{:S(2)}, u32[]{:S(2)}) collective-permute-start(f32[2026]{0:T(1024)S(1)} %add.2804), channel_id=1, source_target_pairs={{0,2},{2,0},{1,3},{3,1},{4,6},{6,4},{5,7},{7,5},{8,10},{10,8},{9,1... | collective-permute-start | bytes 24320 | tf_op jit(solution)/shard_map/ppermute | solution.py:65
  212.0 5.5 %collective-permute-start.12 = (f32[2026]{0:T(1024)S(1)}, f32[2026]{0:T(1024)S(1)}, u32[]{:S(2)}, u32[]{:S(2)}) collective-permute-start(f32[2026]{0:T(1024)S(1)} %add.2805), channel_id=1, source_target_pairs={{0,128},{128,0},{256,384},{384,256},{1,129},{129,1},{257,385},{385... | collective-permute-start | bytes 24320 | tf_op jit(solution)/shard_map/ppermute | solution.py:65
  217.5 7.0 %collective-permute-start.13 = (f32[2026]{0:T(1024)S(1)}, f32[2026]{0:T(1024)S(1)}, u32[]{:S(2)}, u32[]{:S(2)}) collective-permute-start(f32[2026]{0:T(1024)S(1)} %add.2806), channel_id=1, source_target_pairs={{0,256},{128,384},{256,0},{384,128},{1,257},{129,385},{257,1},{385... | collective-permute-start | bytes 24320 | tf_op jit(solution)/shard_map/ppermute | solution.py:65
  247.4 1.0 copy-start.16
  247.4 1.0 copy-start.27
  247.4 0.9 copy-start.30
  248.4 56.9 %copy-start.3 = (f32[5,81,80]{1,2,0:T(8,128)S(1)}, f32[5,81,80]{1,2,0:T(8,128)}, u32[]{:S(2)}) copy-start(f32[5,81,80]{1,2,0:T(8,128)} %param.41) | copy-start | bytes 388804
  248.4 57.0 %copy-start.4 = (f32[5,81,80]{1,2,0:T(8,128)S(1)}, f32[5,81,80]{1,2,0:T(8,128)}, u32[]{:S(2)}) copy-start(f32[5,81,80]{1,2,0:T(8,128)} %param.42) | copy-start | bytes 388804
  271.2 3.1 collective-permute-start.14
  274.3 5.5 %collective-permute-start.15 = (f32[2026]{0:T(1024)S(1)}, f32[2026]{0:T(1024)S(1)}, u32[]{:S(2)}, u32[]{:S(2)}) collective-permute-start(f32[2026]{0:T(1024)S(1)} %add.2850), channel_id=1, source_target_pairs={{0,64},{64,0},{1,65},{65,1},{2,66},{66,2},{3,67},{67,3},{4,68},{68... | collective-permute-start | bytes 24320 | tf_op jit(solution)/shard_map/ppermute | solution.py:65
  279.8 7.0 %collective-permute-start.16 = (f32[2026]{0:T(1024)S(1)}, f32[2026]{0:T(1024)S(1)}, u32[]{:S(2)}, u32[]{:S(2)}) collective-permute-start(f32[2026]{0:T(1024)S(1)} %add.2851), channel_id=1, source_target_pairs={{0,2},{2,0},{1,3},{3,1},{4,6},{6,4},{5,7},{7,5},{8,10},{10,8},{9,1... | collective-permute-start | bytes 24320 | tf_op jit(solution)/shard_map/ppermute | solution.py:65
  286.9 5.5 %collective-permute-start.17 = (f32[2026]{0:T(1024)S(1)}, f32[2026]{0:T(1024)S(1)}, u32[]{:S(2)}, u32[]{:S(2)}) collective-permute-start(f32[2026]{0:T(1024)S(1)} %add.2852), channel_id=1, source_target_pairs={{0,128},{128,0},{256,384},{384,256},{1,129},{129,1},{257,385},{385... | collective-permute-start | bytes 24320 | tf_op jit(solution)/shard_map/ppermute | solution.py:65
  292.4 7.0 %collective-permute-start.18 = (f32[2026]{0:T(1024)S(1)}, f32[2026]{0:T(1024)S(1)}, u32[]{:S(2)}, u32[]{:S(2)}) collective-permute-start(f32[2026]{0:T(1024)S(1)} %add.2853), channel_id=1, source_target_pairs={{0,256},{128,384},{256,0},{384,128},{1,257},{129,385},{257,1},{385... | collective-permute-start | bytes 24320 | tf_op jit(solution)/shard_map/ppermute | solution.py:65
  300.2 17.1 %all-to-all-start.5 = ((f32[16,1,2026]{2,1,0:T(1,128)}), f32[16,1,2026]{2,1,0:T(1,128)S(1)}, u32[]{:S(2)}, u32[]{:S(2)}) async-start(f32[16,1,2026]{2,1,0:T(1,128)} %broadcast_in_dim.118), calls=%async_computation.5 | async-start | bytes 262144 | tf_op jit(solution)/shard_map/all_to_all | solution.py:55
  (4 other events, 2.8 us)

commit v5 on v4

--- a/solution.py
+++ b/solution.py
@@ -14,7 +14,8 @@
 SNAP = ("snap_0", "snap_1")
 BRICK = ("brick_0", "brick_1", "brick_2")
 SNAP_BRICK = ("snap_0", "snap_1", "brick_0", "brick_1", "brick_2")
-BUTTERFLY_ORDER = ("brick_2", "snap_1", "brick_1", "snap_0")
+BUTTERFLY_ORDER = ("brick_2", "snap_1", "brick_1")
+SPREAD_AXES = ("snap_0", "brick_0")
 
 
 cutoff_sq = 36.0
@@ -46,7 +47,9 @@
 
 
 def group_sum(shard, spread_axis, axes):
-    count = lax.axis_size(spread_axis)
+    count = 1
+    for axis in spread_axis:
+        count *= lax.axis_size(axis)
     length = shard.shape[0]
     padded = jnp.pad(shard, (0, (-length) % count))
     parts = lax.all_to_all(padded.reshape(count, -1), spread_axis, 0, 0, tiled=False)
@@ -138,19 +141,26 @@
 def pull_force(slopes, slopes_pad, padded, own_kinds, atom_count):
     delta, radial, slope, other, linked = pair_tables(padded, atom_count)
     own_grid = slopes.reshape(SPECIES, RADIAL, atom_count)
-    there_slopes = shifted_stack(slopes_pad, atom_count).reshape(
-        2 * WINDOW, SPECIES, RADIAL, atom_count
-    )
     outward = jnp.sum(other[:, :, None, :] * own_grid[None], axis=1)
-    inward = jnp.sum(own_kinds[None, :, None, :] * there_slopes, axis=1)
-    strength = jnp.sum((outward + inward) * slope, axis=1) * linked * (2.0 / cutoff_sq)
-    return jnp.sum(strength[:, None, :] * delta, axis=0)
+    total = jnp.zeros((3, atom_count), jnp.float32)
+    for index, offset in enumerate(window_offsets()):
+        there = slopes_pad[:, WINDOW + offset : WINDOW + offset + atom_count].reshape(
+            SPECIES, RADIAL, atom_count
+        )
+        inward = jnp.sum(own_kinds[:, None, :] * there, axis=0)
+        strength = jnp.sum((outward[index] + inward) * slope[index], axis=0)
+        strength = strength * linked[index] * (2.0 / cutoff_sq)
+        total = total + strength[None, :] * delta[index]
+    return total
 
 
 def back_terms(field_density, values, value_pad, padded, own_kinds, atom_count):
     delta, radial, slope, other, linked = pair_tables(padded, atom_count)
-    there_values = shifted_stack(value_pad, atom_count)
-    project = jnp.sum(delta * (values[None] - there_values), axis=1) * linked * (2.0 / cutoff_sq)
+    rows = [
+        jnp.sum(delta[index] * (values - value_pad[:, WINDOW + offset : WINDOW + offset + atom_count]), axis=0)
+        for index, offset in enumerate(window_offsets())
+    ]
+    project = jnp.stack(rows) * linked * (2.0 / cutoff_sq)
     channels = field_density.shape[0]
     weights = jnp.sum(
         other[:, :, None, :] * (slope * project[:, None, :])[:, None], axis=0
@@ -221,7 +231,7 @@
         packed = jnp.concatenate(
             [local_terms.reshape(-1), jnp.sum(raw_left * raw_left)[None]]
         )
-        packed = group_sum(packed, "brick_0", BUTTERFLY_ORDER)
+        packed = group_sum(packed, SPREAD_AXES, BUTTERFLY_ORDER)
         totals = packed[:-1].reshape(local_terms.shape)
         squares = packed[-1]
         beta_norm = jnp.sqrt(squares / left_total + tiny)

time: 326 us -> 274 us (0.84)
  the two profiles are of different devices: /device:TPU:10 before, /device:TPU:1 now
where the time goes in v5:
time: 274 us; the launch traced here: 271 us
  blocking collectives  86.9 us (32%)
  starting transfers between devices  62.9 us (23%)
  waiting for transfers between devices  44.1 us (16%)
  local copies, waits for them, and re-layouts  33.2 us (12%)
  other arithmetic  30.4 us (11%)
  between operations  10.1 us (4%)
  matrix products  3.53 us (1%)
    all_to_all x3, blocking collectives, group_sum(): lax.all_to_all(padded.reshape(count, -1), spread_axis, 0, 0, tiled=False)  67.9 us
    ppermute x9, starting transfers between devices, butterfly_sum(): shard = shard + lax.ppermute(shard, axis, partners)  34.5 us
    all_to_all x2, waiting for transfers between devices, group_sum(): whole = lax.all_to_all(spread, spread_axis, 0, 0, tiled=False)  23.7 us
    ppermute x9, waiting for transfers between devices, butterfly_sum(): shard = shard + lax.ppermute(shard, axis, partners)  20.4 us
    all_to_all x1, blocking collectives, group_sum(): whole = lax.all_to_all(spread, spread_axis, 0, 0, tiled=False)  19 us
    unnamed x237, local copies, waits for them, and re-layouts  12.1 us
    ppermute x2, starting transfers between devices, with_halo(): lax.ppermute(head, axis, [((i + 1) % count, i) for i in range(ends)])  11.7 us
    all_to_all x2, starting transfers between devices, group_sum(): whole = lax.all_to_all(spread, spread_axis, 0, 0, tiled=False)  10.7 us
  transfers between devices with their start and end apart: 15, of which 11 were waited for; matrix products, arithmetic and copies ran while one was open for 11% of the time, Pallas kernels for 0%

profile of v5, /device:TPU:1, one launch (start us, length us, event | category | flops | bytes accessed | tf_op | source)
XLA Modules:
  0.0 271.0 jit_solution(11879311940380148958)
XLA Ops:
  2.0 8.7 %collective-permute-start.3 = (f32[3,15]{1,0:T(4,128)}, f32[3,15]{1,0:T(4,128)S(1)}, u32[]{:S(2)}, u32[]{:S(2)}) collective-permute-start(f32[3,15]{1,0:T(4,128)} %get-tuple-element.546), channel_id=1, source_target_pairs={{1,0},{2,1},{3,2},{4,3},{5,4},{6,5},{7,6},{8,7},{9,8},{10,9},{11,1... | collective-permute-start | bytes 548 | tf_op jit(solution)/shard_map/ppermute | solution.py:38
  10.8 1.9 collective-permute-start.2
  14.8 3.0 %collective-permute-start.1 = (f32[5,45]{1,0:T(8,128)S(1)}, f32[5,45]{1,0:T(8,128)S(1)}, u32[]{:S(2)}, u32[]{:S(2)}) collective-permute-start(f32[5,45]{1,0:T(8,128)S(1)} %get-tuple-element.542), channel_id=1, source_target_pairs={{1,0},{2,1},{3,2},{4,3},{5,4},{6,5},{7,6},{8,7},{9,8},{10,9},{11,1... | collective-permute-start | bytes 2708 | tf_op jit(solution)/shard_map/ppermute | solution.py:38
  17.8 4.1 %collective-permute-start = (f32[5,45]{1,0:T(8,128)S(1)}, f32[5,45]{1,0:T(8,128)S(1)}, u32[]{:S(2)}, u32[]{:S(2)}) collective-permute-start(f32[5,45]{1,0:T(8,128)S(1)} %get-tuple-element.541), channel_id=1, source_target_pairs={{0,1},{1,2},{2,3},{3,4},{4,5},{5,6},{6,7},{7,8},{8,9},{9,10},{10,1... | collective-permute-start | bytes 2708 | tf_op jit(solution)/shard_map/ppermute | solution.py:36
  21.9 0.7 broadcast_multiply_fusion.6
  22.7 1.4 fusion.603
  24.0 1.0 slice.2651
  29.4 1.3 stack.889
  31.9 1.3 fusion.600
  33.3 1.5 fusion.599
  39.6 0.8 multiply_reduce_fusion.104
  40.8 3.6 %fusion.87 = (f32[30,1,286]{2,1,0:T(1,128)}, f32[30,1,286]{2,1,0:T(1,128)}, f32[30,1,286]{2,1,0:T(1,128)}, f32[30,1,286]{2,1,0:T(1,128)}, f32[30,1,286]{2,1,0:T(...) fusion(f32[30,286]{1,0:T(8,128)S(1)} %get-tuple-element.535, ...), kind=kLoop, calls=%fused_computation.506 | loop fusion | flops 1244100 | bytes 617760 | tf_op jit(solution)/shard_map/mul | solution.py:95
  44.4 0.9 multiply_reduce_fusion.85
  45.3 3.1 %stack.923 = f32[30,16,286]{2,1,0:T(8,128)S(1)} concatenate(f32[30,1,286]{2,1,0:T(1,128)} %get-tuple-element.533, f32[30,1,286]{2,1,0:T(1,128)} %get-tuple-element.490, f32[30,1,286]{2,1,0:T(1,128)} %get-tuple-element.492, f32[30,1,286]{2,1,0:T(1,128)} %get-tuple-element.494, f32[30,1,286]{2,1,0:T(1,128)} %get-tuple-element.496, f32[30,1,286]{2,1,0:T(1,128)} %get-tuple-element.498, ...), dimensions={1} | concatenate | bytes 1098240 | tf_op jit(solution)/shard_map/stack | solution.py:96
  48.5 1.7 multiply_reduce_fusion.103
  51.4 1.3 fusion.406
  54.3 1.2 multiply_multiply_fusion.47
  55.6 1.2 fusion.134
  60.0 29.5 %all_to_all.45 = f32[64,1,507]{2,1,0:T(1,128)S(1)} all-to-all(f32[64,1,507]{2,1,0:T(1,128)S(1)} %all_to_all.30), channel_id=1, replica_groups=mesh['snap_0'=4,'snap_1'=2,'brick_0'=16,'brick_1'=2,'brick_2'=2] {'snap_..., dimensions={0} | all-to-all | bytes 259584 | tf_op jit(solution)/shard_map/all_to_all | solution.py:55
  89.6 7.9 %collective-permute-start.4 = (f32[507]{0:T(512)S(1)}, f32[507]{0:T(512)S(1)}, u32[]{:S(2)}, u32[]{:S(2)}) collective-permute-start(f32[507]{0:T(512)S(1)} %reduce_sum.3001), channel_id=1, source_target_pairs={{0,1},{1,0},{2,3},{3,2},{4,5},{5,4},{6,7},{7,6},{8,9},{9,8},{10,11... | collective-permute-start | bytes 6092 | tf_op jit(solution)/shard_map/ppermute | solution.py:68
  97.5 0.8 collective-permute-done.4
  98.3 2.2 collective-permute-start.5
  100.5 2.1 collective-permute-done.5
  102.6 1.9 collective-permute-start.6
  104.5 3.9 %collective-permute-done.6 = f32[507]{0:T(512)S(1)} collective-permute-done((f32[507]{0:T(512)S(1)}, f32[507]{0:T(512)S(1)}, u32[]{:S(2)}, u32[]{:S(2)}) %collective-permute-start.6) | collective-permute-done | bytes 2060 | tf_op jit(solution)/shard_map/ppermute | solution.py:68
  109.2 5.5 %all-to-all-start.1 = ((f32[64,1,507]{2,1,0:T(1,128)}), f32[64,1,507]{2,1,0:T(1,128)S(1)}, u32[]{:S(2)}, u32[]{:S(2)}) async-start(f32[64,1,507]{2,1,0:T(1,128)} %broadcast_in_dim.105), calls=%async_computation.1 | async-start | bytes 262144 | tf_op jit(solution)/shard_map/all_to_all | solution.py:58
  114.8 13.6 %all-to-all-done.1 = f32[64,1,507]{2,1,0:T(1,128)S(1)} async-done(((f32[64,1,507]{2,1,0:T(1,128)}), f32[64,1,507]{2,1,0:T(1,128)S(1)}, u32[]{:S(2)}, u32[]{:S(2)}) %all-to-all-start.1) | async-done | bytes 129824 | tf_op jit(solution)/shard_map/all_to_all | solution.py:58
  139.1 19.2 %all_to_all.46 = f32[64,1,507]{2,1,0:T(1,128)S(1)} all-to-all(f32[64,1,507]{2,1,0:T(1,128)S(1)} %all_to_all.33), channel_id=1, replica_groups=mesh['snap_0'=4,'snap_1'=2,'brick_0'=16,'brick_1'=2,'brick_2'=2] {'snap_..., dimensions={0} | all-to-all | bytes 259584 | tf_op jit(solution)/shard_map/all_to_all | solution.py:55
  158.4 7.1 %collective-permute-start.7 = (f32[507]{0:T(512)S(1)}, f32[507]{0:T(512)S(1)}, u32[]{:S(2)}, u32[]{:S(2)}) collective-permute-start(f32[507]{0:T(512)S(1)} %reduce_sum.3129), channel_id=1, source_target_pairs={{0,1},{1,0},{2,3},{3,2},{4,5},{5,4},{6,7},{7,6},{8,9},{9,8},{10,11... | collective-permute-start | bytes 6092 | tf_op jit(solution)/shard_map/ppermute | solution.py:68
  165.5 0.8 collective-permute-done.7
  166.3 2.2 collective-permute-start.8
  168.6 2.1 collective-permute-done.8
  170.7 1.9 collective-permute-start.9
  172.6 3.9 %collective-permute-done.9 = f32[507]{0:T(512)S(1)} collective-permute-done((f32[507]{0:T(512)S(1)}, f32[507]{0:T(512)S(1)}, u32[]{:S(2)}, u32[]{:S(2)}) %collective-permute-start.9) | collective-permute-done | bytes 2060 | tf_op jit(solution)/shard_map/ppermute | solution.py:68
  176.6 19.0 %all_to_all.47 = f32[64,1,507]{2,1,0:T(1,128)S(1)} all-to-all(f32[64,1,507]{2,1,0:T(1,128)S(1)} %broadcast_in_dim.110), channel_id=1, replica_groups=mesh['snap_0'=4,'snap_1'=2,'brick_0'=16,'brick_1'=2,'brick_2'=2] {'snap_..., dimensions={0} | all-to-all | bytes 259584 | tf_op jit(solution)/shard_map/all_to_all | solution.py:58
  205.2 0.8 select_maximum_fusion
  206.3 19.2 %all_to_all.48 = f32[64,1,507]{2,1,0:T(1,128)S(1)} all-to-all(f32[64,1,507]{2,1,0:T(1,128)S(1)} %all_to_all.36), channel_id=1, replica_groups=mesh['snap_0'=4,'snap_1'=2,'brick_0'=16,'brick_1'=2,'brick_2'=2] {'snap_..., dimensions={0} | all-to-all | bytes 259584 | tf_op jit(solution)/shard_map/all_to_all | solution.py:55
  225.6 7.1 %collective-permute-start.10 = (f32[507]{0:T(512)S(1)}, f32[507]{0:T(512)S(1)}, u32[]{:S(2)}, u32[]{:S(2)}) collective-permute-start(f32[507]{0:T(512)S(1)} %reduce_sum.3258), channel_id=1, source_target_pairs={{0,1},{1,0},{2,3},{3,2},{4,5},{5,4},{6,7},{7,6},{8,9},{9,8},{10,11... | collective-permute-start | bytes 6092 | tf_op jit(solution)/shard_map/ppermute | solution.py:68
  232.7 0.8 collective-permute-done.10
  233.5 2.2 collective-permute-start.11
  235.8 2.1 collective-permute-done.11
  237.9 1.9 collective-permute-start.12
  239.8 3.9 %collective-permute-done.12 = f32[507]{0:T(512)S(1)} collective-permute-done((f32[507]{0:T(512)S(1)}, f32[507]{0:T(512)S(1)}, u32[]{:S(2)}, u32[]{:S(2)}) %collective-permute-start.12) | collective-permute-done | bytes 2060 | tf_op jit(solution)/shard_map/ppermute | solution.py:68
  244.4 5.2 %all-to-all-start.5 = ((f32[64,1,507]{2,1,0:T(1,128)}), f32[64,1,507]{2,1,0:T(1,128)S(1)}, u32[]{:S(2)}, u32[]{:S(2)}) async-start(f32[64,1,507]{2,1,0:T(1,128)} %broadcast_in_dim.115), calls=%async_computation.5 | async-start | bytes 262144 | tf_op jit(solution)/shard_map/all_to_all | solution.py:58
  253.6 10.1 %all-to-all-done.5 = f32[64,1,507]{2,1,0:T(1,128)S(1)} async-done(((f32[64,1,507]{2,1,0:T(1,128)}), f32[64,1,507]{2,1,0:T(1,128)S(1)}, u32[]{:S(2)}, u32[]{:S(2)}) %all-to-all-start.5) | async-done | bytes 129824 | tf_op jit(solution)/shard_map/all_to_all | solution.py:58
  268.0 0.8 copy.95
  268.8 0.8 copy.96
  269.6 0.8 copy.97
  (415 shorter events, 42.8 us)
Async XLA Ops:
  0.6 24.6 %copy-start = (f32[5,81,80]{1,2,0:T(8,128)S(1)}, f32[5,81,80]{1,2,0:T(8,128)}, u32[]{:S(2)}) copy-start(f32[5,81,80]{1,2,0:T(8,128)} %param.40) | copy-start | bytes 388804
  2.0 49.4 %collective-permute-start.3 = (f32[3,15]{1,0:T(4,128)}, f32[3,15]{1,0:T(4,128)S(1)}, u32[]{:S(2)}, u32[]{:S(2)}) collective-permute-start(f32[3,15]{1,0:T(4,128)} %get-tuple-element.546), channel_id=1, source_target_pairs={{1,0},{2,1},{3,2},{4,3},{5,4},{6,5},{7,6},{8,7},{9,8},{10,9},{11,1... | collective-permute-start | bytes 548 | tf_op jit(solution)/shard_map/ppermute | solution.py:38
  10.8 40.6 %collective-permute-start.2 = (f32[3,15]{1,0:T(4,128)}, f32[3,15]{1,0:T(4,128)}, u32[]{:S(2)}, u32[]{:S(2)}) collective-permute-start(f32[3,15]{1,0:T(4,128)} %get-tuple-element.545), channel_id=1, source_target_pairs={{0,1},{1,2},{2,3},{3,4},{4,5},{5,6},{6,7},{7,8},{8,9},{9,10},{10,1... | collective-permute-start | bytes 548 | tf_op jit(solution)/shard_map/ppermute | solution.py:36
  14.8 10.5 %collective-permute-start.1 = (f32[5,45]{1,0:T(8,128)S(1)}, f32[5,45]{1,0:T(8,128)S(1)}, u32[]{:S(2)}, u32[]{:S(2)}) collective-permute-start(f32[5,45]{1,0:T(8,128)S(1)} %get-tuple-element.542), channel_id=1, source_target_pairs={{1,0},{2,1},{3,2},{4,3},{5,4},{6,5},{7,6},{8,7},{9,8},{10,9},{11,1... | collective-permute-start | bytes 2708 | tf_op jit(solution)/shard_map/ppermute | solution.py:38
  17.8 7.6 %collective-permute-start = (f32[5,45]{1,0:T(8,128)S(1)}, f32[5,45]{1,0:T(8,128)S(1)}, u32[]{:S(2)}, u32[]{:S(2)}) collective-permute-start(f32[5,45]{1,0:T(8,128)S(1)} %get-tuple-element.541), channel_id=1, source_target_pairs={{0,1},{1,2},{2,3},{3,4},{4,5},{5,6},{6,7},{7,8},{8,9},{9,10},{10,1... | collective-permute-start | bytes 2708 | tf_op jit(solution)/shard_map/ppermute | solution.py:36
  27.8 1.3 copy-start.21
  27.8 1.3 copy-start.22
  39.6 0.8 copy-start.7
  45.3 3.1 %copy-start.1 = (f32[80,286]{1,0:T(8,128)S(1)}, f32[80,286]{1,0:T(8,128)}, u32[]{:S(2)}) copy-start(f32[80,286]{1,0:T(8,128)} %get-tuple-element.480) | copy-start | bytes 274564
  45.3 3.1 %copy-start.2 = (f32[80,286]{1,0:T(8,128)S(1)}, f32[80,286]{1,0:T(8,128)}, u32[]{:S(2)}) copy-start(f32[80,286]{1,0:T(8,128)} %get-tuple-element.481) | copy-start | bytes 274564
  45.3 3.1 %copy-start.3 = (f32[80,286]{1,0:T(8,128)S(1)}, f32[80,286]{1,0:T(8,128)}, u32[]{:S(2)}) copy-start(f32[80,286]{1,0:T(8,128)} %get-tuple-element.482) | copy-start | bytes 274564
  45.3 3.1 %copy-start.4 = (f32[80,286]{1,0:T(8,128)S(1)}, f32[80,286]{1,0:T(8,128)}, u32[]{:S(2)}) copy-start(f32[80,286]{1,0:T(8,128)} %get-tuple-element.483) | copy-start | bytes 274564
  48.4 1.8 copy-start.16
  48.5 1.8 copy-start.17
  48.5 1.8 copy-start.18
  48.5 1.8 copy-start.19
  48.5 1.8 copy-start.20
  48.5 1.9 copy-start.11
  48.5 1.9 copy-start.12
  48.5 1.9 copy-start.13
  48.5 1.9 copy-start.14
  48.5 1.9 copy-start.15
  50.2 0.7 copy-start.9
  50.2 0.7 copy-start.10
  51.1 2.8 %copy-start.8 = (f32[30,256]{1,0:T(8,128)S(1)}, f32[30,256]{1,0:T(8,128)}, u32[]{:S(2)}) copy-start(f32[30,256]{1,0:T(8,128)} %get-tuple-element.387) | copy-start | bytes 92164
  89.6 8.7 %collective-permute-start.4 = (f32[507]{0:T(512)S(1)}, f32[507]{0:T(512)S(1)}, u32[]{:S(2)}, u32[]{:S(2)}) collective-permute-start(f32[507]{0:T(512)S(1)} %reduce_sum.3001), channel_id=1, source_target_pairs={{0,1},{1,0},{2,3},{3,2},{4,5},{5,4},{6,7},{7,6},{8,9},{9,8},{10,11... | collective-permute-start | bytes 6092 | tf_op jit(solution)/shard_map/ppermute | solution.py:68
  98.3 4.3 %collective-permute-start.5 = (f32[507]{0:T(512)S(1)}, f32[507]{0:T(512)S(1)}, u32[]{:S(2)}, u32[]{:S(2)}) collective-permute-start(f32[507]{0:T(512)S(1)} %add.3335), channel_id=1, source_target_pairs={{0,64},{64,0},{1,65},{65,1},{2,66},{66,2},{3,67},{67,3},{4,68},{68... | collective-permute-start | bytes 6092 | tf_op jit(solution)/shard_map/ppermute | solution.py:68
  102.6 5.8 %collective-permute-start.6 = (f32[507]{0:T(512)S(1)}, f32[507]{0:T(512)S(1)}, u32[]{:S(2)}, u32[]{:S(2)}) collective-permute-start(f32[507]{0:T(512)S(1)} %add.3336), channel_id=1, source_target_pairs={{0,2},{2,0},{1,3},{3,1},{4,6},{6,4},{5,7},{7,5},{8,10},{10,8},{9,1... | collective-permute-start | bytes 6092 | tf_op jit(solution)/shard_map/ppermute | solution.py:68
  109.2 19.2 %all-to-all-start.1 = ((f32[64,1,507]{2,1,0:T(1,128)}), f32[64,1,507]{2,1,0:T(1,128)S(1)}, u32[]{:S(2)}, u32[]{:S(2)}) async-start(f32[64,1,507]{2,1,0:T(1,128)} %broadcast_in_dim.105), calls=%async_computation.1 | async-start | bytes 262144 | tf_op jit(solution)/shard_map/all_to_all | solution.py:58
  158.4 7.9 %collective-permute-start.7 = (f32[507]{0:T(512)S(1)}, f32[507]{0:T(512)S(1)}, u32[]{:S(2)}, u32[]{:S(2)}) collective-permute-start(f32[507]{0:T(512)S(1)} %reduce_sum.3129), channel_id=1, source_target_pairs={{0,1},{1,0},{2,3},{3,2},{4,5},{5,4},{6,7},{7,6},{8,9},{9,8},{10,11... | collective-permute-start | bytes 6092 | tf_op jit(solution)/shard_map/ppermute | solution.py:68
  166.3 4.3 %collective-permute-start.8 = (f32[507]{0:T(512)S(1)}, f32[507]{0:T(512)S(1)}, u32[]{:S(2)}, u32[]{:S(2)}) collective-permute-start(f32[507]{0:T(512)S(1)} %add.3421), channel_id=1, source_target_pairs={{0,64},{64,0},{1,65},{65,1},{2,66},{66,2},{3,67},{67,3},{4,68},{68... | collective-permute-start | bytes 6092 | tf_op jit(solution)/shard_map/ppermute | solution.py:68
  170.7 5.8 %collective-permute-start.9 = (f32[507]{0:T(512)S(1)}, f32[507]{0:T(512)S(1)}, u32[]{:S(2)}, u32[]{:S(2)}) collective-permute-start(f32[507]{0:T(512)S(1)} %add.3422), channel_id=1, source_target_pairs={{0,2},{2,0},{1,3},{3,1},{4,6},{6,4},{5,7},{7,5},{8,10},{10,8},{9,1... | collective-permute-start | bytes 6092 | tf_op jit(solution)/shard_map/ppermute | solution.py:68
  205.2 44.4 %copy-start.5 = (f32[5,81,80]{1,2,0:T(8,128)S(1)}, f32[5,81,80]{1,2,0:T(8,128)}, u32[]{:S(2)}) copy-start(f32[5,81,80]{1,2,0:T(8,128)} %param.41) | copy-start | bytes 388804
  206.0 45.1 %copy-start.6 = (f32[5,81,80]{1,2,0:T(8,128)S(1)}, f32[5,81,80]{1,2,0:T(8,128)}, u32[]{:S(2)}) copy-start(f32[5,81,80]{1,2,0:T(8,128)} %param.42) | copy-start | bytes 388804
  225.6 7.9 %collective-permute-start.10 = (f32[507]{0:T(512)S(1)}, f32[507]{0:T(512)S(1)}, u32[]{:S(2)}, u32[]{:S(2)}) collective-permute-start(f32[507]{0:T(512)S(1)} %reduce_sum.3258), channel_id=1, source_target_pairs={{0,1},{1,0},{2,3},{3,2},{4,5},{5,4},{6,7},{7,6},{8,9},{9,8},{10,11... | collective-permute-start | bytes 6092 | tf_op jit(solution)/shard_map/ppermute | solution.py:68
  233.5 4.3 %collective-permute-start.11 = (f32[507]{0:T(512)S(1)}, f32[507]{0:T(512)S(1)}, u32[]{:S(2)}, u32[]{:S(2)}) collective-permute-start(f32[507]{0:T(512)S(1)} %add.3524), channel_id=1, source_target_pairs={{0,64},{64,0},{1,65},{65,1},{2,66},{66,2},{3,67},{67,3},{4,68},{68... | collective-permute-start | bytes 6092 | tf_op jit(solution)/shard_map/ppermute | solution.py:68
  237.9 5.8 %collective-permute-start.12 = (f32[507]{0:T(512)S(1)}, f32[507]{0:T(512)S(1)}, u32[]{:S(2)}, u32[]{:S(2)}) collective-permute-start(f32[507]{0:T(512)S(1)} %add.3525), channel_id=1, source_target_pairs={{0,2},{2,0},{1,3},{3,1},{4,6},{6,4},{5,7},{7,5},{8,10},{10,8},{9,1... | collective-permute-start | bytes 6092 | tf_op jit(solution)/shard_map/ppermute | solution.py:68
  244.4 19.2 %all-to-all-start.5 = ((f32[64,1,507]{2,1,0:T(1,128)}), f32[64,1,507]{2,1,0:T(1,128)S(1)}, u32[]{:S(2)}, u32[]{:S(2)}) async-start(f32[64,1,507]{2,1,0:T(1,128)} %broadcast_in_dim.115), calls=%async_computation.5 | async-start | bytes 262144 | tf_op jit(solution)/shard_map/all_to_all | solution.py:58

commit v6 on v5

--- a/solution.py
+++ b/solution.py
@@ -138,8 +138,14 @@
     return jnp.sum(own_kinds[:, None, :] * part, axis=0)
 
 
-def pull_force(slopes, slopes_pad, padded, own_kinds, atom_count):
-    delta, radial, slope, other, linked = pair_tables(padded, atom_count)
+def cut_tables(tables, start, count):
+    return tuple(lax.slice_in_dim(table, start, start + count, axis=table.ndim - 1) for table in tables)
+
+
+def pull_force(slopes, slopes_pad, padded, own_kinds, atom_count, tables=None):
+    if tables is None:
+        tables = pair_tables(padded, atom_count)
+    delta, radial, slope, other, linked = tables
     own_grid = slopes.reshape(SPECIES, RADIAL, atom_count)
     outward = jnp.sum(other[:, :, None, :] * own_grid[None], axis=1)
     total = jnp.zeros((3, atom_count), jnp.float32)
@@ -154,17 +160,18 @@
     return total
 
 
-def back_terms(field_density, values, value_pad, padded, own_kinds, atom_count):
-    delta, radial, slope, other, linked = pair_tables(padded, atom_count)
-    rows = [
-        jnp.sum(delta[index] * (values - value_pad[:, WINDOW + offset : WINDOW + offset + atom_count]), axis=0)
-        for index, offset in enumerate(window_offsets())
-    ]
-    project = jnp.stack(rows) * linked * (2.0 / cutoff_sq)
+def back_terms(field_density, values, value_pad, padded, own_kinds, atom_count, tables=None):
+    if tables is None:
+        tables = pair_tables(padded, atom_count)
+    delta, radial, slope, other, linked = tables
     channels = field_density.shape[0]
-    weights = jnp.sum(
-        other[:, :, None, :] * (slope * project[:, None, :])[:, None], axis=0
-    ).reshape(channels, atom_count)
+    weights = jnp.zeros((SPECIES, RADIAL, atom_count), jnp.float32)
+    for index, offset in enumerate(window_offsets()):
+        there = value_pad[:, WINDOW + offset : WINDOW + offset + atom_count]
+        project = jnp.sum(delta[index] * (values - there), axis=0)
+        project = project * linked[index] * (2.0 / cutoff_sq)
+        weights = weights + other[index][:, None, :] * (slope[index] * project[None, :])[None]
+    weights = weights.reshape(channels, atom_count)
     masked = own_kinds[:, None, :] * field_density[None]
     cross = jnp.einsum("zbi,ai->zba", masked, weights, precision=HIGHEST)
     linear = jnp.sum(own_kinds[:, None, :] * weights[None], axis=2)
@@ -199,7 +206,13 @@
     kind_values = jnp.arange(SPECIES, dtype=jnp.float32)
     ext_count = atom_count + 4 * WINDOW
     mid_count = atom_count + 2 * WINDOW
-    density_ext = density(padded_all, ext_count)
+    tables_ext = pair_tables(padded_all, ext_count)
+    _, radial_ext, _, other_ext, linked_ext = tables_ext
+    density_ext = jnp.sum(
+        other_ext[:, :, None, :] * (radial_ext * linked_ext[:, None, :])[:, None], axis=0
+    ).reshape(SPECIES * RADIAL, ext_count)
+    tables_mid = cut_tables(tables_ext, WINDOW, mid_count)
+    tables_own = cut_tables(tables_ext, 2 * WINDOW, atom_count)
     kinds_ext = (
         padded_all[3, WINDOW : WINDOW + ext_count][None, :] == kind_values[:, None]
     ).astype(jnp.float32)
@@ -224,10 +237,13 @@
             mid_geometry,
             mid_kinds,
             mid_count,
+            tables_mid,
         )
         raw_pad = force_unit * force_ext - alpha_norm * left_ext
         raw_left = raw_pad[:, WINDOW : WINDOW + atom_count]
-        local_terms = back_terms(field_density, raw_left, raw_pad, padded, own_kinds, atom_count)
+        local_terms = back_terms(
+            field_density, raw_left, raw_pad, padded, own_kinds, atom_count, tables_own
+        )
         packed = jnp.concatenate(
             [local_terms.reshape(-1), jnp.sum(raw_left * raw_left)[None]]
         )

time: 274 us -> 269 us (0.982)
  local copies, waits for them, and re-layouts: 33.2 us -> 27.8 us
    unnamed x237 -> x80, local copies, waits for them, and re-layouts: 12.1 us -> 7.51 us
  transfers between devices with their start and end apart: 15 -> 15, of which waited for: 11 -> 11; matrix products, arithmetic and copies ran while one was open for 11% -> 10% of each run, Pallas kernels for 0% -> 0%
where the time goes in v6:
time: 269 us; the launch traced here: 266 us
  blocking collectives  86.9 us (32%)
  starting transfers between devices  62.8 us (23%)
  waiting for transfers between devices  43.9 us (16%)
  other arithmetic  30.5 us (11%)
  local copies, waits for them, and re-layouts  27.8 us (10%)
  between operations  10.3 us (4%)
  matrix products  3.54 us (1%)
    all_to_all x3, blocking collectives, group_sum(): lax.all_to_all(padded.reshape(count, -1), spread_axis, 0, 0, tiled=False)  67.9 us
    ppermute x9, starting transfers between devices, butterfly_sum(): shard = shard + lax.ppermute(shard, axis, partners)  34.4 us
    all_to_all x2, waiting for transfers between devices, group_sum(): whole = lax.all_to_all(spread, spread_axis, 0, 0, tiled=False)  23.5 us
    ppermute x9, waiting for transfers between devices, butterfly_sum(): shard = shard + lax.ppermute(shard, axis, partners)  20.4 us
    all_to_all x1, blocking collectives, group_sum(): whole = lax.all_to_all(spread, spread_axis, 0, 0, tiled=False)  19 us
    ppermute x2, starting transfers between devices, with_halo(): lax.ppermute(head, axis, [((i + 1) % count, i) for i in range(ends)])  11.1 us
    all_to_all x2, starting transfers between devices, group_sum(): whole = lax.all_to_all(spread, spread_axis, 0, 0, tiled=False)  10.7 us
    unnamed x80, local copies, waits for them, and re-layouts  7.51 us
  transfers between devices with their start and end apart: 15, of which 11 were waited for; matrix products, arithmetic and copies ran while one was open for 10% of the time, Pallas kernels for 0%

profile of v6, /device:TPU:1, one launch (start us, length us, event | category | flops | bytes accessed | tf_op | source)
XLA Modules:
  0.0 265.8 jit_solution(17671930104436873183)
XLA Ops:
  0.6 0.7 copy.97
  2.0 8.7 %collective-permute-start.3 = (f32[3,15]{1,0:T(4,128)}, f32[3,15]{1,0:T(4,128)S(1)}, u32[]{:S(2)}, u32[]{:S(2)}) collective-permute-start(f32[3,15]{1,0:T(4,128)} %get-tuple-element.732), channel_id=1, source_target_pairs={{1,0},{2,1},{3,2},{4,3},{5,4},{6,5},{7,6},{8,7},{9,8},{10,9},{11,1... | collective-permute-start | bytes 548 | tf_op jit(solution)/shard_map/ppermute | solution.py:38
  10.8 1.9 collective-permute-start.2
  14.8 2.4 collective-permute-start.1
  17.2 4.7 %collective-permute-start = (f32[5,45]{1,0:T(8,128)S(1)}, f32[5,45]{1,0:T(8,128)S(1)}, u32[]{:S(2)}, u32[]{:S(2)}) collective-permute-start(f32[5,45]{1,0:T(8,128)S(1)} %get-tuple-element.729), channel_id=1, source_target_pairs={{0,1},{1,2},{2,3},{3,4},{4,5},{5,6},{6,7},{7,8},{8,9},{9,10},{10,1... | collective-permute-start | bytes 2708 | tf_op jit(solution)/shard_map/ppermute | solution.py:36
  21.9 0.7 broadcast_multiply_fusion.44
  22.6 1.4 fusion.550
  24.1 1.0 slice.2328
  28.3 3.6 %fusion.84 = (f32[30,1,316]{2,1,0:T(1,128)}, f32[30,1,316]{2,1,0:T(1,128)}, f32[30,1,316]{2,1,0:T(1,128)}, f32[30,1,316]{2,1,0:T(1,128)}, f32[30,1,316]{2,1,0:T(...) fusion(f32[30,316]{1,0:T(8,128)S(1)} %get-tuple-element.727, ...), kind=kLoop, calls=%fused_computation.351 | loop fusion | flops 1403040 | bytes 758400 | tf_op jit(solution)/shard_map/mul | solution.py:95
  32.9 1.4 stack.174
  34.8 0.7 fusion.8
  35.6 1.2 fusion.547
  36.8 1.5 fusion.546
  39.4 0.9 multiply_reduce_fusion.82
  40.3 2.9 %stack.175 = f32[30,16,316]{2,1,0:T(8,128)S(1)} concatenate(f32[30,1,316]{2,1,0:T(1,128)} %get-tuple-element.726, f32[30,1,316]{2,1,0:T(1,128)} %get-tuple-element.607, f32[30,1,316]{2,1,0:T(1,128)} %get-tuple-element.609, f32[30,1,316]{2,1,0:T(1,128)} %get-tuple-element.611, f32[30,1,316]{2,1,0:T(1,128)} %get-tuple-element.613, f32[30,1,316]{2,1,0:T(1,128)} %get-tuple-element.615, ...), dimensions={1} | concatenate | bytes 1213440 | tf_op jit(solution)/shard_map/stack | solution.py:96
  43.3 1.7 multiply_reduce_fusion.100
  46.7 0.8 fusion.356
  52.2 29.5 %all_to_all.45 = f32[64,1,507]{2,1,0:T(1,128)S(1)} all-to-all(f32[64,1,507]{2,1,0:T(1,128)S(1)} %all_to_all.30), channel_id=1, replica_groups=mesh['snap_0'=4,'snap_1'=2,'brick_0'=16,'brick_1'=2,'brick_2'=2] {'snap_..., dimensions={0} | all-to-all | bytes 259584 | tf_op jit(solution)/shard_map/all_to_all | solution.py:55
  81.9 7.9 %collective-permute-start.4 = (f32[507]{0:T(512)S(1)}, f32[507]{0:T(512)S(1)}, u32[]{:S(2)}, u32[]{:S(2)}) collective-permute-start(f32[507]{0:T(512)S(1)} %reduce_sum.3126), channel_id=1, source_target_pairs={{0,1},{1,0},{2,3},{3,2},{4,5},{5,4},{6,7},{7,6},{8,9},{9,8},{10,11... | collective-permute-start | bytes 6092 | tf_op jit(solution)/shard_map/ppermute | solution.py:68
  89.7 0.8 collective-permute-done.4
  90.5 2.2 collective-permute-start.5
  92.8 2.1 collective-permute-done.5
  94.9 1.9 collective-permute-start.6
  96.8 3.9 %collective-permute-done.6 = f32[507]{0:T(512)S(1)} collective-permute-done((f32[507]{0:T(512)S(1)}, f32[507]{0:T(512)S(1)}, u32[]{:S(2)}, u32[]{:S(2)}) %collective-permute-start.6) | collective-permute-done | bytes 2060 | tf_op jit(solution)/shard_map/ppermute | solution.py:68
  100.7 0.7 broadcast_in_dim.46
  101.4 5.4 %all-to-all-start.1 = ((f32[64,1,507]{2,1,0:T(1,128)}), f32[64,1,507]{2,1,0:T(1,128)S(1)}, u32[]{:S(2)}, u32[]{:S(2)}) async-start(f32[64,1,507]{2,1,0:T(1,128)} %broadcast_in_dim.46), calls=%async_computation.1 | async-start | bytes 262144 | tf_op jit(solution)/shard_map/all_to_all | solution.py:58
  107.0 13.6 %all-to-all-done.1 = f32[64,1,507]{2,1,0:T(1,128)S(1)} async-done(((f32[64,1,507]{2,1,0:T(1,128)}), f32[64,1,507]{2,1,0:T(1,128)S(1)}, u32[]{:S(2)}, u32[]{:S(2)}) %all-to-all-start.1) | async-done | bytes 129824 | tf_op jit(solution)/shard_map/all_to_all | solution.py:58
  132.6 19.2 %all_to_all.46 = f32[64,1,507]{2,1,0:T(1,128)S(1)} all-to-all(f32[64,1,507]{2,1,0:T(1,128)S(1)} %all_to_all.33), channel_id=1, replica_groups=mesh['snap_0'=4,'snap_1'=2,'brick_0'=16,'brick_1'=2,'brick_2'=2] {'snap_..., dimensions={0} | all-to-all | bytes 259584 | tf_op jit(solution)/shard_map/all_to_all | solution.py:55
  151.9 7.1 %collective-permute-start.7 = (f32[507]{0:T(512)S(1)}, f32[507]{0:T(512)S(1)}, u32[]{:S(2)}, u32[]{:S(2)}) collective-permute-start(f32[507]{0:T(512)S(1)} %reduce_sum.3282), channel_id=1, source_target_pairs={{0,1},{1,0},{2,3},{3,2},{4,5},{5,4},{6,7},{7,6},{8,9},{9,8},{10,11... | collective-permute-start | bytes 6092 | tf_op jit(solution)/shard_map/ppermute | solution.py:68
  159.0 0.8 collective-permute-done.7
  159.8 2.2 collective-permute-start.8
  162.0 2.1 collective-permute-done.8
  164.1 1.9 collective-permute-start.9
  166.1 3.9 %collective-permute-done.9 = f32[507]{0:T(512)S(1)} collective-permute-done((f32[507]{0:T(512)S(1)}, f32[507]{0:T(512)S(1)}, u32[]{:S(2)}, u32[]{:S(2)}) %collective-permute-start.9) | collective-permute-done | bytes 2060 | tf_op jit(solution)/shard_map/ppermute | solution.py:68
  170.1 19.0 %all_to_all.47 = f32[64,1,507]{2,1,0:T(1,128)S(1)} all-to-all(f32[64,1,507]{2,1,0:T(1,128)S(1)} %broadcast_in_dim.49), channel_id=1, replica_groups=mesh['snap_0'=4,'snap_1'=2,'brick_0'=16,'brick_1'=2,'brick_2'=2] {'snap_..., dimensions={0} | all-to-all | bytes 259584 | tf_op jit(solution)/shard_map/all_to_all | solution.py:58
  200.0 0.8 select_maximum_fusion
  201.1 19.2 %all_to_all.48 = f32[64,1,507]{2,1,0:T(1,128)S(1)} all-to-all(f32[64,1,507]{2,1,0:T(1,128)S(1)} %all_to_all.36), channel_id=1, replica_groups=mesh['snap_0'=4,'snap_1'=2,'brick_0'=16,'brick_1'=2,'brick_2'=2] {'snap_..., dimensions={0} | all-to-all | bytes 259584 | tf_op jit(solution)/shard_map/all_to_all | solution.py:55
  220.4 7.1 %collective-permute-start.10 = (f32[507]{0:T(512)S(1)}, f32[507]{0:T(512)S(1)}, u32[]{:S(2)}, u32[]{:S(2)}) collective-permute-start(f32[507]{0:T(512)S(1)} %reduce_sum.3438), channel_id=1, source_target_pairs={{0,1},{1,0},{2,3},{3,2},{4,5},{5,4},{6,7},{7,6},{8,9},{9,8},{10,11... | collective-permute-start | bytes 6092 | tf_op jit(solution)/shard_map/ppermute | solution.py:68
  227.5 0.8 collective-permute-done.10
  228.3 2.2 collective-permute-start.11
  230.5 2.1 collective-permute-done.11
  232.6 1.9 collective-permute-start.12
  234.5 3.9 %collective-permute-done.12 = f32[507]{0:T(512)S(1)} collective-permute-done((f32[507]{0:T(512)S(1)}, f32[507]{0:T(512)S(1)}, u32[]{:S(2)}, u32[]{:S(2)}) %collective-permute-start.12) | collective-permute-done | bytes 2060 | tf_op jit(solution)/shard_map/ppermute | solution.py:68
  239.2 5.2 %all-to-all-start.5 = ((f32[64,1,507]{2,1,0:T(1,128)}), f32[64,1,507]{2,1,0:T(1,128)S(1)}, u32[]{:S(2)}, u32[]{:S(2)}) async-start(f32[64,1,507]{2,1,0:T(1,128)} %broadcast_in_dim.52), calls=%async_computation.5 | async-start | bytes 262144 | tf_op jit(solution)/shard_map/all_to_all | solution.py:58
  248.5 9.9 %all-to-all-done.5 = f32[64,1,507]{2,1,0:T(1,128)S(1)} async-done(((f32[64,1,507]{2,1,0:T(1,128)}), f32[64,1,507]{2,1,0:T(1,128)S(1)}, u32[]{:S(2)}, u32[]{:S(2)}) %all-to-all-start.5) | async-done | bytes 129824 | tf_op jit(solution)/shard_map/all_to_all | solution.py:58
  262.7 0.8 copy.71
  263.6 0.8 copy.72
  264.4 0.8 copy.73
  (302 shorter events, 39.1 us)
Async XLA Ops:
  0.6 24.6 %copy-start = (f32[5,81,80]{1,2,0:T(8,128)S(1)}, f32[5,81,80]{1,2,0:T(8,128)}, u32[]{:S(2)}) copy-start(f32[5,81,80]{1,2,0:T(8,128)} %param.16) | copy-start | bytes 388804
  2.0 44.6 %collective-permute-start.3 = (f32[3,15]{1,0:T(4,128)}, f32[3,15]{1,0:T(4,128)S(1)}, u32[]{:S(2)}, u32[]{:S(2)}) collective-permute-start(f32[3,15]{1,0:T(4,128)} %get-tuple-element.732), channel_id=1, source_target_pairs={{1,0},{2,1},{3,2},{4,3},{5,4},{6,5},{7,6},{8,7},{9,8},{10,9},{11,1... | collective-permute-start | bytes 548 | tf_op jit(solution)/shard_map/ppermute | solution.py:38
  10.8 35.9 %collective-permute-start.2 = (f32[3,15]{1,0:T(4,128)}, f32[3,15]{1,0:T(4,128)S(1)}, u32[]{:S(2)}, u32[]{:S(2)}) collective-permute-start(f32[3,15]{1,0:T(4,128)} %get-tuple-element.731), channel_id=1, source_target_pairs={{0,1},{1,2},{2,3},{3,4},{4,5},{5,6},{6,7},{7,8},{8,9},{9,10},{10,1... | collective-permute-start | bytes 548 | tf_op jit(solution)/shard_map/ppermute | solution.py:36
  14.8 10.6 %collective-permute-start.1 = (f32[5,45]{1,0:T(8,128)S(1)}, f32[5,45]{1,0:T(8,128)S(1)}, u32[]{:S(2)}, u32[]{:S(2)}) collective-permute-start(f32[5,45]{1,0:T(8,128)S(1)} %get-tuple-element.730), channel_id=1, source_target_pairs={{1,0},{2,1},{3,2},{4,3},{5,4},{6,5},{7,6},{8,7},{9,8},{10,9},{11,1... | collective-permute-start | bytes 2708 | tf_op jit(solution)/shard_map/ppermute | solution.py:38
  17.2 8.2 %collective-permute-start = (f32[5,45]{1,0:T(8,128)S(1)}, f32[5,45]{1,0:T(8,128)S(1)}, u32[]{:S(2)}, u32[]{:S(2)}) collective-permute-start(f32[5,45]{1,0:T(8,128)S(1)} %get-tuple-element.729), channel_id=1, source_target_pairs={{0,1},{1,2},{2,3},{3,4},{4,5},{5,6},{6,7},{7,8},{8,9},{9,10},{10,1... | collective-permute-start | bytes 2708 | tf_op jit(solution)/shard_map/ppermute | solution.py:36
  28.2 4.3 %copy-start.15 = (pred[30]{0:T(512)(128)(4,1)S(1)}, pred[30]{0:T(512)(128)(4,1)}, u32[]{:S(2)}) copy-start(pred[30]{0:T(512)(128)(4,1)} %constant.124.clone) | copy-start | bytes 94
  28.3 4.3 %copy-start.17 = (s32[30]{0:T(128)S(1)}, s32[30]{0:T(128)}, u32[]{:S(2)}) copy-start(s32[30]{0:T(128)} %constant.125.clone) | copy-start | bytes 364
  38.3 0.7 copy-start.16
  38.3 0.7 copy-start.18
  43.2 1.9 copy-start.10
  43.2 1.9 copy-start.11
  43.2 1.9 copy-start.12
  43.2 1.9 copy-start.13
  43.2 1.9 copy-start.14
  43.2 2.0 copy-start.5
  43.2 2.0 copy-start.6
  43.2 2.0 copy-start.7
  43.2 2.0 copy-start.8
  43.3 2.0 copy-start.9
  45.0 0.7 copy-start.3
  45.0 0.7 copy-start.4
  81.9 8.7 %collective-permute-start.4 = (f32[507]{0:T(512)S(1)}, f32[507]{0:T(512)S(1)}, u32[]{:S(2)}, u32[]{:S(2)}) collective-permute-start(f32[507]{0:T(512)S(1)} %reduce_sum.3126), channel_id=1, source_target_pairs={{0,1},{1,0},{2,3},{3,2},{4,5},{5,4},{6,7},{7,6},{8,9},{9,8},{10,11... | collective-permute-start | bytes 6092 | tf_op jit(solution)/shard_map/ppermute | solution.py:68
  90.5 4.3 %collective-permute-start.5 = (f32[507]{0:T(512)S(1)}, f32[507]{0:T(512)S(1)}, u32[]{:S(2)}, u32[]{:S(2)}) collective-permute-start(f32[507]{0:T(512)S(1)} %add.1986), channel_id=1, source_target_pairs={{0,64},{64,0},{1,65},{65,1},{2,66},{66,2},{3,67},{67,3},{4,68},{68... | collective-permute-start | bytes 6092 | tf_op jit(solution)/shard_map/ppermute | solution.py:68
  94.9 5.8 %collective-permute-start.6 = (f32[507]{0:T(512)S(1)}, f32[507]{0:T(512)S(1)}, u32[]{:S(2)}, u32[]{:S(2)}) collective-permute-start(f32[507]{0:T(512)S(1)} %add.1987), channel_id=1, source_target_pairs={{0,2},{2,0},{1,3},{3,1},{4,6},{6,4},{5,7},{7,5},{8,10},{10,8},{9,1... | collective-permute-start | bytes 6092 | tf_op jit(solution)/shard_map/ppermute | solution.py:68
  101.4 19.2 %all-to-all-start.1 = ((f32[64,1,507]{2,1,0:T(1,128)}), f32[64,1,507]{2,1,0:T(1,128)S(1)}, u32[]{:S(2)}, u32[]{:S(2)}) async-start(f32[64,1,507]{2,1,0:T(1,128)} %broadcast_in_dim.46), calls=%async_computation.1 | async-start | bytes 262144 | tf_op jit(solution)/shard_map/all_to_all | solution.py:58
  151.9 7.9 %collective-permute-start.7 = (f32[507]{0:T(512)S(1)}, f32[507]{0:T(512)S(1)}, u32[]{:S(2)}, u32[]{:S(2)}) collective-permute-start(f32[507]{0:T(512)S(1)} %reduce_sum.3282), channel_id=1, source_target_pairs={{0,1},{1,0},{2,3},{3,2},{4,5},{5,4},{6,7},{7,6},{8,9},{9,8},{10,11... | collective-permute-start | bytes 6092 | tf_op jit(solution)/shard_map/ppermute | solution.py:68
  159.8 4.3 %collective-permute-start.8 = (f32[507]{0:T(512)S(1)}, f32[507]{0:T(512)S(1)}, u32[]{:S(2)}, u32[]{:S(2)}) collective-permute-start(f32[507]{0:T(512)S(1)} %add.2085), channel_id=1, source_target_pairs={{0,64},{64,0},{1,65},{65,1},{2,66},{66,2},{3,67},{67,3},{4,68},{68... | collective-permute-start | bytes 6092 | tf_op jit(solution)/shard_map/ppermute | solution.py:68
  164.1 5.8 %collective-permute-start.9 = (f32[507]{0:T(512)S(1)}, f32[507]{0:T(512)S(1)}, u32[]{:S(2)}, u32[]{:S(2)}) collective-permute-start(f32[507]{0:T(512)S(1)} %add.2086), channel_id=1, source_target_pairs={{0,2},{2,0},{1,3},{3,1},{4,6},{6,4},{5,7},{7,5},{8,10},{10,8},{9,1... | collective-permute-start | bytes 6092 | tf_op jit(solution)/shard_map/ppermute | solution.py:68
  200.0 44.4 %copy-start.1 = (f32[5,81,80]{1,2,0:T(8,128)S(1)}, f32[5,81,80]{1,2,0:T(8,128)}, u32[]{:S(2)}) copy-start(f32[5,81,80]{1,2,0:T(8,128)} %param.17) | copy-start | bytes 388804
  200.8 45.2 %copy-start.2 = (f32[5,81,80]{1,2,0:T(8,128)S(1)}, f32[5,81,80]{1,2,0:T(8,128)}, u32[]{:S(2)}) copy-start(f32[5,81,80]{1,2,0:T(8,128)} %param.18) | copy-start | bytes 388804
  220.4 7.9 %collective-permute-start.10 = (f32[507]{0:T(512)S(1)}, f32[507]{0:T(512)S(1)}, u32[]{:S(2)}, u32[]{:S(2)}) collective-permute-start(f32[507]{0:T(512)S(1)} %reduce_sum.3438), channel_id=1, source_target_pairs={{0,1},{1,0},{2,3},{3,2},{4,5},{5,4},{6,7},{7,6},{8,9},{9,8},{10,11... | collective-permute-start | bytes 6092 | tf_op jit(solution)/shard_map/ppermute | solution.py:68
  228.3 4.3 %collective-permute-start.11 = (f32[507]{0:T(512)S(1)}, f32[507]{0:T(512)S(1)}, u32[]{:S(2)}, u32[]{:S(2)}) collective-permute-start(f32[507]{0:T(512)S(1)} %add.2184), channel_id=1, source_target_pairs={{0,64},{64,0},{1,65},{65,1},{2,66},{66,2},{3,67},{67,3},{4,68},{68... | collective-permute-start | bytes 6092 | tf_op jit(solution)/shard_map/ppermute | solution.py:68
  232.6 5.8 %collective-permute-start.12 = (f32[507]{0:T(512)S(1)}, f32[507]{0:T(512)S(1)}, u32[]{:S(2)}, u32[]{:S(2)}) collective-permute-start(f32[507]{0:T(512)S(1)} %add.2185), channel_id=1, source_target_pairs={{0,2},{2,0},{1,3},{3,1},{4,6},{6,4},{5,7},{7,5},{8,10},{10,8},{9,1... | collective-permute-start | bytes 6092 | tf_op jit(solution)/shard_map/ppermute | solution.py:68
  239.2 19.2 %all-to-all-start.5 = ((f32[64,1,507]{2,1,0:T(1,128)}), f32[64,1,507]{2,1,0:T(1,128)S(1)}, u32[]{:S(2)}, u32[]{:S(2)}) async-start(f32[64,1,507]{2,1,0:T(1,128)} %broadcast_in_dim.52), calls=%async_computation.5 | async-start | bytes 262144 | tf_op jit(solution)/shard_map/all_to_all | solution.py:58

commit v7 on v6

--- a/solution.py
+++ b/solution.py
@@ -202,7 +202,8 @@
         axis=0,
     )
     depth = 3 * WINDOW
-    padded_all = with_halo(geometry, ((BRICK, 1),), depth)
+    stacked_all = with_halo(jnp.concatenate([geometry, left_vector[0]], axis=0), ((BRICK, 1),), depth)
+    padded_all = stacked_all[:5]
     kind_values = jnp.arange(SPECIES, dtype=jnp.float32)
     ext_count = atom_count + 4 * WINDOW
     mid_count = atom_count + 2 * WINDOW
@@ -221,7 +222,7 @@
     padded = padded_all[:, 2 * WINDOW : 4 * WINDOW + atom_count]
     mid_geometry = padded_all[:, WINDOW : 3 * WINDOW + mid_count]
     mid_kinds = kinds_ext[:, WINDOW : WINDOW + mid_count]
-    left_ext = with_halo(left_vector[0], ((BRICK, 1),), WINDOW)
+    left_ext = stacked_all[5:, 2 * WINDOW : 4 * WINDOW + atom_count]
     alpha_norm = scalars[0]
     rho_bar = scalars[1]
     phi_bar = scalars[2]

time: 269 us -> 259 us (0.963)
  starting transfers between devices: 62.8 us -> 58.4 us
  waiting for transfers between devices: 43.9 us -> 39.6 us
    ppermute x9, waiting for transfers between devices: 20.4 us -> 15.7 us  [butterfly_sum(): shard = shard + lax.ppermute(shard, axis, partners)]
    ppermute x2 -> x1, starting transfers between devices: 6.58 us -> 1.92 us  [with_halo(): lax.ppermute(tail, axis, [(i, (i + 1) % count) for i in range(ends)])]
    ppermute x9, starting transfers between devices: 34.4 us -> 37.2 us  [butterfly_sum(): shard = shard + lax.ppermute(shard, axis, partners)]
    ppermute x2 -> x1, starting transfers between devices: 11.1 us -> 8.74 us  [with_halo(): lax.ppermute(head, axis, [((i + 1) % count, i) for i in range(ends)])]
    unnamed x80 -> x67, local copies, waits for them, and re-layouts: 7.51 us -> 7.18 us
  transfers between devices with their start and end apart: 15 -> 13, of which waited for: 11 -> 11; matrix products, arithmetic and copies ran while one was open for 10% -> 2% of each run, Pallas kernels for 0% -> 0%
where the time goes in v7:
time: 259 us; the launch traced here: 256 us
  blocking collectives  86.9 us (34%)
  starting transfers between devices  58.4 us (23%)
  waiting for transfers between devices  39.6 us (15%)
  other arithmetic  30.1 us (12%)
  local copies, waits for them, and re-layouts  27.2 us (11%)
  between operations  9.87 us (4%)
  matrix products  3.54 us (1%)
    all_to_all x3, blocking collectives, group_sum(): lax.all_to_all(padded.reshape(count, -1), spread_axis, 0, 0, tiled=False)  67.9 us
    ppermute x9, starting transfers between devices, butterfly_sum(): shard = shard + lax.ppermute(shard, axis, partners)  37.2 us
    all_to_all x2, waiting for transfers between devices, group_sum(): whole = lax.all_to_all(spread, spread_axis, 0, 0, tiled=False)  23.9 us
    all_to_all x1, blocking collectives, group_sum(): whole = lax.all_to_all(spread, spread_axis, 0, 0, tiled=False)  19 us
    ppermute x9, waiting for transfers between devices, butterfly_sum(): shard = shard + lax.ppermute(shard, axis, partners)  15.7 us
    all_to_all x2, starting transfers between devices, group_sum(): whole = lax.all_to_all(spread, spread_axis, 0, 0, tiled=False)  10.6 us
    ppermute x1, starting transfers between devices, with_halo(): lax.ppermute(head, axis, [((i + 1) % count, i) for i in range(ends)])  8.74 us
    unnamed x67, local copies, waits for them, and re-layouts  7.18 us
  transfers between devices with their start and end apart: 13, of which 11 were waited for; matrix products, arithmetic and copies ran while one was open for 2% of the time, Pallas kernels for 0%

profile of v7, /device:TPU:1, one launch (start us, length us, event | category | flops | bytes accessed | tf_op | source)
XLA Modules:
  0.0 255.6 jit_solution(12691066537944110327)
XLA Ops:
  0.6 0.7 convert_element_type.46
  2.8 8.7 %collective-permute-start.1 = (f32[8,45]{1,0:T(8,128)S(1)}, f32[8,45]{1,0:T(8,128)S(1)}, u32[]{:S(2)}, u32[]{:S(2)}) collective-permute-start(f32[8,45]{1,0:T(8,128)S(1)} %get-tuple-element.730), channel_id=1, source_target_pairs={{1,0},{2,1},{3,2},{4,3},{5,4},{6,5},{7,6},{8,7},{9,8},{10,9},{11,1... | collective-permute-start | bytes 4328 | tf_op jit(solution)/shard_map/ppermute | solution.py:38
  11.6 1.9 collective-permute-start
  13.5 0.7 broadcast_multiply_fusion.44
  14.3 1.4 fusion.549
  15.6 1.0 slice.2358
  19.8 3.6 %fusion.84 = (f32[30,1,316]{2,1,0:T(1,128)}, f32[30,1,316]{2,1,0:T(1,128)}, f32[30,1,316]{2,1,0:T(1,128)}, f32[30,1,316]{2,1,0:T(1,128)}, f32[30,1,316]{2,1,0:T(...) fusion(f32[30,316]{1,0:T(8,128)S(1)} %get-tuple-element.727, ...), kind=kLoop, calls=%fused_computation.351 | loop fusion | flops 1403040 | bytes 758400 | tf_op jit(solution)/shard_map/mul | solution.py:95
  24.4 1.4 stack.174
  26.3 0.7 fusion.8
  27.1 1.5 fusion.547
  28.6 1.8 fusion.546
  31.4 2.9 %stack.175 = f32[30,16,316]{2,1,0:T(8,128)S(1)} concatenate(f32[30,1,316]{2,1,0:T(1,128)} %get-tuple-element.726, f32[30,1,316]{2,1,0:T(1,128)} %get-tuple-element.607, f32[30,1,316]{2,1,0:T(1,128)} %get-tuple-element.609, f32[30,1,316]{2,1,0:T(1,128)} %get-tuple-element.611, f32[30,1,316]{2,1,0:T(1,128)} %get-tuple-element.613, f32[30,1,316]{2,1,0:T(1,128)} %get-tuple-element.615, ...), dimensions={1} | concatenate | bytes 1213440 | tf_op jit(solution)/shard_map/stack | solution.py:96
  34.3 1.9 multiply_reduce_fusion.100
  38.4 0.8 fusion.356
  43.0 0.7 fusion.30
  44.1 29.5 %all_to_all.45 = f32[64,1,507]{2,1,0:T(1,128)S(1)} all-to-all(f32[64,1,507]{2,1,0:T(1,128)S(1)} %all_to_all.30), channel_id=1, replica_groups=mesh['snap_0'=4,'snap_1'=2,'brick_0'=16,'brick_1'=2,'brick_2'=2] {'snap_..., dimensions={0} | all-to-all | bytes 259584 | tf_op jit(solution)/shard_map/all_to_all | solution.py:55
  73.7 5.9 %collective-permute-start.2 = (f32[507]{0:T(512)S(1)}, f32[507]{0:T(512)S(1)}, u32[]{:S(2)}, u32[]{:S(2)}) collective-permute-start(f32[507]{0:T(512)S(1)} %reduce_sum.3126), channel_id=1, source_target_pairs={{0,1},{1,0},{2,3},{3,2},{4,5},{5,4},{6,7},{7,6},{8,9},{9,8},{10,11... | collective-permute-start | bytes 6092 | tf_op jit(solution)/shard_map/ppermute | solution.py:68
  79.6 0.8 collective-permute-done.2
  80.4 2.5 collective-permute-start.3
  82.9 1.8 collective-permute-done.3
  84.7 2.8 %collective-permute-start.4 = (f32[507]{0:T(512)S(1)}, f32[507]{0:T(512)S(1)}, u32[]{:S(2)}, u32[]{:S(2)}) collective-permute-start(f32[507]{0:T(512)S(1)} %add.1987), channel_id=1, source_target_pairs={{0,2},{2,0},{1,3},{3,1},{4,6},{6,4},{5,7},{7,5},{8,10},{10,8},{9,1... | collective-permute-start | bytes 6092 | tf_op jit(solution)/shard_map/ppermute | solution.py:68
  87.6 3.0 %collective-permute-done.4 = f32[507]{0:T(512)S(1)} collective-permute-done((f32[507]{0:T(512)S(1)}, f32[507]{0:T(512)S(1)}, u32[]{:S(2)}, u32[]{:S(2)}) %collective-permute-start.4) | collective-permute-done | bytes 2060 | tf_op jit(solution)/shard_map/ppermute | solution.py:68
  90.6 0.7 broadcast_in_dim.46
  91.3 5.3 %all-to-all-start.1 = ((f32[64,1,507]{2,1,0:T(1,128)}), f32[64,1,507]{2,1,0:T(1,128)S(1)}, u32[]{:S(2)}, u32[]{:S(2)}) async-start(f32[64,1,507]{2,1,0:T(1,128)} %broadcast_in_dim.46), calls=%async_computation.1 | async-start | bytes 262144 | tf_op jit(solution)/shard_map/all_to_all | solution.py:58
  96.8 13.6 %all-to-all-done.1 = f32[64,1,507]{2,1,0:T(1,128)S(1)} async-done(((f32[64,1,507]{2,1,0:T(1,128)}), f32[64,1,507]{2,1,0:T(1,128)S(1)}, u32[]{:S(2)}, u32[]{:S(2)}) %all-to-all-start.1) | async-done | bytes 129824 | tf_op jit(solution)/shard_map/all_to_all | solution.py:58
  121.4 0.7 select_maximum_fusion.1
  122.4 19.2 %all_to_all.46 = f32[64,1,507]{2,1,0:T(1,128)S(1)} all-to-all(f32[64,1,507]{2,1,0:T(1,128)S(1)} %all_to_all.33), channel_id=1, replica_groups=mesh['snap_0'=4,'snap_1'=2,'brick_0'=16,'brick_1'=2,'brick_2'=2] {'snap_..., dimensions={0} | all-to-all | bytes 259584 | tf_op jit(solution)/shard_map/all_to_all | solution.py:55
  141.7 7.1 %collective-permute-start.5 = (f32[507]{0:T(512)S(1)}, f32[507]{0:T(512)S(1)}, u32[]{:S(2)}, u32[]{:S(2)}) collective-permute-start(f32[507]{0:T(512)S(1)} %reduce_sum.3282), channel_id=1, source_target_pairs={{0,1},{1,0},{2,3},{3,2},{4,5},{5,4},{6,7},{7,6},{8,9},{9,8},{10,11... | collective-permute-start | bytes 6092 | tf_op jit(solution)/shard_map/ppermute | solution.py:68
  148.8 0.8 collective-permute-done.5
  149.6 2.6 %collective-permute-start.6 = (f32[507]{0:T(512)S(1)}, f32[507]{0:T(512)S(1)}, u32[]{:S(2)}, u32[]{:S(2)}) collective-permute-start(f32[507]{0:T(512)S(1)} %add.2085), channel_id=1, source_target_pairs={{0,64},{64,0},{1,65},{65,1},{2,66},{66,2},{3,67},{67,3},{4,68},{68... | collective-permute-start | bytes 6092 | tf_op jit(solution)/shard_map/ppermute | solution.py:68
  152.2 1.7 collective-permute-done.6
  153.9 3.3 %collective-permute-start.7 = (f32[507]{0:T(512)S(1)}, f32[507]{0:T(512)S(1)}, u32[]{:S(2)}, u32[]{:S(2)}) collective-permute-start(f32[507]{0:T(512)S(1)} %add.2086), channel_id=1, source_target_pairs={{0,2},{2,0},{1,3},{3,1},{4,6},{6,4},{5,7},{7,5},{8,10},{10,8},{9,1... | collective-permute-start | bytes 6092 | tf_op jit(solution)/shard_map/ppermute | solution.py:68
  157.3 2.5 collective-permute-done.7
  159.8 19.0 %all_to_all.47 = f32[64,1,507]{2,1,0:T(1,128)S(1)} all-to-all(f32[64,1,507]{2,1,0:T(1,128)S(1)} %broadcast_in_dim.49), channel_id=1, replica_groups=mesh['snap_0'=4,'snap_1'=2,'brick_0'=16,'brick_1'=2,'brick_2'=2] {'snap_..., dimensions={0} | all-to-all | bytes 259584 | tf_op jit(solution)/shard_map/all_to_all | solution.py:58
  189.8 0.8 select_maximum_fusion
  190.8 19.2 %all_to_all.48 = f32[64,1,507]{2,1,0:T(1,128)S(1)} all-to-all(f32[64,1,507]{2,1,0:T(1,128)S(1)} %all_to_all.36), channel_id=1, replica_groups=mesh['snap_0'=4,'snap_1'=2,'brick_0'=16,'brick_1'=2,'brick_2'=2] {'snap_..., dimensions={0} | all-to-all | bytes 259584 | tf_op jit(solution)/shard_map/all_to_all | solution.py:55
  210.2 7.1 %collective-permute-start.8 = (f32[507]{0:T(512)S(1)}, f32[507]{0:T(512)S(1)}, u32[]{:S(2)}, u32[]{:S(2)}) collective-permute-start(f32[507]{0:T(512)S(1)} %reduce_sum.3438), channel_id=1, source_target_pairs={{0,1},{1,0},{2,3},{3,2},{4,5},{5,4},{6,7},{7,6},{8,9},{9,8},{10,11... | collective-permute-start | bytes 6092 | tf_op jit(solution)/shard_map/ppermute | solution.py:68
  217.3 0.8 collective-permute-done.8
  218.1 2.6 %collective-permute-start.9 = (f32[507]{0:T(512)S(1)}, f32[507]{0:T(512)S(1)}, u32[]{:S(2)}, u32[]{:S(2)}) collective-permute-start(f32[507]{0:T(512)S(1)} %add.2184), channel_id=1, source_target_pairs={{0,64},{64,0},{1,65},{65,1},{2,66},{66,2},{3,67},{67,3},{4,68},{68... | collective-permute-start | bytes 6092 | tf_op jit(solution)/shard_map/ppermute | solution.py:68
  220.7 1.7 collective-permute-done.9
  222.4 3.3 %collective-permute-start.10 = (f32[507]{0:T(512)S(1)}, f32[507]{0:T(512)S(1)}, u32[]{:S(2)}, u32[]{:S(2)}) collective-permute-start(f32[507]{0:T(512)S(1)} %add.2185), channel_id=1, source_target_pairs={{0,2},{2,0},{1,3},{3,1},{4,6},{6,4},{5,7},{7,5},{8,10},{10,8},{9,1... | collective-permute-start | bytes 6092 | tf_op jit(solution)/shard_map/ppermute | solution.py:68
  225.7 2.5 collective-permute-done.10
  228.2 0.7 broadcast_in_dim.52
  229.0 5.2 %all-to-all-start.5 = ((f32[64,1,507]{2,1,0:T(1,128)}), f32[64,1,507]{2,1,0:T(1,128)S(1)}, u32[]{:S(2)}, u32[]{:S(2)}) async-start(f32[64,1,507]{2,1,0:T(1,128)} %broadcast_in_dim.52), calls=%async_computation.5 | async-start | bytes 262144 | tf_op jit(solution)/shard_map/all_to_all | solution.py:58
  237.9 10.3 %all-to-all-done.5 = f32[64,1,507]{2,1,0:T(1,128)S(1)} async-done(((f32[64,1,507]{2,1,0:T(1,128)}), f32[64,1,507]{2,1,0:T(1,128)S(1)}, u32[]{:S(2)}, u32[]{:S(2)}) %all-to-all-start.5) | async-done | bytes 129824 | tf_op jit(solution)/shard_map/all_to_all | solution.py:58
  252.5 0.8 copy.71
  253.3 0.8 copy.72
  254.2 0.8 copy.73
  (291 shorter events, 36.2 us)
Async XLA Ops:
  0.6 16.2 %copy-start = (f32[5,81,80]{1,2,0:T(8,128)S(1)}, f32[5,81,80]{1,2,0:T(8,128)}, u32[]{:S(2)}) copy-start(f32[5,81,80]{1,2,0:T(8,128)} %param.16) | copy-start | bytes 388804
  2.8 14.1 %collective-permute-start.1 = (f32[8,45]{1,0:T(8,128)S(1)}, f32[8,45]{1,0:T(8,128)S(1)}, u32[]{:S(2)}, u32[]{:S(2)}) collective-permute-start(f32[8,45]{1,0:T(8,128)S(1)} %get-tuple-element.730), channel_id=1, source_target_pairs={{1,0},{2,1},{3,2},{4,3},{5,4},{6,5},{7,6},{8,7},{9,8},{10,9},{11,1... | collective-permute-start | bytes 4328 | tf_op jit(solution)/shard_map/ppermute | solution.py:38
  11.6 5.4 %collective-permute-start = (f32[8,45]{1,0:T(8,128)S(1)}, f32[8,45]{1,0:T(8,128)S(1)}, u32[]{:S(2)}, u32[]{:S(2)}) collective-permute-start(f32[8,45]{1,0:T(8,128)S(1)} %get-tuple-element.729), channel_id=1, source_target_pairs={{0,1},{1,2},{2,3},{3,4},{4,5},{5,6},{6,7},{7,8},{8,9},{9,10},{10,1... | collective-permute-start | bytes 4328 | tf_op jit(solution)/shard_map/ppermute | solution.py:36
  19.8 4.3 %copy-start.9 = (pred[30]{0:T(512)(128)(4,1)S(1)}, pred[30]{0:T(512)(128)(4,1)}, u32[]{:S(2)}) copy-start(pred[30]{0:T(512)(128)(4,1)} %constant.124.clone) | copy-start | bytes 94
  19.8 4.3 %copy-start.11 = (s32[30]{0:T(128)S(1)}, s32[30]{0:T(128)}, u32[]{:S(2)}) copy-start(s32[30]{0:T(128)} %constant.125.clone) | copy-start | bytes 364
  30.3 0.7 copy-start.10
  30.3 0.7 copy-start.12
  36.3 0.9 copy-start.1
  36.3 1.0 copy-start.2
  36.3 1.0 copy-start.3
  36.3 1.1 copy-start.4
  36.3 1.1 copy-start.5
  36.3 1.2 copy-start.6
  73.7 6.8 %collective-permute-start.2 = (f32[507]{0:T(512)S(1)}, f32[507]{0:T(512)S(1)}, u32[]{:S(2)}, u32[]{:S(2)}) collective-permute-start(f32[507]{0:T(512)S(1)} %reduce_sum.3126), channel_id=1, source_target_pairs={{0,1},{1,0},{2,3},{3,2},{4,5},{5,4},{6,7},{7,6},{8,9},{9,8},{10,11... | collective-permute-start | bytes 6092 | tf_op jit(solution)/shard_map/ppermute | solution.py:68
  80.4 4.3 %collective-permute-start.3 = (f32[507]{0:T(512)S(1)}, f32[507]{0:T(512)S(1)}, u32[]{:S(2)}, u32[]{:S(2)}) collective-permute-start(f32[507]{0:T(512)S(1)} %add.1986), channel_id=1, source_target_pairs={{0,64},{64,0},{1,65},{65,1},{2,66},{66,2},{3,67},{67,3},{4,68},{68... | collective-permute-start | bytes 6092 | tf_op jit(solution)/shard_map/ppermute | solution.py:68
  84.7 5.8 %collective-permute-start.4 = (f32[507]{0:T(512)S(1)}, f32[507]{0:T(512)S(1)}, u32[]{:S(2)}, u32[]{:S(2)}) collective-permute-start(f32[507]{0:T(512)S(1)} %add.1987), channel_id=1, source_target_pairs={{0,2},{2,0},{1,3},{3,1},{4,6},{6,4},{5,7},{7,5},{8,10},{10,8},{9,1... | collective-permute-start | bytes 6092 | tf_op jit(solution)/shard_map/ppermute | solution.py:68
  91.3 19.1 %all-to-all-start.1 = ((f32[64,1,507]{2,1,0:T(1,128)}), f32[64,1,507]{2,1,0:T(1,128)S(1)}, u32[]{:S(2)}, u32[]{:S(2)}) async-start(f32[64,1,507]{2,1,0:T(1,128)} %broadcast_in_dim.46), calls=%async_computation.1 | async-start | bytes 262144 | tf_op jit(solution)/shard_map/all_to_all | solution.py:58
  141.7 7.9 %collective-permute-start.5 = (f32[507]{0:T(512)S(1)}, f32[507]{0:T(512)S(1)}, u32[]{:S(2)}, u32[]{:S(2)}) collective-permute-start(f32[507]{0:T(512)S(1)} %reduce_sum.3282), channel_id=1, source_target_pairs={{0,1},{1,0},{2,3},{3,2},{4,5},{5,4},{6,7},{7,6},{8,9},{9,8},{10,11... | collective-permute-start | bytes 6092 | tf_op jit(solution)/shard_map/ppermute | solution.py:68
  149.6 4.3 %collective-permute-start.6 = (f32[507]{0:T(512)S(1)}, f32[507]{0:T(512)S(1)}, u32[]{:S(2)}, u32[]{:S(2)}) collective-permute-start(f32[507]{0:T(512)S(1)} %add.2085), channel_id=1, source_target_pairs={{0,64},{64,0},{1,65},{65,1},{2,66},{66,2},{3,67},{67,3},{4,68},{68... | collective-permute-start | bytes 6092 | tf_op jit(solution)/shard_map/ppermute | solution.py:68
  153.9 5.8 %collective-permute-start.7 = (f32[507]{0:T(512)S(1)}, f32[507]{0:T(512)S(1)}, u32[]{:S(2)}, u32[]{:S(2)}) collective-permute-start(f32[507]{0:T(512)S(1)} %add.2086), channel_id=1, source_target_pairs={{0,2},{2,0},{1,3},{3,1},{4,6},{6,4},{5,7},{7,5},{8,10},{10,8},{9,1... | collective-permute-start | bytes 6092 | tf_op jit(solution)/shard_map/ppermute | solution.py:68
  189.8 44.4 %copy-start.7 = (f32[5,81,80]{1,2,0:T(8,128)S(1)}, f32[5,81,80]{1,2,0:T(8,128)}, u32[]{:S(2)}) copy-start(f32[5,81,80]{1,2,0:T(8,128)} %param.17) | copy-start | bytes 388804
  190.6 44.9 %copy-start.8 = (f32[5,81,80]{1,2,0:T(8,128)S(1)}, f32[5,81,80]{1,2,0:T(8,128)}, u32[]{:S(2)}) copy-start(f32[5,81,80]{1,2,0:T(8,128)} %param.18) | copy-start | bytes 388804
  210.2 7.9 %collective-permute-start.8 = (f32[507]{0:T(512)S(1)}, f32[507]{0:T(512)S(1)}, u32[]{:S(2)}, u32[]{:S(2)}) collective-permute-start(f32[507]{0:T(512)S(1)} %reduce_sum.3438), channel_id=1, source_target_pairs={{0,1},{1,0},{2,3},{3,2},{4,5},{5,4},{6,7},{7,6},{8,9},{9,8},{10,11... | collective-permute-start | bytes 6092 | tf_op jit(solution)/shard_map/ppermute | solution.py:68
  218.1 4.3 %collective-permute-start.9 = (f32[507]{0:T(512)S(1)}, f32[507]{0:T(512)S(1)}, u32[]{:S(2)}, u32[]{:S(2)}) collective-permute-start(f32[507]{0:T(512)S(1)} %add.2184), channel_id=1, source_target_pairs={{0,64},{64,0},{1,65},{65,1},{2,66},{66,2},{3,67},{67,3},{4,68},{68... | collective-permute-start | bytes 6092 | tf_op jit(solution)/shard_map/ppermute | solution.py:68
  222.4 5.8 %collective-permute-start.10 = (f32[507]{0:T(512)S(1)}, f32[507]{0:T(512)S(1)}, u32[]{:S(2)}, u32[]{:S(2)}) collective-permute-start(f32[507]{0:T(512)S(1)} %add.2185), channel_id=1, source_target_pairs={{0,2},{2,0},{1,3},{3,1},{4,6},{6,4},{5,7},{7,5},{8,10},{10,8},{9,1... | collective-permute-start | bytes 6092 | tf_op jit(solution)/shard_map/ppermute | solution.py:68
  229.0 19.2 %all-to-all-start.5 = ((f32[64,1,507]{2,1,0:T(1,128)}), f32[64,1,507]{2,1,0:T(1,128)S(1)}, u32[]{:S(2)}, u32[]{:S(2)}) async-start(f32[64,1,507]{2,1,0:T(1,128)} %broadcast_in_dim.52), calls=%async_computation.5 | async-start | bytes 262144 | tf_op jit(solution)/shard_map/all_to_all | solution.py:58
